TPU v7x, 768 devices: a whole 4x8x12 slice. The times are simulated.
768 devices in a mesh: gx: 8 (over x, core), gy: 96 (over z, y).
Axes of the slice: x: 4, y: 8, z: 12, core: 2. Of those that a mesh axis runs over, the one named last changes fastest.
Arguments:
- positions: float32 [3, 196608], P(None, ('gx', 'gy')), may hold values from -1.5 to 1.5
- species: int32 [196608], P(('gx', 'gy')), may hold values from 0 to 3
- neighbours: int32 [1536, 2], P(('gx', 'gy')), may hold values from 0 to 17
- pair_masks: int32 [1536, 2, 128, 128], P(('gx', 'gy')), may hold values 0 or 1
- send_lists: int32 [8, 96, 8, 2], P('gx', 'gy'), may hold values from 0 to 1
- embedding: float32 [4, 64], replicated, may hold values from -6 to 6
- radial: float32 [4, 64], replicated, may hold values from -6 to 6
- readin: float32 [192, 64], replicated, may hold values from -0.4375 to 0.4375
- readout: float32 [64], replicated, may hold values from -0.75 to 0.75
Outputs:
- energies: float32 [196608], P(('gx', 'gy'))
- forces: float32 [3, 196608], P(None, ('gx', 'gy'))
Inputs may be any that keep to these rules, and one draw needn't show every extreme that they name: `neighbours`: slot index into the owning device's table of own blocks then ghost blocks. `send_lists`: index of one of the sending device's own blocks.
All inputs are finite; a program needn't handle non-finite values. No bound on the sum of `pair_masks` on one device may be relied on, other than what follows from the above.
Results may differ from a plain program's by a relative error of at most 0.0099.
Values sent between devices are 32-bit elements; how exact they have to be, the bound alone decides.
No kernel may reach another device: no remote copies, remote signals or barrier semaphores. Data moves between devices by JAX's collectives and lax.ppermute only.
A program may use at most 32 MiB of HBM per device.

v0:
```python
import math

import jax
import jax.numpy as jnp
from jax import lax
from jax.sharding import PartitionSpec as P

OFFSETS = ((-1, -1), (-1, 0), (-1, 1), (0, -1), (0, 1), (1, -1), (1, 0), (1, 1))
HIGHEST = lax.Precision.HIGHEST


def extended(cells, sides, width):
    for axis, dim in sides:
        count = lax.axis_size(axis)
        head = lax.slice_in_dim(cells, 0, width, axis=dim)
        tail = lax.slice_in_dim(cells, cells.shape[dim] - width, cells.shape[dim], axis=dim)
        cells = jnp.concatenate(
            [
                lax.ppermute(tail, axis, [(i, (i + 1) % count) for i in range(count)]),
                cells,
                lax.ppermute(head, axis, [((i + 1) % count, i) for i in range(count)]),
            ],
            axis=dim,
        )
    return cells


def harmonics(rel, dist):
    ux = rel[0] / dist
    uy = rel[1] / dist
    uz = rel[2] / dist
    root = math.sqrt(3.0)
    return jnp.stack(
        [
            jnp.ones_like(ux),
            ux,
            uy,
            uz,
            root * ux * uy,
            root * uy * uz,
            root * ux * uz,
            0.5 * root * (ux * ux - uy * uy),
            0.5 * (3.0 * uz * uz - 1.0),
        ]
    )


def tile_terms(own_pos, other_pos, other_feat, pair_mask, listed, count):
    atoms = own_pos.shape[1]
    centres = 0.5 + jnp.arange(count).astype(jnp.float32)
    rel = other_pos[:, None, :] - own_pos[:, :, None]
    dist = jnp.sqrt(jnp.sum(rel * rel, axis=0) + 0.25)
    offset = dist[None] - centres[:, None, None]
    basis = jnp.exp(-0.5 * offset * offset)
    angular = harmonics(rel, dist)
    weight = pair_mask.astype(jnp.float32) * (1.0 / math.sqrt(listed * atoms))
    tiles = (basis[:, None] * angular[None] * weight[None, None]).reshape(count * 9, atoms, atoms)
    return jnp.einsum(
        "qij,cj->qci", tiles.astype(jnp.bfloat16), other_feat, preferred_element_type=jnp.float32
    )


def atom_energy(own_pos, table_pos, table_feat, listed_slots, masks, radial, readin, readout):
    count = radial.shape[0]
    width = table_feat.shape[1]
    atoms = own_pos.shape[1]
    listed = listed_slots.shape[0]
    total = jnp.zeros((count * 9, width, atoms), jnp.float32)
    for slot in range(listed):
        index = listed_slots[slot]
        other_pos = lax.dynamic_index_in_dim(table_pos, index, 0, keepdims=False)
        other_feat = lax.dynamic_index_in_dim(table_feat, index, 0, keepdims=False)
        total = total + tile_terms(own_pos, other_pos, other_feat, masks[slot], listed, count)
    proj = total.reshape(count, 9, width, atoms)
    message = jnp.einsum("kc,kmci->mci", radial, proj, precision=HIGHEST)
    first = jnp.sum(message[1:4] * message[1:4], axis=0)
    second = jnp.sum(message[4:9] * message[4:9], axis=0)
    invariants = jnp.concatenate([message[0], first, second], axis=0)
    hidden = jax.nn.silu(jnp.dot(readin.T, invariants, precision=HIGHEST))
    return jnp.dot(readout, hidden, precision=HIGHEST)


def place(parts):
    empty = jnp.zeros_like(parts[0:1])
    full = jnp.concatenate([parts[:4], empty, parts[4:]], axis=0)
    return full.reshape((3, 3) + parts.shape[1:])


def collect(padded):
    return jnp.stack([padded[2 + 2 * pair[0], 2 + 2 * pair[1]] for pair in OFFSETS], axis=0)


def exchange_ghosts(grid):
    return extended(grid, (("gx", 0), ("gy", 1)), 1)


def return_forces(grid):
    return extended(grid, (("gx", 0), ("gy", 1)), 1)


def local(
    positions, species, neighbours, pair_masks, send_lists, embedding, radial, readin, readout
):
    atoms = pair_masks.shape[2]
    blocks = positions.shape[1] // atoms
    kinds = embedding.shape[0]
    width = embedding.shape[1]
    sends = send_lists.shape[3]
    own_pos = positions.reshape(3, blocks, atoms).transpose(1, 0, 2)
    onehot = (species[None, :] == jnp.arange(kinds)[:, None]).astype(jnp.float32)
    feats = (
        jnp.dot(embedding.T, onehot, precision=HIGHEST)
        .reshape(width, blocks, atoms)
        .transpose(1, 0, 2)
    )
    payload = jnp.concatenate([own_pos, feats], axis=1)
    chosen = send_lists.reshape(8, sends)
    pick = (chosen[:, :, None] == jnp.arange(blocks)).astype(jnp.float32)
    outgoing = jnp.einsum("dgb,bra->dgra", pick, payload, precision=HIGHEST)
    incoming = collect(exchange_ghosts(place(outgoing))).reshape(8 * sends, payload.shape[1], atoms)
    ghost_pos = incoming[:, :3]
    ghost_feat = incoming[:, 3:].astype(jnp.bfloat16)
    own_feat = feats.astype(jnp.bfloat16)

    def energies_of(own_now, ghost_now):
        table_pos = jnp.concatenate([own_now, ghost_now], axis=0)
        table_feat = jnp.concatenate([own_feat, ghost_feat], axis=0)
        return jnp.stack(
            [
                atom_energy(
                    own_now[block],
                    table_pos,
                    table_feat,
                    neighbours[block],
                    pair_masks[block],
                    radial,
                    readin,
                    readout,
                )
                for block in range(blocks)
            ]
        )

    energy, pullback = jax.vjp(energies_of, own_pos, ghost_pos)
    grad_own, grad_ghost = pullback(jnp.ones_like(energy))
    returned = collect(return_forces(place(grad_ghost.reshape(8, sends, 3, atoms))))
    back = jnp.einsum("dgb,dgca->bca", pick, returned, precision=HIGHEST)
    forces = -(grad_own + back)
    return (energy.reshape(blocks * atoms), forces.transpose(1, 0, 2).reshape(3, blocks * atoms))


def solution(mesh):
    placed = (
        P(None, ("gx", "gy")),
        P(("gx", "gy")),
        P(("gx", "gy"), None),
        P(("gx", "gy"), None, None, None),
        P("gx", "gy", None, None),
        P(),
        P(),
        P(),
        P(),
    )
    return jax.shard_map(
        local,
        mesh=mesh,
        in_specs=placed,
        out_specs=(P(("gx", "gy")), P(None, ("gx", "gy"))),
        check_vma=False,
    )
```

profile of v0, /device:TPU:1, one launch (start us, length us, event | category | flops | bytes accessed | tf_op | source)
XLA Modules:
  0.0 99.0 jit_solution(9945691477986964077)
XLA Ops:
  1.4 0.9 convolution_bitcast_fusion.2
  2.4 1.1 %fusion.55 = f32[8,2,67,128]{3,0,2,1:T(8,128)S(1)} fusion(f32[2,64,128]{2,0,1:T(2,128)S(1)} %bitcast.819, f32[2,3,128]{2,0,1:T(2,128)S(1)} %bitcast.821, s32[8,2]{0,1:T(2,128)} %bitcast.847), kind=kOutput, calls=%fused_computation.199 | convolution fusion | flops 3310368 | bytes 617536 | tf_op jit(solution)/shard_map/dgb,bra->dgra/dot_general | solution.py:119
  3.5 0.8 slice_bitcast_fusion.1
  4.5 2.6 %collective-permute-start = (f32[1,3,2,67,128]{4,0,3,2,1:T(1,128)S(1)}, f32[1,3,2,67,128]{4,0,3,2,1:T(1,128)}, u32[]{:S(2)}, u32[]{:S(2)}) collective-permute-start(f32[1,3,2,67,128]{4,0,3,2,1:T(1,128)S(1)} %copy.42), channel_id=1, source_target_pairs={{0,96},{96,192},{192,288},{288,384},{384,480},{480,576},{576,672},... | collective-permute-start | bytes 617480 | tf_op jit(solution)/shard_map/ppermute | solution.py:19
  7.1 7.9 %collective-permute-start.1 = (f32[1,3,2,67,128]{4,1,3,2,0:T(4,128)}, f32[1,3,2,67,128]{4,1,3,2,0:T(4,128)}, u32[]{:S(2)}, u32[]{:S(2)}) collective-permute-start(f32[1,3,2,67,128]{4,1,3,2,0:T(4,128)} %get-tuple-element.47), channel_id=1, source_target_pairs={{96,0},{192,96},{288,192},{384,288},{480,384},{576,480},{672,576},... | collective-permute-start | bytes 617480 | tf_op jit(solution)/shard_map/ppermute | solution.py:21
  26.6 1.2 %copy.45 = f32[1,3,2,67,128]{4,0,3,2,1:T(1,128)S(1)} copy(f32[1,3,2,67,128]{4,1,3,2,0:T(4,128)} %collective-permute-done.1) | data formatting | bytes 411648 | tf_op jit(solution)/shard_map/ppermute | solution.py:21
  27.7 1.3 %pad_maximum_fusion.1 = (f32[5,1,2,67,128]{4,0,3,2,1:T(8,128)S(1)}, f32[5,1,2,67,128]{4,0,3,2,1:T(8,128)S(1)}) fusion(f32[1,3,2,67,128]{4,0,3,2,1:T(1,128)S(1)} %copy.45, f32[3,3,2,67,128]{4,0,3,2,1:T(4,128)S(1)} %copy.44, f32[1,3,2,67,128]{4,0,3,2,1:T(1,128)} %collective-permute-done), kind=kLoop, calls=%fused_computation.50 | loop fusion | flops 343040 | bytes 1715200 | tf_op jit(solution)/shard_map/concatenate | solution.py:17
  29.0 9.3 %collective-permute-start.3 = (f32[5,1,2,67,128]{4,0,3,2,1:T(8,128)S(1)}, f32[5,1,2,67,128]{4,0,3,2,1:T(8,128)S(1)}, u32[]{:S(2)}, u32[]{:S(2)}) collective-permute-start(f32[5,1,2,67,128]{4,0,3,2,1:T(8,128)S(1)} %get-tuple-element.30), channel_id=1, source_target_pairs={{1,0},{2,1},{3,2},{4,3},{5,4},{6,5},{7,6},{8,7},{9,8},{10,9},{11,1... | collective-permute-start | bytes 1029128 | tf_op jit(solution)/shard_map/ppermute | solution.py:21
  38.3 1.9 %collective-permute-start.2 = (f32[5,1,2,67,128]{4,0,3,2,1:T(8,128)S(1)}, f32[5,1,2,67,128]{4,0,3,2,1:T(8,128)S(1)}, u32[]{:S(2)}, u32[]{:S(2)}) collective-permute-start(f32[5,1,2,67,128]{4,0,3,2,1:T(8,128)S(1)} %get-tuple-element.31), channel_id=1, source_target_pairs={{0,1},{1,2},{2,3},{3,4},{4,5},{5,6},{6,7},{7,8},{8,9},{9,10},{10,1... | collective-permute-start | bytes 1029128 | tf_op jit(solution)/shard_map/ppermute | solution.py:19
  40.2 1.0 %slice_bitcast_fusion.3 = f32[1,2,67,128]{3,0,2,1:T(1,128)S(1)} fusion(f32[1,3,2,67,128]{4,1,3,2,0:T(4,128)} %collective-permute-done.1), kind=kLoop, calls=%fused_computation.191 | loop fusion | bytes 137216 | tf_op jit(solution)/shard_map/stack;squeeze | solution.py:90
  41.2 1.5 %slice_bitcast_fusion.8 = f32[1,2,67,128]{3,0,2,1:T(1,128)} fusion(f32[1,3,2,67,128]{4,0,3,2,1:T(1,128)} %collective-permute-done), kind=kLoop, calls=%fused_computation.196 | loop fusion | bytes 137216 | tf_op jit(solution)/shard_map/stack;squeeze | solution.py:90
  42.8 5.4 %collective-permute-done.3 = f32[5,1,2,67,128]{4,0,3,2,1:T(8,128)S(1)} collective-permute-done((f32[5,1,2,67,128]{4,0,3,2,1:T(8,128)S(1)}, f32[5,1,2,67,128]{4,0,3,2,1:T(8,128)S(1)}, u32[]{:S(2)}, u32[]{:S(2)}) %collective-permute-start.3) | collective-permute-done | bytes 343072 | tf_op jit(solution)/shard_map/ppermute | solution.py:21
  48.3 7.0 %collective-permute-done.2 = f32[5,1,2,67,128]{4,0,3,2,1:T(8,128)S(1)} collective-permute-done((f32[5,1,2,67,128]{4,0,3,2,1:T(8,128)S(1)}, f32[5,1,2,67,128]{4,0,3,2,1:T(8,128)S(1)}, u32[]{:S(2)}, u32[]{:S(2)}) %collective-permute-start.2) | collective-permute-done | bytes 343072 | tf_op jit(solution)/shard_map/ppermute | solution.py:19
  55.5 3.1 %stack.18 = f32[8,2,67,128]{3,0,2,1:T(8,128)S(1)} concatenate(f32[1,2,67,128]{3,0,2,1:T(1,128)S(1)} %get-tuple-element.45, f32[1,2,67,128]{3,0,2,1:T(1,128)} %slice_bitcast_fusion.8, f32[1,2,67,128]{3,0,2,1:T(1,128)S(1)} %get-tuple-element.42, f32[1,2,67,128]{3,0,2,1:T(1,128)S(1)} %get-tuple-element.44, f32[1,2,67,128]{3,0,2,1:T(1,128)S(1)} %get-tuple-element.41, ...), dimensions={0} | concatenate | bytes 1097728 | tf_op jit(solution)/shard_map/stack | solution.py:90
  63.3 3.0 %fusion.18 = f32[64,1,9,128]{3,1,2,0:T(1,128)S(1)} fusion(f32[4,64,1,1]{0,2,3,1:T(1,128)S(1)} %copy.60, f32[4,9,64,128]{3,2,1,0:T(8,128)S(1)} %bitcast.797), kind=kOutput, calls=%fused_computation.32 | convolution fusion | flops 3538944 | bytes 1475584 | tf_op jit(solution)/shard_map/jvp(kc,kmci->mci)/dot_general | solution.py:75
  70.4 3.1 %fusion.16 = f32[64,1,9,128]{3,1,2,0:T(1,128)S(1)} fusion(f32[4,64,1,1]{0,2,3,1:T(1,128)S(1)} %copy.60, f32[4,9,64,128]{3,2,1,0:T(8,128)S(1)} %bitcast.796), kind=kOutput, calls=%fused_computation.30 | convolution fusion | flops 3538944 | bytes 1475584 | tf_op jit(solution)/shard_map/jvp(kc,kmci->mci)/dot_general | solution.py:75
  77.7 0.9 fusion.2
  79.0 0.9 fusion.10
  82.3 3.1 %collective-permute-start.5 = (f32[1,3,2,3,128]{4,2,3,1,0:T(2,128)S(1)}, f32[1,3,2,3,128]{4,2,3,1,0:T(2,128)S(1)}, u32[]{:S(2)}, u32[]{:S(2)}) collective-permute-start(f32[1,3,2,3,128]{4,2,3,1,0:T(2,128)S(1)} %copy.50), channel_id=1, source_target_pairs={{96,0},{192,96},{288,192},{384,288},{480,384},{576,480},{672,576},... | collective-permute-start | bytes 27656 | tf_op jit(solution)/shard_map/ppermute | solution.py:21
  85.4 1.1 %collective-permute-start.4 = (f32[1,3,2,3,128]{4,2,3,1,0:T(2,128)S(1)}, f32[1,3,2,3,128]{4,2,3,1,0:T(2,128)S(1)}, u32[]{:S(2)}, u32[]{:S(2)}) collective-permute-start(f32[1,3,2,3,128]{4,2,3,1,0:T(2,128)S(1)} %copy.47), channel_id=1, source_target_pairs={{0,96},{96,192},{192,288},{288,384},{384,480},{480,576},{576,672},... | collective-permute-start | bytes 27656 | tf_op jit(solution)/shard_map/ppermute | solution.py:19
  86.6 1.2 %collective-permute-done.5 = f32[1,3,2,3,128]{4,2,3,1,0:T(2,128)S(1)} collective-permute-done((f32[1,3,2,3,128]{4,2,3,1,0:T(2,128)S(1)}, f32[1,3,2,3,128]{4,2,3,1,0:T(2,128)S(1)}, u32[]{:S(2)}, u32[]{:S(2)}) %collective-permute-start.5) | collective-permute-done | bytes 9248 | tf_op jit(solution)/shard_map/ppermute | solution.py:21
  87.8 1.9 %collective-permute-start.7 = (f32[5,1,2,3,128]{4,2,3,1,0:T(2,128)S(1)}, f32[5,1,2,3,128]{4,2,3,1,0:T(2,128)S(1)}, u32[]{:S(2)}, u32[]{:S(2)}) collective-permute-start(f32[5,1,2,3,128]{4,2,3,1,0:T(2,128)S(1)} %get-tuple-element.64), channel_id=1, source_target_pairs={{1,0},{2,1},{3,2},{4,3},{5,4},{6,5},{7,6},{8,7},{9,8},{10,9},{11,1... | collective-permute-start | bytes 46088 | tf_op jit(solution)/shard_map/ppermute | solution.py:21
  90.3 3.4 %collective-permute-start.6 = (f32[5,1,2,3,128]{4,2,3,1,0:T(2,128)S(1)}, f32[5,1,2,3,128]{4,2,3,1,0:T(2,128)S(1)}, u32[]{:S(2)}, u32[]{:S(2)}) collective-permute-start(f32[5,1,2,3,128]{4,2,3,1,0:T(2,128)S(1)} %get-tuple-element.65), channel_id=1, source_target_pairs={{0,1},{1,2},{2,3},{3,4},{4,5},{5,6},{6,7},{7,8},{8,9},{9,10},{10,1... | collective-permute-start | bytes 46088 | tf_op jit(solution)/shard_map/ppermute | solution.py:19
  93.7 4.4 %collective-permute-done.6 = f32[5,1,2,3,128]{4,2,3,1,0:T(2,128)S(1)} collective-permute-done((f32[5,1,2,3,128]{4,2,3,1,0:T(2,128)S(1)}, f32[5,1,2,3,128]{4,2,3,1,0:T(2,128)S(1)}, u32[]{:S(2)}, u32[]{:S(2)}) %collective-permute-start.6) | collective-permute-done | bytes 15392 | tf_op jit(solution)/shard_map/ppermute | solution.py:19
  (190 shorter events, 21.3 us)
Async XLA Ops:
  0.6 65.8 %copy-start = (f32[192,64]{0,1:T(8,128)S(1)}, f32[192,64]{0,1:T(8,128)}, u32[]{:S(2)}) copy-start(f32[192,64]{0,1:T(8,128)} %param.16) | copy-start | bytes 147460
  1.4 3.1 %copy-start.9 = (f32[3,2,128]{2,1,0:T(2,128)}, f32[3,2,128]{2,1,0:T(2,128)S(1)}, u32[]{:S(2)}) copy-start(f32[3,2,128]{2,1,0:T(2,128)S(1)} %reshape.450) | copy-start | bytes 9220
  2.3 13.3 %copy-start.14 = (s32[2,2]{1,0:T(2,128)S(1)}, s32[2,2]{1,0:T(2,128)}, u32[]{:S(2)}) copy-start(s32[2,2]{1,0:T(2,128)} %param.11) | copy-start | bytes 52
  2.4 18.5 %copy-start.5 = (f32[64,2,128]{2,1,0:T(2,128)}, f32[64,2,128]{2,1,0:T(2,128)S(1)}, u32[]{:S(2)}) copy-start(f32[64,2,128]{2,1,0:T(2,128)S(1)} %reshape.449) | copy-start | bytes 196612
  4.3 17.3 %copy-start.11 = (f32[4,64]{1,0:T(4,128)S(1)}, f32[4,64]{1,0:T(4,128)}, u32[]{:S(2)}) copy-start(f32[4,64]{1,0:T(4,128)} %param.15) | copy-start | bytes 3076
  4.3 17.5 %copy-start.7 = (s32[2,2,128,128]{3,2,1,0:T(8,128)S(1)}, s32[2,2,128,128]{3,2,1,0:T(8,128)}, u32[]{:S(2)}) copy-start(s32[2,2,128,128]{3,2,1,0:T(8,128)} %param.12) | copy-start | bytes 786436
  4.5 23.2 %collective-permute-start = (f32[1,3,2,67,128]{4,0,3,2,1:T(1,128)S(1)}, f32[1,3,2,67,128]{4,0,3,2,1:T(1,128)}, u32[]{:S(2)}, u32[]{:S(2)}) collective-permute-start(f32[1,3,2,67,128]{4,0,3,2,1:T(1,128)S(1)} %copy.42), channel_id=1, source_target_pairs={{0,96},{96,192},{192,288},{288,384},{384,480},{480,576},{576,672},... | collective-permute-start | bytes 617480 | tf_op jit(solution)/shard_map/ppermute | solution.py:19
  7.1 19.4 %collective-permute-start.1 = (f32[1,3,2,67,128]{4,1,3,2,0:T(4,128)}, f32[1,3,2,67,128]{4,1,3,2,0:T(4,128)}, u32[]{:S(2)}, u32[]{:S(2)}) collective-permute-start(f32[1,3,2,67,128]{4,1,3,2,0:T(4,128)} %get-tuple-element.47), channel_id=1, source_target_pairs={{96,0},{192,96},{288,192},{384,288},{480,384},{576,480},{672,576},... | collective-permute-start | bytes 617480 | tf_op jit(solution)/shard_map/ppermute | solution.py:21
  22.8 3.2 %copy-start.6 = (f32[64,2,128]{2,1,0:T(2,128)S(1)}, f32[64,2,128]{2,1,0:T(2,128)}, u32[]{:S(2)}) copy-start(f32[64,2,128]{2,1,0:T(2,128)} %copy-done.5) | copy-start | bytes 196612
  29.0 19.1 %collective-permute-start.3 = (f32[5,1,2,67,128]{4,0,3,2,1:T(8,128)S(1)}, f32[5,1,2,67,128]{4,0,3,2,1:T(8,128)S(1)}, u32[]{:S(2)}, u32[]{:S(2)}) collective-permute-start(f32[5,1,2,67,128]{4,0,3,2,1:T(8,128)S(1)} %get-tuple-element.30), channel_id=1, source_target_pairs={{1,0},{2,1},{3,2},{4,3},{5,4},{6,5},{7,6},{8,7},{9,8},{10,9},{11,1... | collective-permute-start | bytes 1029128 | tf_op jit(solution)/shard_map/ppermute | solution.py:21
  38.3 17.0 %collective-permute-start.2 = (f32[5,1,2,67,128]{4,0,3,2,1:T(8,128)S(1)}, f32[5,1,2,67,128]{4,0,3,2,1:T(8,128)S(1)}, u32[]{:S(2)}, u32[]{:S(2)}) collective-permute-start(f32[5,1,2,67,128]{4,0,3,2,1:T(8,128)S(1)} %get-tuple-element.31), channel_id=1, source_target_pairs={{0,1},{1,2},{2,3},{3,4},{4,5},{5,6},{6,7},{7,8},{8,9},{9,10},{10,1... | collective-permute-start | bytes 1029128 | tf_op jit(solution)/shard_map/ppermute | solution.py:19
  55.5 3.4 %copy-start.10 = (f32[3,2,128]{2,1,0:T(2,128)S(1)}, f32[3,2,128]{2,1,0:T(2,128)}, u32[]{:S(2)}) copy-start(f32[3,2,128]{2,1,0:T(2,128)} %copy-done.9) | copy-start | bytes 9220
  59.7 1.2 %copy-start.18 = (f32[4]{0:T(128)S(1)}, f32[4]{0:T(128)}, u32[]{:S(2)}) copy-start(f32[4]{0:T(128)} %convert_add_fusion) | copy-start | bytes 52
  59.9 1.3 %copy-start.4 = (f32[128,128]{1,0:T(8,128)S(1)}, f32[128,128]{1,0:T(8,128)}, u32[]{:S(2)}) copy-start(f32[128,128]{1,0:T(8,128)} %get-tuple-element.55) | copy-start | bytes 196612
  61.5 0.8 copy-start.3
  63.3 3.4 %copy-start.15 = (f32[64]{0:T(128)S(1)}, f32[64]{0:T(128)}, u32[]{:S(2)}) copy-start(f32[64]{0:T(128)} %param.17) | copy-start | bytes 772
  67.4 0.8 copy-start.2
  68.6 0.8 copy-start.1
  81.2 5.3 %copy-start.17 = (f32[9]{0:T(128)S(1)}, f32[9]{0:T(128)}, u32[]{:S(2)}) copy-start(f32[9]{0:T(128)} %copy-done.16) | copy-start | bytes 112
  81.2 17.0 %copy-start.13 = (s32[1,1,8,2]{2,3,1,0:T(2,128)S(1)}, s32[1,1,8,2]{2,3,1,0:T(2,128)}, u32[]{:S(2)}) copy-start(s32[1,1,8,2]{2,3,1,0:T(2,128)} %param.13) | copy-start | bytes 196
  82.3 5.5 %collective-permute-start.5 = (f32[1,3,2,3,128]{4,2,3,1,0:T(2,128)S(1)}, f32[1,3,2,3,128]{4,2,3,1,0:T(2,128)S(1)}, u32[]{:S(2)}, u32[]{:S(2)}) collective-permute-start(f32[1,3,2,3,128]{4,2,3,1,0:T(2,128)S(1)} %copy.50), channel_id=1, source_target_pairs={{96,0},{192,96},{288,192},{384,288},{480,384},{576,480},{672,576},... | collective-permute-start | bytes 27656 | tf_op jit(solution)/shard_map/ppermute | solution.py:21
  85.4 2.4 %collective-permute-start.4 = (f32[1,3,2,3,128]{4,2,3,1,0:T(2,128)S(1)}, f32[1,3,2,3,128]{4,2,3,1,0:T(2,128)S(1)}, u32[]{:S(2)}, u32[]{:S(2)}) collective-permute-start(f32[1,3,2,3,128]{4,2,3,1,0:T(2,128)S(1)} %copy.47), channel_id=1, source_target_pairs={{0,96},{96,192},{192,288},{288,384},{384,480},{480,576},{576,672},... | collective-permute-start | bytes 27656 | tf_op jit(solution)/shard_map/ppermute | solution.py:19
  87.8 5.9 %collective-permute-start.7 = (f32[5,1,2,3,128]{4,2,3,1,0:T(2,128)S(1)}, f32[5,1,2,3,128]{4,2,3,1,0:T(2,128)S(1)}, u32[]{:S(2)}, u32[]{:S(2)}) collective-permute-start(f32[5,1,2,3,128]{4,2,3,1,0:T(2,128)S(1)} %get-tuple-element.64), channel_id=1, source_target_pairs={{1,0},{2,1},{3,2},{4,3},{5,4},{6,5},{7,6},{8,7},{9,8},{10,9},{11,1... | collective-permute-start | bytes 46088 | tf_op jit(solution)/shard_map/ppermute | solution.py:21
  90.3 7.8 %collective-permute-start.6 = (f32[5,1,2,3,128]{4,2,3,1,0:T(2,128)S(1)}, f32[5,1,2,3,128]{4,2,3,1,0:T(2,128)S(1)}, u32[]{:S(2)}, u32[]{:S(2)}) collective-permute-start(f32[5,1,2,3,128]{4,2,3,1,0:T(2,128)S(1)} %get-tuple-element.65), channel_id=1, source_target_pairs={{0,1},{1,2},{2,3},{3,4},{4,5},{5,6},{6,7},{7,8},{8,9},{9,10},{10,1... | collective-permute-start | bytes 46088 | tf_op jit(solution)/shard_map/ppermute | solution.py:19
  (3 other events, 2.0 us)
where the time goes:
time: 100 us; the launch traced here: 99 us
  starting transfers between devices  31.2 us (31%)
  waiting for transfers between devices  18 us (18%)
  matrix products  14.3 us (14%)
  local copies, waits for them, and re-layouts  13.6 us (14%)
  other arithmetic  12.3 us (12%)
  between operations  9.62 us (10%)
    ppermute x4, starting transfers between devices, extended(): lax.ppermute(head, axis, [((i + 1) % count, i) for i in range(count)])  22.2 us
    ppermute x4, waiting for transfers between devices, extended(): lax.ppermute(tail, axis, [(i, (i + 1) % count) for i in range(count)])  11.4 us
    ppermute x4, starting transfers between devices, extended(): lax.ppermute(tail, axis, [(i, (i + 1) % count) for i in range(count)])  9 us
    ppermute x4, waiting for transfers between devices, extended(): lax.ppermute(head, axis, [((i + 1) % count, i) for i in range(count)])  6.61 us
    another operation x7, local copies, waits for them, and re-layouts, collect(): jnp.stack([padded[2 + 2 * pair[0], 2 + 2 * pair[1]] for pair in OFFSETS],...  6.22 us
    dot_general x2, matrix products, atom_energy(): message = jnp.einsum('kc,kmci->mci', radial, proj, precision=HIGHEST)  6.1 us
    dot_general x8, matrix products, tile_terms(): jnp.einsum('qij,cj->qci', tiles.astype(jnp.bfloat16), other_feat, preferr...  4.2 us
    unnamed x50, local copies, waits for them, and re-layouts  2.71 us
  transfers between devices with their start and end apart: 8, of which 4 were waited for; matrix products, arithmetic and copies ran while one was open for 8% of the time, Pallas kernels for 0%

commit v1 on v0

--- a/solution.py
+++ b/solution.py
@@ -7,22 +7,6 @@
 
 OFFSETS = ((-1, -1), (-1, 0), (-1, 1), (0, -1), (0, 1), (1, -1), (1, 0), (1, 1))
 HIGHEST = lax.Precision.HIGHEST
-
-
-def extended(cells, sides, width):
-    for axis, dim in sides:
-        count = lax.axis_size(axis)
-        head = lax.slice_in_dim(cells, 0, width, axis=dim)
-        tail = lax.slice_in_dim(cells, cells.shape[dim] - width, cells.shape[dim], axis=dim)
-        cells = jnp.concatenate(
-            [
-                lax.ppermute(tail, axis, [(i, (i + 1) % count) for i in range(count)]),
-                cells,
-                lax.ppermute(head, axis, [((i + 1) % count, i) for i in range(count)]),
-            ],
-            axis=dim,
-        )
-    return cells
 
 
 def harmonics(rel, dist):
@@ -80,22 +64,15 @@
     return jnp.dot(readout, hidden, precision=HIGHEST)
 
 
-def place(parts):
-    empty = jnp.zeros_like(parts[0:1])
-    full = jnp.concatenate([parts[:4], empty, parts[4:]], axis=0)
-    return full.reshape((3, 3) + parts.shape[1:])
-
-
-def collect(padded):
-    return jnp.stack([padded[2 + 2 * pair[0], 2 + 2 * pair[1]] for pair in OFFSETS], axis=0)
-
-
-def exchange_ghosts(grid):
-    return extended(grid, (("gx", 0), ("gy", 1)), 1)
-
-
-def return_forces(grid):
-    return extended(grid, (("gx", 0), ("gy", 1)), 1)
+def neighbour_shift(x, offset):
+    count_x = lax.axis_size("gx")
+    count_y = lax.axis_size("gy")
+    pairs = []
+    for a in range(count_x):
+        for b in range(count_y):
+            target = ((a + offset[0]) % count_x) * count_y + (b + offset[1]) % count_y
+            pairs.append((a * count_y + b, target))
+    return lax.ppermute(x, ("gx", "gy"), pairs)
 
 
 def local(
@@ -104,23 +81,31 @@
     atoms = pair_masks.shape[2]
     blocks = positions.shape[1] // atoms
     kinds = embedding.shape[0]
-    width = embedding.shape[1]
     sends = send_lists.shape[3]
     own_pos = positions.reshape(3, blocks, atoms).transpose(1, 0, 2)
-    onehot = (species[None, :] == jnp.arange(kinds)[:, None]).astype(jnp.float32)
-    feats = (
-        jnp.dot(embedding.T, onehot, precision=HIGHEST)
-        .reshape(width, blocks, atoms)
-        .transpose(1, 0, 2)
-    )
-    payload = jnp.concatenate([own_pos, feats], axis=1)
+    own_kind = species.reshape(blocks, 1, atoms).astype(jnp.float32)
+    payload = jnp.concatenate([own_pos, own_kind], axis=1)
     chosen = send_lists.reshape(8, sends)
     pick = (chosen[:, :, None] == jnp.arange(blocks)).astype(jnp.float32)
     outgoing = jnp.einsum("dgb,bra->dgra", pick, payload, precision=HIGHEST)
-    incoming = collect(exchange_ghosts(place(outgoing))).reshape(8 * sends, payload.shape[1], atoms)
+    incoming = jnp.stack(
+        [neighbour_shift(outgoing[7 - d], OFFSETS[7 - d]) for d in range(8)], axis=0
+    ).reshape(8 * sends, 4, atoms)
     ghost_pos = incoming[:, :3]
-    ghost_feat = incoming[:, 3:].astype(jnp.bfloat16)
-    own_feat = feats.astype(jnp.bfloat16)
+    ghost_kind = incoming[:, 3]
+
+    def features(kind):
+        onehot = (kind[None, :] == jnp.arange(kinds).astype(kind.dtype)[:, None]).astype(jnp.float32)
+        return jnp.dot(embedding.T, onehot, precision=HIGHEST)
+
+    own_feats = features(species)
+    own_feat = own_feats.reshape(-1, blocks, atoms).transpose(1, 0, 2).astype(jnp.bfloat16)
+    ghost_feat = (
+        features(ghost_kind.reshape(-1))
+        .reshape(-1, 8 * sends, atoms)
+        .transpose(1, 0, 2)
+        .astype(jnp.bfloat16)
+    )
 
     def energies_of(own_now, ghost_now):
         table_pos = jnp.concatenate([own_now, ghost_now], axis=0)
@@ -143,7 +128,10 @@
 
     energy, pullback = jax.vjp(energies_of, own_pos, ghost_pos)
     grad_own, grad_ghost = pullback(jnp.ones_like(energy))
-    returned = collect(return_forces(place(grad_ghost.reshape(8, sends, 3, atoms))))
+    grad_ghost = grad_ghost.reshape(8, sends, 3, atoms)
+    returned = jnp.stack(
+        [neighbour_shift(grad_ghost[7 - e], OFFSETS[7 - e]) for e in range(8)], axis=0
+    )
     back = jnp.einsum("dgb,dgca->bca", pick, returned, precision=HIGHEST)
     forces = -(grad_own + back)
     return (energy.reshape(blocks * atoms), forces.transpose(1, 0, 2).reshape(3, blocks * atoms))

time: 100 us -> 122 us (1.22)
  starting transfers between devices: 31.2 us -> 73.6 us
  local copies, waits for them, and re-layouts: 13.6 us -> 4.65 us
  waiting for transfers between devices: 18 us -> 9.06 us
  other arithmetic: 12.3 us -> 9.97 us
    ppermute x8 -> x16, starting transfers between devices: 31.2 us -> 73.6 us  [neighbour_shift(): return lax.ppermute(x, ('gx', 'gy'), pairs)]
    ppermute x8 -> x16, waiting for transfers between devices: 18 us -> 9.06 us  [neighbour_shift(): return lax.ppermute(x, ('gx', 'gy'), pairs)]
    another operation x7 -> x2, local copies, waits for them, and re-layouts: 6.22 us -> 0.06 us  [the longest x1 0.05 us: local(): jnp.stack([neighbour_shift(grad_ghost[7 - e], OFFSETS[7 - e]) for e in ra...]
    concatenate x6 -> x0, other arithmetic: 2.15 us -> none  [the longest x2 1.28 us: extended(): jnp.concatenate([lax.ppermute(tail, axis, [(i, (i + 1) % count) for i in...]
    unnamed x50 -> x25, local copies, waits for them, and re-layouts: 2.71 us -> 2.02 us
  transfers between devices with their start and end apart: 8 -> 16, of which waited for: 4 -> 4; matrix products, arithmetic and copies ran while one was open for 8% -> 4% of each run, Pallas kernels for 0% -> 0%
where the time goes in v1:
time: 122 us; the launch traced here: 121 us
  starting transfers between devices  73.6 us (60%)
  matrix products  14.3 us (12%)
  other arithmetic  9.97 us (8%)
  between operations  9.38 us (8%)
  waiting for transfers between devices  9.06 us (7%)
  local copies, waits for them, and re-layouts  4.65 us (4%)
    ppermute x16, starting transfers between devices, neighbour_shift(): return lax.ppermute(x, ('gx', 'gy'), pairs)  73.6 us
    ppermute x16, waiting for transfers between devices, neighbour_shift(): return lax.ppermute(x, ('gx', 'gy'), pairs)  9.06 us
    dot_general x2, matrix products, atom_energy(): message = jnp.einsum('kc,kmci->mci', radial, proj, precision=HIGHEST)  6.1 us
    dot_general x8, matrix products, tile_terms(): jnp.einsum('qij,cj->qci', tiles.astype(jnp.bfloat16), other_feat, preferr...  4.21 us
  transfers between devices with their start and end apart: 16, of which 4 were waited for; matrix products, arithmetic and copies ran while one was open for 4% of the time, Pallas kernels for 0%

profile of v1, /device:TPU:1, one launch (start us, length us, event | category | flops | bytes accessed | tf_op | source)
XLA Modules:
  0.0 120.9 jit_solution(8263032103143468464)
XLA Ops:
  3.0 4.6 %collective-permute-start.5 = (f32[2,4,128]{2,1,0:T(4,128)S(1)}, f32[2,4,128]{2,1,0:T(4,128)S(1)}, u32[]{:S(2)}, u32[]{:S(2)}) collective-permute-start(f32[2,4,128]{2,1,0:T(4,128)S(1)} %bitcast.873), channel_id=1, source_target_pairs={{0,673},{1,674},{2,675},{3,676},{4,677},{5,678},{6,679},{7,680},{8... | collective-permute-start | bytes 12296 | tf_op jit(solution)/shard_map/ppermute | solution.py:75
  7.6 15.9 %collective-permute-start.7 = (f32[2,4,128]{2,1,0:T(4,128)S(1)}, f32[2,4,128]{2,1,0:T(4,128)S(1)}, u32[]{:S(2)}, u32[]{:S(2)}) collective-permute-start(f32[2,4,128]{2,1,0:T(4,128)S(1)} %bitcast.871), channel_id=1, source_target_pairs={{0,767},{1,672},{2,673},{3,674},{4,675},{5,676},{6,677},{7,678},{8... | collective-permute-start | bytes 12296 | tf_op jit(solution)/shard_map/ppermute | solution.py:75
  23.5 5.3 %collective-permute-start.4 = (f32[2,4,128]{2,1,0:T(4,128)S(1)}, f32[2,4,128]{2,1,0:T(4,128)S(1)}, u32[]{:S(2)}, u32[]{:S(2)}) collective-permute-start(f32[2,4,128]{2,1,0:T(4,128)S(1)} %bitcast.874), channel_id=1, source_target_pairs={{0,95},{1,0},{2,1},{3,2},{4,3},{5,4},{6,5},{7,6},{8,7},{9,8},{10,9... | collective-permute-start | bytes 12296 | tf_op jit(solution)/shard_map/ppermute | solution.py:75
  28.8 1.9 %collective-permute-start.3 = (f32[2,4,128]{2,1,0:T(4,128)S(1)}, f32[2,4,128]{2,1,0:T(4,128)S(1)}, u32[]{:S(2)}, u32[]{:S(2)}) collective-permute-start(f32[2,4,128]{2,1,0:T(4,128)S(1)} %bitcast.875), channel_id=1, source_target_pairs={{0,1},{1,2},{2,3},{3,4},{4,5},{5,6},{6,7},{7,8},{8,9},{9,10},{10,1... | collective-permute-start | bytes 12296 | tf_op jit(solution)/shard_map/ppermute | solution.py:75
  30.7 1.9 %collective-permute-start = (f32[2,4,128]{2,1,0:T(4,128)S(1)}, f32[2,4,128]{2,1,0:T(4,128)S(1)}, u32[]{:S(2)}, u32[]{:S(2)}) collective-permute-start(f32[2,4,128]{2,1,0:T(4,128)S(1)} %bitcast.878), channel_id=1, source_target_pairs={{0,97},{1,98},{2,99},{3,100},{4,101},{5,102},{6,103},{7,104},{8,10... | collective-permute-start | bytes 12296 | tf_op jit(solution)/shard_map/ppermute | solution.py:75
  32.7 1.5 %fusion.293 = (s32[1,1]{1,0:T(1,128)}, s32[1,1]{1,0:T(1,128)}, s32[1,1]{1,0:T(1,128)}, s32[1,1]{1,0:T(1,128)}) fusion(s32[2,2]{1,0:T(2,128)} %param.11), kind=kLoop, calls=%fused_computation.546 | loop fusion | bytes 32 | tf_op jit(solution)/shard_map/jvp()/slice | solution.py:54
  34.2 0.9 fusion.21
  35.2 1.0 multiply_bitcast_fusion.2
  44.6 1.6 %collective-permute-done.1 = f32[2,4,128]{2,1,0:T(4,128)S(1)} collective-permute-done((f32[2,4,128]{2,1,0:T(4,128)S(1)}, f32[2,4,128]{2,1,0:T(4,128)S(1)}, u32[]{:S(2)}, u32[]{:S(2)}) %collective-permute-start.1) | collective-permute-done | bytes 4128 | tf_op jit(solution)/shard_map/ppermute | solution.py:75
  46.2 7.9 %collective-permute-start.2 = (f32[2,4,128]{2,1,0:T(4,128)S(1)}, f32[2,4,128]{2,1,0:T(4,128)S(1)}, u32[]{:S(2)}, u32[]{:S(2)}) collective-permute-start(f32[2,4,128]{2,1,0:T(4,128)S(1)} %bitcast.876), channel_id=1, source_target_pairs={{0,191},{1,96},{2,97},{3,98},{4,99},{5,100},{6,101},{7,102},{8,103... | collective-permute-start | bytes 12296 | tf_op jit(solution)/shard_map/ppermute | solution.py:75
  54.9 2.0 %collective-permute-start.6 = (f32[2,4,128]{2,1,0:T(4,128)S(1)}, f32[2,4,128]{2,1,0:T(4,128)S(1)}, u32[]{:S(2)}, u32[]{:S(2)}) collective-permute-start(f32[2,4,128]{2,1,0:T(4,128)S(1)} %bitcast.872), channel_id=1, source_target_pairs={{0,672},{1,673},{2,674},{3,675},{4,676},{5,677},{6,678},{7,679},{8... | collective-permute-start | bytes 12296 | tf_op jit(solution)/shard_map/ppermute | solution.py:75
  56.9 1.0 collective-permute-done.6
  61.6 3.0 %fusion.18 = f32[64,1,9,128]{3,1,2,0:T(1,128)S(1)} fusion(f32[4,64,1,1]{0,2,3,1:T(1,128)S(1)} %copy.45, f32[4,9,64,128]{3,2,1,0:T(8,128)S(1)} %bitcast.838), kind=kOutput, calls=%fused_computation.33 | convolution fusion | flops 3538944 | bytes 1475584 | tf_op jit(solution)/shard_map/jvp(kc,kmci->mci)/dot_general | solution.py:59
  67.9 3.1 %fusion.16 = f32[64,1,9,128]{3,1,2,0:T(1,128)S(1)} fusion(f32[4,64,1,1]{0,2,3,1:T(1,128)S(1)} %copy.45, f32[4,9,64,128]{3,2,1,0:T(8,128)S(1)} %bitcast.837), kind=kOutput, calls=%fused_computation.31 | convolution fusion | flops 3538944 | bytes 1475584 | tf_op jit(solution)/shard_map/jvp(kc,kmci->mci)/dot_general | solution.py:59
  75.0 0.9 fusion.2
  76.3 0.9 fusion.10
  79.6 10.4 %collective-permute-start.15 = (f32[2,3,128]{2,0,1:T(2,128)S(1)}, f32[2,3,128]{2,0,1:T(2,128)S(1)}, u32[]{:S(2)}, u32[]{:S(2)}) collective-permute-start(f32[2,3,128]{2,0,1:T(2,128)S(1)} %get-tuple-element.48), channel_id=1, source_target_pairs={{0,767},{1,672},{2,673},{3,674},{4,675},{5,676},{6,677},{7,678},{8... | collective-permute-start | bytes 9224 | tf_op jit(solution)/shard_map/ppermute | solution.py:75
  90.0 2.8 %collective-permute-start.14 = (f32[2,3,128]{2,0,1:T(2,128)S(1)}, f32[2,3,128]{2,0,1:T(2,128)S(1)}, u32[]{:S(2)}, u32[]{:S(2)}) collective-permute-start(f32[2,3,128]{2,0,1:T(2,128)S(1)} %get-tuple-element.49), channel_id=1, source_target_pairs={{0,672},{1,673},{2,674},{3,675},{4,676},{5,677},{6,678},{7,679},{8... | collective-permute-start | bytes 9224 | tf_op jit(solution)/shard_map/ppermute | solution.py:75
  92.8 1.9 %collective-permute-start.13 = (f32[2,3,128]{2,0,1:T(2,128)S(1)}, f32[2,3,128]{2,0,1:T(2,128)S(1)}, u32[]{:S(2)}, u32[]{:S(2)}) collective-permute-start(f32[2,3,128]{2,0,1:T(2,128)S(1)} %get-tuple-element.50), channel_id=1, source_target_pairs={{0,673},{1,674},{2,675},{3,676},{4,677},{5,678},{6,679},{7,680},{8... | collective-permute-start | bytes 9224 | tf_op jit(solution)/shard_map/ppermute | solution.py:75
  94.7 6.6 %collective-permute-start.12 = (f32[2,3,128]{2,0,1:T(2,128)S(1)}, f32[2,3,128]{2,0,1:T(2,128)S(1)}, u32[]{:S(2)}, u32[]{:S(2)}) collective-permute-start(f32[2,3,128]{2,0,1:T(2,128)S(1)} %get-tuple-element.51), channel_id=1, source_target_pairs={{0,95},{1,0},{2,1},{3,2},{4,3},{5,4},{6,5},{7,6},{8,7},{9,8},{10,9... | collective-permute-start | bytes 9224 | tf_op jit(solution)/shard_map/ppermute | solution.py:75
  101.3 1.9 %collective-permute-start.11 = (f32[2,3,128]{2,0,1:T(2,128)S(1)}, f32[2,3,128]{2,0,1:T(2,128)S(1)}, u32[]{:S(2)}, u32[]{:S(2)}) collective-permute-start(f32[2,3,128]{2,0,1:T(2,128)S(1)} %get-tuple-element.52), channel_id=1, source_target_pairs={{0,1},{1,2},{2,3},{3,4},{4,5},{5,6},{6,7},{7,8},{8,9},{9,10},{10,1... | collective-permute-start | bytes 9224 | tf_op jit(solution)/shard_map/ppermute | solution.py:75
  103.2 8.5 %collective-permute-start.10 = (f32[2,3,128]{2,0,1:T(2,128)S(1)}, f32[2,3,128]{2,0,1:T(2,128)S(1)}, u32[]{:S(2)}, u32[]{:S(2)}) collective-permute-start(f32[2,3,128]{2,0,1:T(2,128)S(1)} %get-tuple-element.53), channel_id=1, source_target_pairs={{0,191},{1,96},{2,97},{3,98},{4,99},{5,100},{6,101},{7,102},{8,103... | collective-permute-start | bytes 9224 | tf_op jit(solution)/shard_map/ppermute | solution.py:75
  111.8 1.9 %collective-permute-start.8 = (f32[2,3,128]{2,0,1:T(2,128)S(1)}, f32[2,3,128]{2,0,1:T(2,128)S(1)}, u32[]{:S(2)}, u32[]{:S(2)}) collective-permute-start(f32[2,3,128]{2,0,1:T(2,128)S(1)} %get-tuple-element.55), channel_id=1, source_target_pairs={{0,97},{1,98},{2,99},{3,100},{4,101},{5,102},{6,103},{7,104},{8,10... | collective-permute-start | bytes 9224 | tf_op jit(solution)/shard_map/ppermute | solution.py:75
  114.3 5.7 %collective-permute-done.8 = f32[2,3,128]{2,0,1:T(2,128)S(1)} collective-permute-done((f32[2,3,128]{2,0,1:T(2,128)S(1)}, f32[2,3,128]{2,0,1:T(2,128)S(1)}, u32[]{:S(2)}, u32[]{:S(2)}) %collective-permute-start.8) | collective-permute-done | bytes 3104 | tf_op jit(solution)/shard_map/ppermute | solution.py:75
  (160 shorter events, 18.3 us)
Async XLA Ops:
  0.6 64.1 %copy-start = (f32[192,64]{0,1:T(8,128)S(1)}, f32[192,64]{0,1:T(8,128)}, u32[]{:S(2)}) copy-start(f32[192,64]{0,1:T(8,128)} %param.16) | copy-start | bytes 147460
  0.6 57.3 %copy-start.3 = (f32[4,64]{1,0:T(4,128)S(1)}, f32[4,64]{1,0:T(4,128)}, u32[]{:S(2)}) copy-start(f32[4,64]{1,0:T(4,128)} %param.14) | copy-start | bytes 3076
  3.0 53.9 %collective-permute-start.5 = (f32[2,4,128]{2,1,0:T(4,128)S(1)}, f32[2,4,128]{2,1,0:T(4,128)S(1)}, u32[]{:S(2)}, u32[]{:S(2)}) collective-permute-start(f32[2,4,128]{2,1,0:T(4,128)S(1)} %bitcast.873), channel_id=1, source_target_pairs={{0,673},{1,674},{2,675},{3,676},{4,677},{5,678},{6,679},{7,680},{8... | collective-permute-start | bytes 12296 | tf_op jit(solution)/shard_map/ppermute | solution.py:75
  7.6 50.3 %collective-permute-start.7 = (f32[2,4,128]{2,1,0:T(4,128)S(1)}, f32[2,4,128]{2,1,0:T(4,128)S(1)}, u32[]{:S(2)}, u32[]{:S(2)}) collective-permute-start(f32[2,4,128]{2,1,0:T(4,128)S(1)} %bitcast.871), channel_id=1, source_target_pairs={{0,767},{1,672},{2,673},{3,674},{4,675},{5,676},{6,677},{7,678},{8... | collective-permute-start | bytes 12296 | tf_op jit(solution)/shard_map/ppermute | solution.py:75
  23.5 33.3 %collective-permute-start.4 = (f32[2,4,128]{2,1,0:T(4,128)S(1)}, f32[2,4,128]{2,1,0:T(4,128)S(1)}, u32[]{:S(2)}, u32[]{:S(2)}) collective-permute-start(f32[2,4,128]{2,1,0:T(4,128)S(1)} %bitcast.874), channel_id=1, source_target_pairs={{0,95},{1,0},{2,1},{3,2},{4,3},{5,4},{6,5},{7,6},{8,7},{9,8},{10,9... | collective-permute-start | bytes 12296 | tf_op jit(solution)/shard_map/ppermute | solution.py:75
  28.8 28.0 %collective-permute-start.3 = (f32[2,4,128]{2,1,0:T(4,128)S(1)}, f32[2,4,128]{2,1,0:T(4,128)S(1)}, u32[]{:S(2)}, u32[]{:S(2)}) collective-permute-start(f32[2,4,128]{2,1,0:T(4,128)S(1)} %bitcast.875), channel_id=1, source_target_pairs={{0,1},{1,2},{2,3},{3,4},{4,5},{5,6},{6,7},{7,8},{8,9},{9,10},{10,1... | collective-permute-start | bytes 12296 | tf_op jit(solution)/shard_map/ppermute | solution.py:75
  30.7 13.9 %collective-permute-start = (f32[2,4,128]{2,1,0:T(4,128)S(1)}, f32[2,4,128]{2,1,0:T(4,128)S(1)}, u32[]{:S(2)}, u32[]{:S(2)}) collective-permute-start(f32[2,4,128]{2,1,0:T(4,128)S(1)} %bitcast.878), channel_id=1, source_target_pairs={{0,97},{1,98},{2,99},{3,100},{4,101},{5,102},{6,103},{7,104},{8,10... | collective-permute-start | bytes 12296 | tf_op jit(solution)/shard_map/ppermute | solution.py:75
  44.6 1.6 %collective-permute-start.1 = (f32[2,4,128]{2,1,0:T(4,128)S(1)}, f32[2,4,128]{2,1,0:T(4,128)S(1)}, u32[]{:S(2)}, u32[]{:S(2)}) collective-permute-start(f32[2,4,128]{2,1,0:T(4,128)S(1)} %bitcast.877), channel_id=1, source_target_pairs={{0,96},{1,97},{2,98},{3,99},{4,100},{5,101},{6,102},{7,103},{8,104... | collective-permute-start | bytes 12296 | tf_op jit(solution)/shard_map/ppermute | solution.py:75
  46.2 8.7 %collective-permute-start.2 = (f32[2,4,128]{2,1,0:T(4,128)S(1)}, f32[2,4,128]{2,1,0:T(4,128)S(1)}, u32[]{:S(2)}, u32[]{:S(2)}) collective-permute-start(f32[2,4,128]{2,1,0:T(4,128)S(1)} %bitcast.876), channel_id=1, source_target_pairs={{0,191},{1,96},{2,97},{3,98},{4,99},{5,100},{6,101},{7,102},{8,103... | collective-permute-start | bytes 12296 | tf_op jit(solution)/shard_map/ppermute | solution.py:75
  54.9 3.0 %collective-permute-start.6 = (f32[2,4,128]{2,1,0:T(4,128)S(1)}, f32[2,4,128]{2,1,0:T(4,128)S(1)}, u32[]{:S(2)}, u32[]{:S(2)}) collective-permute-start(f32[2,4,128]{2,1,0:T(4,128)S(1)} %bitcast.872), channel_id=1, source_target_pairs={{0,672},{1,673},{2,674},{3,675},{4,676},{5,677},{6,678},{7,679},{8... | collective-permute-start | bytes 12296 | tf_op jit(solution)/shard_map/ppermute | solution.py:75
  61.6 3.4 %copy-start.4 = (f32[64]{0:T(128)S(1)}, f32[64]{0:T(128)}, u32[]{:S(2)}) copy-start(f32[64]{0:T(128)} %param.17) | copy-start | bytes 772
  71.8 0.7 copy-start.1
  78.5 41.6 %copy-start.2 = (s32[1,1,8,2]{2,3,1,0:T(2,128)S(1)}, s32[1,1,8,2]{2,3,1,0:T(2,128)}, u32[]{:S(2)}) copy-start(s32[1,1,8,2]{2,3,1,0:T(2,128)} %param.13) | copy-start | bytes 196
  79.6 23.7 %collective-permute-start.15 = (f32[2,3,128]{2,0,1:T(2,128)S(1)}, f32[2,3,128]{2,0,1:T(2,128)S(1)}, u32[]{:S(2)}, u32[]{:S(2)}) collective-permute-start(f32[2,3,128]{2,0,1:T(2,128)S(1)} %get-tuple-element.48), channel_id=1, source_target_pairs={{0,767},{1,672},{2,673},{3,674},{4,675},{5,676},{6,677},{7,678},{8... | collective-permute-start | bytes 9224 | tf_op jit(solution)/shard_map/ppermute | solution.py:75
  90.0 21.8 %collective-permute-start.14 = (f32[2,3,128]{2,0,1:T(2,128)S(1)}, f32[2,3,128]{2,0,1:T(2,128)S(1)}, u32[]{:S(2)}, u32[]{:S(2)}) collective-permute-start(f32[2,3,128]{2,0,1:T(2,128)S(1)} %get-tuple-element.49), channel_id=1, source_target_pairs={{0,672},{1,673},{2,674},{3,675},{4,676},{5,677},{6,678},{7,679},{8... | collective-permute-start | bytes 9224 | tf_op jit(solution)/shard_map/ppermute | solution.py:75
  92.8 19.0 %collective-permute-start.13 = (f32[2,3,128]{2,0,1:T(2,128)S(1)}, f32[2,3,128]{2,0,1:T(2,128)S(1)}, u32[]{:S(2)}, u32[]{:S(2)}) collective-permute-start(f32[2,3,128]{2,0,1:T(2,128)S(1)} %get-tuple-element.50), channel_id=1, source_target_pairs={{0,673},{1,674},{2,675},{3,676},{4,677},{5,678},{6,679},{7,680},{8... | collective-permute-start | bytes 9224 | tf_op jit(solution)/shard_map/ppermute | solution.py:75
  94.7 19.6 %collective-permute-start.12 = (f32[2,3,128]{2,0,1:T(2,128)S(1)}, f32[2,3,128]{2,0,1:T(2,128)S(1)}, u32[]{:S(2)}, u32[]{:S(2)}) collective-permute-start(f32[2,3,128]{2,0,1:T(2,128)S(1)} %get-tuple-element.51), channel_id=1, source_target_pairs={{0,95},{1,0},{2,1},{3,2},{4,3},{5,4},{6,5},{7,6},{8,7},{9,8},{10,9... | collective-permute-start | bytes 9224 | tf_op jit(solution)/shard_map/ppermute | solution.py:75
  101.3 13.0 %collective-permute-start.11 = (f32[2,3,128]{2,0,1:T(2,128)S(1)}, f32[2,3,128]{2,0,1:T(2,128)S(1)}, u32[]{:S(2)}, u32[]{:S(2)}) collective-permute-start(f32[2,3,128]{2,0,1:T(2,128)S(1)} %get-tuple-element.52), channel_id=1, source_target_pairs={{0,1},{1,2},{2,3},{3,4},{4,5},{5,6},{6,7},{7,8},{8,9},{9,10},{10,1... | collective-permute-start | bytes 9224 | tf_op jit(solution)/shard_map/ppermute | solution.py:75
  103.2 11.1 %collective-permute-start.10 = (f32[2,3,128]{2,0,1:T(2,128)S(1)}, f32[2,3,128]{2,0,1:T(2,128)S(1)}, u32[]{:S(2)}, u32[]{:S(2)}) collective-permute-start(f32[2,3,128]{2,0,1:T(2,128)S(1)} %get-tuple-element.53), channel_id=1, source_target_pairs={{0,191},{1,96},{2,97},{3,98},{4,99},{5,100},{6,101},{7,102},{8,103... | collective-permute-start | bytes 9224 | tf_op jit(solution)/shard_map/ppermute | solution.py:75
  111.8 2.6 %collective-permute-start.9 = (f32[2,3,128]{2,0,1:T(2,128)S(1)}, f32[2,3,128]{2,0,1:T(2,128)S(1)}, u32[]{:S(2)}, u32[]{:S(2)}) collective-permute-start(f32[2,3,128]{2,0,1:T(2,128)S(1)} %get-tuple-element.54), channel_id=1, source_target_pairs={{0,96},{1,97},{2,98},{3,99},{4,100},{5,101},{6,102},{7,103},{8,104... | collective-permute-start | bytes 9224 | tf_op jit(solution)/shard_map/ppermute | solution.py:75
  111.8 8.2 %collective-permute-start.8 = (f32[2,3,128]{2,0,1:T(2,128)S(1)}, f32[2,3,128]{2,0,1:T(2,128)S(1)}, u32[]{:S(2)}, u32[]{:S(2)}) collective-permute-start(f32[2,3,128]{2,0,1:T(2,128)S(1)} %get-tuple-element.55), channel_id=1, source_target_pairs={{0,97},{1,98},{2,99},{3,100},{4,101},{5,102},{6,103},{7,104},{8,10... | collective-permute-start | bytes 9224 | tf_op jit(solution)/shard_map/ppermute | solution.py:75

commit v2 on v1

--- a/solution.py
+++ b/solution.py
@@ -64,15 +64,29 @@
     return jnp.dot(readout, hidden, precision=HIGHEST)
 
 
-def neighbour_shift(x, offset):
+def halo(grid):
     count_x = lax.axis_size("gx")
     count_y = lax.axis_size("gy")
-    pairs = []
-    for a in range(count_x):
-        for b in range(count_y):
-            target = ((a + offset[0]) % count_x) * count_y + (b + offset[1]) % count_y
-            pairs.append((a * count_y + b, target))
-    return lax.ppermute(x, ("gx", "gy"), pairs)
+    up_x = [(i, (i + 1) % count_x) for i in range(count_x)]
+    down_x = [((i + 1) % count_x, i) for i in range(count_x)]
+    up_y = [(i, (i + 1) % count_y) for i in range(count_y)]
+    down_y = [((i + 1) % count_y, i) for i in range(count_y)]
+    from_left_x = lax.ppermute(grid[2], "gx", up_x)
+    from_right_x = lax.ppermute(grid[0], "gx", down_x)
+    rows = jnp.stack([from_left_x, grid[1], from_right_x], axis=0)
+    from_left_y = lax.ppermute(rows[:, 2], "gy", up_y)
+    from_right_y = lax.ppermute(rows[:, 0], "gy", down_y)
+    return jnp.stack([from_left_y, rows[:, 1], from_right_y], axis=1)
+
+
+def place(parts):
+    empty = jnp.zeros_like(parts[0:1])
+    full = jnp.concatenate([parts[:4], empty, parts[4:]], axis=0)
+    return full.reshape((3, 3) + parts.shape[1:])
+
+
+def collect(grid):
+    return jnp.stack([grid[1 + pair[0], 1 + pair[1]] for pair in OFFSETS], axis=0)
 
 
 def local(
@@ -88,9 +102,7 @@
     chosen = send_lists.reshape(8, sends)
     pick = (chosen[:, :, None] == jnp.arange(blocks)).astype(jnp.float32)
     outgoing = jnp.einsum("dgb,bra->dgra", pick, payload, precision=HIGHEST)
-    incoming = jnp.stack(
-        [neighbour_shift(outgoing[7 - d], OFFSETS[7 - d]) for d in range(8)], axis=0
-    ).reshape(8 * sends, 4, atoms)
+    incoming = collect(halo(place(outgoing))).reshape(8 * sends, 4, atoms)
     ghost_pos = incoming[:, :3]
     ghost_kind = incoming[:, 3]
 
@@ -128,10 +140,7 @@
 
     energy, pullback = jax.vjp(energies_of, own_pos, ghost_pos)
     grad_own, grad_ghost = pullback(jnp.ones_like(energy))
-    grad_ghost = grad_ghost.reshape(8, sends, 3, atoms)
-    returned = jnp.stack(
-        [neighbour_shift(grad_ghost[7 - e], OFFSETS[7 - e]) for e in range(8)], axis=0
-    )
+    returned = collect(halo(place(grad_ghost.reshape(8, sends, 3, atoms))))
     back = jnp.einsum("dgb,dgca->bca", pick, returned, precision=HIGHEST)
     forces = -(grad_own + back)
     return (energy.reshape(blocks * atoms), forces.transpose(1, 0, 2).reshape(3, blocks * atoms))

time: 122 us -> 79.6 us (0.65)
  starting transfers between devices: 73.6 us -> 33.6 us
  waiting for transfers between devices: 9.06 us -> 7.18 us
    ppermute x16 -> x8, starting transfers between devices: 73.6 us -> 33.6 us  [the longest x2 16.5 us: halo(): from_right_y = lax.ppermute(rows[:, 0], 'gy', down_y)]
    ppermute x16 -> x8, waiting for transfers between devices: 9.06 us -> 7.18 us  [the longest x2 5.81 us: halo(): from_left_y = lax.ppermute(rows[:, 2], 'gy', up_y)]
  transfers between devices with their start and end apart: 16 -> 8, of which waited for: 4 -> 3; matrix products, arithmetic and copies ran while one was open for 4% -> 6% of each run, Pallas kernels for 0% -> 0%
where the time goes in v2:
time: 79.6 us; the launch traced here: 78.4 us
  starting transfers between devices  33.6 us (42%)
  matrix products  14.3 us (18%)
  other arithmetic  10.3 us (13%)
  between operations  9.38 us (12%)
  waiting for transfers between devices  7.18 us (9%)
  local copies, waits for them, and re-layouts  3.67 us (5%)
    ppermute x2, starting transfers between devices, halo(): from_right_y = lax.ppermute(rows[:, 0], 'gy', down_y)  16.5 us
    ppermute x2, starting transfers between devices, halo(): from_right_x = lax.ppermute(grid[0], 'gx', down_x)  10.7 us
    dot_general x2, matrix products, atom_energy(): message = jnp.einsum('kc,kmci->mci', radial, proj, precision=HIGHEST)  6.1 us
    ppermute x2, waiting for transfers between devices, halo(): from_left_y = lax.ppermute(rows[:, 2], 'gy', up_y)  5.81 us
    dot_general x8, matrix products, tile_terms(): jnp.einsum('qij,cj->qci', tiles.astype(jnp.bfloat16), other_feat, preferr...  4.2 us
    ppermute x2, starting transfers between devices, halo(): from_left_y = lax.ppermute(rows[:, 2], 'gy', up_y)  3.84 us
    ppermute x2, starting transfers between devices, halo(): from_left_x = lax.ppermute(grid[2], 'gx', up_x)  2.61 us
    reduce_sum x2, other arithmetic, tile_terms(): basis[:, None] * angular[None] * weight[None, None]  1.88 us
  transfers between devices with their start and end apart: 8, of which 3 were waited for; matrix products, arithmetic and copies ran while one was open for 6% of the time, Pallas kernels for 0%

profile of v2, /device:TPU:1, one launch (start us, length us, event | category | flops | bytes accessed | tf_op | source)
XLA Modules:
  0.0 78.4 jit_solution(3774948376620199622)
XLA Ops:
  0.7 0.7 convert_bitcast_fusion
  1.4 0.7 reshape.493
  2.1 0.9 %fusion.257 = f32[8,2,4,128]{3,0,2,1:T(8,128)S(1)} fusion(f32[2,1,128]{2,0,1:T(2,128)S(1)} %convert_bitcast_fusion, f32[2,3,128]{2,0,1:T(2,128)S(1)} %bitcast.837, s32[8,2]{0,1:T(2,128)} %bitcast.859), kind=kOutput, calls=%fused_computation.518 | convolution fusion | flops 197664 | bytes 36928 | tf_op jit(solution)/shard_map/dgb,bra->dgra/dot_general | solution.py:104
  3.0 2.6 %collective-permute-start = (f32[3,2,4,128]{3,2,1,0:T(4,128)S(1)}, f32[3,2,4,128]{3,2,1,0:T(4,128)S(1)}, u32[]{:S(2)}, u32[]{:S(2)}) collective-permute-start(f32[3,2,4,128]{3,2,1,0:T(4,128)S(1)} %copy.40), channel_id=1, source_target_pairs={{0,96},{96,192},{192,288},{288,384},{384,480},{480,576},{576,672},... | collective-permute-start | bytes 36872 | tf_op jit(solution)/shard_map/ppermute | solution.py:74
  5.6 7.9 %collective-permute-start.1 = (f32[3,2,4,128]{3,0,2,1:T(4,128)S(1)}, f32[3,2,4,128]{3,0,2,1:T(4,128)S(1)}, u32[]{:S(2)}, u32[]{:S(2)}) collective-permute-start(f32[3,2,4,128]{3,0,2,1:T(4,128)S(1)} %get-tuple-element.59), channel_id=1, source_target_pairs={{96,0},{192,96},{288,192},{384,288},{480,384},{576,480},{672,576},... | collective-permute-start | bytes 36872 | tf_op jit(solution)/shard_map/ppermute | solution.py:75
  13.8 1.5 %fusion.300 = (s32[1,1]{1,0:T(1,128)}, s32[1,1]{1,0:T(1,128)}, s32[1,1]{1,0:T(1,128)}, s32[1,1]{1,0:T(1,128)}) fusion(s32[2,2]{1,0:T(2,128)} %param.11), kind=kLoop, calls=%fused_computation.566 | loop fusion | bytes 32 | tf_op jit(solution)/shard_map/jvp()/slice | solution.py:54
  15.3 0.9 %fusion.21 = bf16[8,2,8,128]{3,2,1,0:T(8,128)(2,1)S(1)} fusion(f32[4,64]{1,0:T(4,128)} %param.14, s32[256]{0:T(256)} %param.10), kind=kOutput, calls=%fused_computation.41 | convolution fusion | flops 803840 | bytes 34816 | tf_op jit(solution)/shard_map/dot_general | solution.py:111
  16.2 1.0 %multiply_bitcast_fusion.2 = (f32[128,128]{1,0:T(8,128)S(1)}, f32[128,128]{1,0:T(8,128)S(1)}, f32[128,128]{1,0:T(8,128)S(1)}, f32[128,128]{1,0:T(8,128)S(1)}) fusion(s32[2,2,128,128]{3,2,1,0:T(8,128)} %param.12), kind=kLoop, calls=%fused_computation.433 | loop fusion | flops 131072 | bytes 524288 | tf_op jit(solution)/shard_map/jvp()/mul | solution.py:41
  17.3 1.9 %collective-permute-start.2 = (f32[3,2,4,128]{3,2,1,0:T(4,128)S(1)}, f32[3,2,4,128]{3,2,1,0:T(4,128)S(1)}, u32[]{:S(2)}, u32[]{:S(2)}) collective-permute-start(f32[3,2,4,128]{3,2,1,0:T(4,128)S(1)} %get-tuple-element.57), channel_id=1, source_target_pairs={{0,1},{1,2},{2,3},{3,4},{4,5},{5,6},{6,7},{7,8},{8,9},{9,10},{10,1... | collective-permute-start | bytes 36872 | tf_op jit(solution)/shard_map/ppermute | solution.py:77
  27.0 9.3 %collective-permute-start.3 = (f32[3,2,4,128]{3,2,1,0:T(4,128)S(1)}, f32[3,2,4,128]{3,2,1,0:T(4,128)S(1)}, u32[]{:S(2)}, u32[]{:S(2)}) collective-permute-start(f32[3,2,4,128]{3,2,1,0:T(4,128)S(1)} %get-tuple-element.56), channel_id=1, source_target_pairs={{1,0},{2,1},{3,2},{4,3},{5,4},{6,5},{7,6},{8,7},{9,8},{10,9},{11,1... | collective-permute-start | bytes 36872 | tf_op jit(solution)/shard_map/ppermute | solution.py:78
  36.3 0.8 collective-permute-done.3
  39.7 0.5 fusion.244
  40.8 3.0 %fusion.18 = f32[64,1,9,128]{3,1,2,0:T(1,128)S(1)} fusion(f32[4,64,1,1]{0,2,3,1:T(1,128)S(1)} %copy.33, f32[4,9,64,128]{3,2,1,0:T(8,128)S(1)} %bitcast.814), kind=kOutput, calls=%fused_computation.33 | convolution fusion | flops 3538944 | bytes 1475584 | tf_op jit(solution)/shard_map/jvp(kc,kmci->mci)/dot_general | solution.py:59
  47.1 3.1 %fusion.16 = f32[64,1,9,128]{3,1,2,0:T(1,128)S(1)} fusion(f32[4,64,1,1]{0,2,3,1:T(1,128)S(1)} %copy.33, f32[4,9,64,128]{3,2,1,0:T(8,128)S(1)} %bitcast.813), kind=kOutput, calls=%fused_computation.31 | convolution fusion | flops 3538944 | bytes 1475584 | tf_op jit(solution)/shard_map/jvp(kc,kmci->mci)/dot_general | solution.py:59
  51.2 0.5 broadcast_multiply_fusion.1
  53.9 0.9 %fusion.2 = (f32[9,128,128]{2,1,0:T(8,128)S(1)}, f32[4,128,128]{2,1,0:T(8,128)S(1)}, f32[4,128,128]{2,1,0:T(8,128)S(1)}, f32[9,128,128]{2,1,0:T(8,128)S(1)}) fusion(bf16[4,9,128,128]{3,2,1,0:T(8,128)(2,1)S(1)} %bitcast.811, f32[128,128]{1,0:T(8,128)S(1)} %get-tuple-element.39, f32[4,128,128]{2,1,0:T(8,128)S(1)} %get-tuple-element.83, ...), kind=kLoop, calls=%fused_computation.3 | loop fusion | flops 6651904 | bytes 5898240 | tf_op jit(solution)/shard_map/transpose(jvp())/reduce_sum | solution.py:41
  55.2 0.9 %fusion.10 = (f32[9,128,128]{2,1,0:T(8,128)S(1)}, f32[4,128,128]{2,1,0:T(8,128)S(1)}, f32[4,128,128]{2,1,0:T(8,128)S(1)}, f32[9,128,128]{2,1,0:T(8,128)S(1)}) fusion(bf16[4,9,128,128]{3,2,1,0:T(8,128)(2,1)S(1)} %bitcast.809, f32[128,128]{1,0:T(8,128)S(1)} %get-tuple-element.41, f32[4,128,128]{2,1,0:T(8,128)S(1)} %get-tuple-element.85, ...), kind=kLoop, calls=%fused_computation.13 | loop fusion | flops 6651904 | bytes 5898240 | tf_op jit(solution)/shard_map/transpose(jvp())/reduce_sum | solution.py:41
  58.6 2.7 %collective-permute-start.5 = (f32[3,2,3,128]{3,1,2,0:T(2,128)S(1)}, f32[3,2,3,128]{3,1,2,0:T(2,128)S(1)}, u32[]{:S(2)}, u32[]{:S(2)}) collective-permute-start(f32[3,2,3,128]{3,1,2,0:T(2,128)S(1)} %copy.28), channel_id=1, source_target_pairs={{96,0},{192,96},{288,192},{384,288},{480,384},{576,480},{672,576},... | collective-permute-start | bytes 27656 | tf_op jit(solution)/shard_map/ppermute | solution.py:75
  61.3 0.6 maximum_bitcast_fusion.4
  61.9 0.6 collective-permute-done.5
  62.5 7.2 %collective-permute-start.7 = (f32[3,2,3,128]{3,0,1,2:T(4,128)S(1)}, f32[3,2,3,128]{3,0,1,2:T(4,128)S(1)}, u32[]{:S(2)}, u32[]{:S(2)}) collective-permute-start(f32[3,2,3,128]{3,0,1,2:T(4,128)S(1)} %get-tuple-element.62), channel_id=1, source_target_pairs={{1,0},{2,1},{3,2},{4,3},{5,4},{6,5},{7,6},{8,7},{9,8},{10,9},{11,1... | collective-permute-start | bytes 27656 | tf_op jit(solution)/shard_map/ppermute | solution.py:78
  69.8 1.9 %collective-permute-start.6 = (f32[3,2,3,128]{3,0,1,2:T(4,128)S(1)}, f32[3,2,3,128]{3,0,1,2:T(4,128)S(1)}, u32[]{:S(2)}, u32[]{:S(2)}) collective-permute-start(f32[3,2,3,128]{3,0,1,2:T(4,128)S(1)} %get-tuple-element.63), channel_id=1, source_target_pairs={{0,1},{1,2},{2,3},{3,4},{4,5},{5,6},{6,7},{7,8},{8,9},{9,10},{10,1... | collective-permute-start | bytes 27656 | tf_op jit(solution)/shard_map/ppermute | solution.py:77
  71.8 5.8 %collective-permute-done.6 = f32[3,2,3,128]{3,0,1,2:T(4,128)S(1)} collective-permute-done((f32[3,2,3,128]{3,0,1,2:T(4,128)S(1)}, f32[3,2,3,128]{3,0,1,2:T(4,128)S(1)}, u32[]{:S(2)}, u32[]{:S(2)}) %collective-permute-start.6) | collective-permute-done | bytes 9248 | tf_op jit(solution)/shard_map/ppermute | solution.py:77
  77.8 0.6 copy.65
  (165 shorter events, 12.4 us)
Async XLA Ops:
  0.6 43.3 %copy-start = (f32[192,64]{0,1:T(8,128)S(1)}, f32[192,64]{0,1:T(8,128)}, u32[]{:S(2)}) copy-start(f32[192,64]{0,1:T(8,128)} %param.16) | copy-start | bytes 147460
  0.6 36.5 %copy-start.3 = (f32[4,64]{1,0:T(4,128)S(1)}, f32[4,64]{1,0:T(4,128)}, u32[]{:S(2)}) copy-start(f32[4,64]{1,0:T(4,128)} %param.14) | copy-start | bytes 3076
  0.7 23.7 %copy-start.1 = (f32[4,64]{1,0:T(4,128)S(1)}, f32[4,64]{1,0:T(4,128)}, u32[]{:S(2)}) copy-start(f32[4,64]{1,0:T(4,128)} %param.15) | copy-start | bytes 3076
  3.0 14.3 %collective-permute-start = (f32[3,2,4,128]{3,2,1,0:T(4,128)S(1)}, f32[3,2,4,128]{3,2,1,0:T(4,128)S(1)}, u32[]{:S(2)}, u32[]{:S(2)}) collective-permute-start(f32[3,2,4,128]{3,2,1,0:T(4,128)S(1)} %copy.40), channel_id=1, source_target_pairs={{0,96},{96,192},{192,288},{288,384},{384,480},{480,576},{576,672},... | collective-permute-start | bytes 36872 | tf_op jit(solution)/shard_map/ppermute | solution.py:74
  5.6 11.7 %collective-permute-start.1 = (f32[3,2,4,128]{3,0,2,1:T(4,128)S(1)}, f32[3,2,4,128]{3,0,2,1:T(4,128)S(1)}, u32[]{:S(2)}, u32[]{:S(2)}) collective-permute-start(f32[3,2,4,128]{3,0,2,1:T(4,128)S(1)} %get-tuple-element.59), channel_id=1, source_target_pairs={{96,0},{192,96},{288,192},{384,288},{480,384},{576,480},{672,576},... | collective-permute-start | bytes 36872 | tf_op jit(solution)/shard_map/ppermute | solution.py:75
  17.3 19.0 %collective-permute-start.2 = (f32[3,2,4,128]{3,2,1,0:T(4,128)S(1)}, f32[3,2,4,128]{3,2,1,0:T(4,128)S(1)}, u32[]{:S(2)}, u32[]{:S(2)}) collective-permute-start(f32[3,2,4,128]{3,2,1,0:T(4,128)S(1)} %get-tuple-element.57), channel_id=1, source_target_pairs={{0,1},{1,2},{2,3},{3,4},{4,5},{5,6},{6,7},{7,8},{8,9},{9,10},{10,1... | collective-permute-start | bytes 36872 | tf_op jit(solution)/shard_map/ppermute | solution.py:77
  27.0 10.1 %collective-permute-start.3 = (f32[3,2,4,128]{3,2,1,0:T(4,128)S(1)}, f32[3,2,4,128]{3,2,1,0:T(4,128)S(1)}, u32[]{:S(2)}, u32[]{:S(2)}) collective-permute-start(f32[3,2,4,128]{3,2,1,0:T(4,128)S(1)} %get-tuple-element.56), channel_id=1, source_target_pairs={{1,0},{2,1},{3,2},{4,3},{5,4},{6,5},{7,6},{8,7},{9,8},{10,9},{11,1... | collective-permute-start | bytes 36872 | tf_op jit(solution)/shard_map/ppermute | solution.py:78
  40.8 3.4 %copy-start.4 = (f32[64]{0:T(128)S(1)}, f32[64]{0:T(128)}, u32[]{:S(2)}) copy-start(f32[64]{0:T(128)} %param.17) | copy-start | bytes 772
  57.4 20.2 %copy-start.2 = (s32[1,1,8,2]{2,3,1,0:T(2,128)S(1)}, s32[1,1,8,2]{2,3,1,0:T(2,128)}, u32[]{:S(2)}) copy-start(s32[1,1,8,2]{2,3,1,0:T(2,128)} %param.13) | copy-start | bytes 196
  58.6 4.0 %collective-permute-start.5 = (f32[3,2,3,128]{3,1,2,0:T(2,128)S(1)}, f32[3,2,3,128]{3,1,2,0:T(2,128)S(1)}, u32[]{:S(2)}, u32[]{:S(2)}) collective-permute-start(f32[3,2,3,128]{3,1,2,0:T(2,128)S(1)} %copy.28), channel_id=1, source_target_pairs={{96,0},{192,96},{288,192},{384,288},{480,384},{576,480},{672,576},... | collective-permute-start | bytes 27656 | tf_op jit(solution)/shard_map/ppermute | solution.py:75
  61.3 1.2 %collective-permute-start.4 = (f32[3,2,3,128]{3,1,2,0:T(2,128)S(1)}, f32[3,2,3,128]{3,1,2,0:T(2,128)S(1)}, u32[]{:S(2)}, u32[]{:S(2)}) collective-permute-start(f32[3,2,3,128]{3,1,2,0:T(2,128)S(1)} %copy.25), channel_id=1, source_target_pairs={{0,96},{96,192},{192,288},{288,384},{384,480},{480,576},{576,672},... | collective-permute-start | bytes 27656 | tf_op jit(solution)/shard_map/ppermute | solution.py:74
  62.5 9.2 %collective-permute-start.7 = (f32[3,2,3,128]{3,0,1,2:T(4,128)S(1)}, f32[3,2,3,128]{3,0,1,2:T(4,128)S(1)}, u32[]{:S(2)}, u32[]{:S(2)}) collective-permute-start(f32[3,2,3,128]{3,0,1,2:T(4,128)S(1)} %get-tuple-element.62), channel_id=1, source_target_pairs={{1,0},{2,1},{3,2},{4,3},{5,4},{6,5},{7,6},{8,7},{9,8},{10,9},{11,1... | collective-permute-start | bytes 27656 | tf_op jit(solution)/shard_map/ppermute | solution.py:78
  69.8 7.8 %collective-permute-start.6 = (f32[3,2,3,128]{3,0,1,2:T(4,128)S(1)}, f32[3,2,3,128]{3,0,1,2:T(4,128)S(1)}, u32[]{:S(2)}, u32[]{:S(2)}) collective-permute-start(f32[3,2,3,128]{3,0,1,2:T(4,128)S(1)} %get-tuple-element.63), channel_id=1, source_target_pairs={{0,1},{1,2},{2,3},{3,4},{4,5},{5,6},{6,7},{7,8},{8,9},{9,10},{10,1... | collective-permute-start | bytes 27656 | tf_op jit(solution)/shard_map/ppermute | solution.py:77

commit v3 on v2

--- a/solution.py
+++ b/solution.py
@@ -44,24 +44,30 @@
     )
 
 
-def atom_energy(own_pos, table_pos, table_feat, listed_slots, masks, radial, readin, readout):
+def atom_energy(own_pos, others_pos, others_feat, masks, radial, readin, readout):
     count = radial.shape[0]
-    width = table_feat.shape[1]
+    width = others_feat.shape[1]
     atoms = own_pos.shape[1]
-    listed = listed_slots.shape[0]
+    listed = others_pos.shape[0]
     total = jnp.zeros((count * 9, width, atoms), jnp.float32)
     for slot in range(listed):
-        index = listed_slots[slot]
-        other_pos = lax.dynamic_index_in_dim(table_pos, index, 0, keepdims=False)
-        other_feat = lax.dynamic_index_in_dim(table_feat, index, 0, keepdims=False)
-        total = total + tile_terms(own_pos, other_pos, other_feat, masks[slot], listed, count)
+        total = total + tile_terms(
+            own_pos, others_pos[slot], others_feat[slot], masks[slot], listed, count
+        )
     proj = total.reshape(count, 9, width, atoms)
-    message = jnp.einsum("kc,kmci->mci", radial, proj, precision=HIGHEST)
+    message = jnp.sum(radial[:, None, :, None] * proj, axis=0)
     first = jnp.sum(message[1:4] * message[1:4], axis=0)
     second = jnp.sum(message[4:9] * message[4:9], axis=0)
     invariants = jnp.concatenate([message[0], first, second], axis=0)
     hidden = jax.nn.silu(jnp.dot(readin.T, invariants, precision=HIGHEST))
     return jnp.dot(readout, hidden, precision=HIGHEST)
+
+
+def select_slots(table, chosen):
+    slots = table.shape[0]
+    hit = chosen[..., None] == jnp.arange(slots, dtype=chosen.dtype)
+    hit = hit.reshape(hit.shape + (1,) * (table.ndim - 1))
+    return jnp.sum(jnp.where(hit, table, jnp.zeros((), table.dtype)), axis=2)
 
 
 def halo(grid):
@@ -110,25 +116,22 @@
         onehot = (kind[None, :] == jnp.arange(kinds).astype(kind.dtype)[:, None]).astype(jnp.float32)
         return jnp.dot(embedding.T, onehot, precision=HIGHEST)
 
-    own_feats = features(species)
-    own_feat = own_feats.reshape(-1, blocks, atoms).transpose(1, 0, 2).astype(jnp.bfloat16)
-    ghost_feat = (
-        features(ghost_kind.reshape(-1))
-        .reshape(-1, 8 * sends, atoms)
-        .transpose(1, 0, 2)
-        .astype(jnp.bfloat16)
+    own_feats32 = features(species).reshape(-1, blocks, atoms).transpose(1, 0, 2)
+    ghost_feats32 = (
+        features(ghost_kind.reshape(-1)).reshape(-1, 8 * sends, atoms).transpose(1, 0, 2)
     )
 
     def energies_of(own_now, ghost_now):
         table_pos = jnp.concatenate([own_now, ghost_now], axis=0)
-        table_feat = jnp.concatenate([own_feat, ghost_feat], axis=0)
+        table_feat = jnp.concatenate([own_feats32, ghost_feats32], axis=0)
+        others_pos = select_slots(table_pos, neighbours)
+        others_feat = select_slots(table_feat, neighbours).astype(jnp.bfloat16)
         return jnp.stack(
             [
                 atom_energy(
                     own_now[block],
-                    table_pos,
-                    table_feat,
-                    neighbours[block],
+                    others_pos[block],
+                    others_feat[block],
                     pair_masks[block],
                     radial,
                     readin,

time: 79.6 us -> 61 us (0.77)
  between operations: 9.38 us -> 1.74 us
  matrix products: 14.3 us -> 8.15 us
  waiting for transfers between devices: 7.18 us -> 2.26 us
  other arithmetic: 10.3 us -> 11.8 us
  local copies, waits for them, and re-layouts: 3.67 us -> 2.34 us
    dot_general x2 -> x0, matrix products: 6.1 us -> none  [atom_energy(): message = jnp.einsum('kc,kmci->mci', radial, proj, precision=HIGHEST)]
    ppermute x2, waiting for transfers between devices: 5.81 us -> 0.01 us  [halo(): from_left_y = lax.ppermute(rows[:, 2], 'gy', up_y)]
    ppermute x2, starting transfers between devices: 10.7 us -> 13.9 us  [halo(): from_right_x = lax.ppermute(grid[0], 'gx', down_x)]
    ppermute x2, starting transfers between devices: 2.61 us -> 0.02 us  [halo(): from_left_x = lax.ppermute(grid[2], 'gx', up_x)]
    slice x1, local copies, waits for them, and re-layouts: 1.49 us -> 0.01 us  [atom_energy(): others_pos[slot]]
    reduce_sum x0 -> x4, other arithmetic: none -> 0.87 us  [the longest x3 0.54 us: select_slots(): return jnp.sum(jnp.where(hit, table, jnp.zeros((), table.dtype)), axis=2)]
where the time goes in v3:
time: 61 us; the launch traced here: 60.4 us
  starting transfers between devices  34.1 us (56%)
  other arithmetic  11.8 us (19%)
  matrix products  8.15 us (13%)
  local copies, waits for them, and re-layouts  2.34 us (4%)
  waiting for transfers between devices  2.26 us (4%)
  between operations  1.74 us (3%)
    ppermute x2, starting transfers between devices, halo(): from_right_y = lax.ppermute(rows[:, 0], 'gy', down_y)  16.4 us
    ppermute x2, starting transfers between devices, halo(): from_right_x = lax.ppermute(grid[0], 'gx', down_x)  13.9 us
    dot_general x8, matrix products, tile_terms(): jnp.einsum('qij,cj->qci', tiles.astype(jnp.bfloat16), other_feat, preferr...  4.2 us
    ppermute x2, starting transfers between devices, halo(): from_left_y = lax.ppermute(rows[:, 2], 'gy', up_y)  3.84 us
    reduce_sum x2, other arithmetic, tile_terms(): basis[:, None] * angular[None] * weight[None, None]  1.88 us
    ppermute x2, waiting for transfers between devices, halo(): from_right_y = lax.ppermute(rows[:, 0], 'gy', down_y)  1.56 us
    convert_element_type x4, other arithmetic, tile_terms(): tiles.astype(jnp.bfloat16)  1.39 us
    dot_general x2, matrix products, features(): return jnp.dot(embedding.T, onehot, precision=HIGHEST)  1.36 us
  transfers between devices with their start and end apart: 8, of which 3 were waited for; matrix products, arithmetic and copies ran while one was open for 6% of the time, Pallas kernels for 0%

profile of v3, /device:TPU:1, one launch (start us, length us, event | category | flops | bytes accessed | tf_op | source)
XLA Modules:
  0.0 60.4 jit_solution(2230030133215395896)
XLA Ops:
  0.7 0.7 %convert_bitcast_fusion = f32[2,1,128]{2,0,1:T(2,128)S(1)} fusion(s32[256]{0:T(256)} %param.10), kind=kLoop, calls=%fused_computation.514 | loop fusion | flops 256 | bytes 2048 | tf_op jit(solution)/shard_map/convert_element_type | solution.py:106
  1.4 0.7 %reshape.507 = f32[3,2,128]{2,1,0:T(2,128)S(1)} reshape(f32[3,256]{1,0:T(4,128)} %param.9) | data formatting | bytes 6144 | tf_op jit(solution)/shard_map/reshape | solution.py:105
  2.1 0.9 %fusion.241 = f32[8,2,4,128]{3,0,2,1:T(8,128)S(1)} fusion(f32[2,1,128]{2,0,1:T(2,128)S(1)} %convert_bitcast_fusion, f32[2,3,128]{2,0,1:T(2,128)S(1)} %bitcast.786, s32[8,2]{0,1:T(2,128)} %bitcast.814), kind=kOutput, calls=%fused_computation.492 | convolution fusion | flops 197664 | bytes 36928 | tf_op jit(solution)/shard_map/dgb,bra->dgra/dot_general | solution.py:110
  3.0 10.5 %collective-permute-start.1 = (f32[3,2,4,128]{3,0,2,1:T(4,128)S(1)}, f32[3,2,4,128]{3,0,2,1:T(4,128)S(1)}, u32[]{:S(2)}, u32[]{:S(2)}) collective-permute-start(f32[3,2,4,128]{3,0,2,1:T(4,128)S(1)} %get-tuple-element.57), channel_id=1, source_target_pairs={{96,0},{192,96},{288,192},{384,288},{480,384},{576,480},{672,576},... | collective-permute-start | bytes 36872 | tf_op jit(solution)/shard_map/ppermute | solution.py:81
  13.6 1.0 %multiply_bitcast_fusion = (f32[128,128]{1,0:T(8,128)S(1)}, f32[128,128]{1,0:T(8,128)S(1)}, f32[128,128]{1,0:T(8,128)S(1)}, f32[128,128]{1,0:T(8,128)S(1)}) fusion(s32[2,2,128,128]{3,2,1,0:T(8,128)} %param.12), kind=kLoop, calls=%fused_computation.418 | loop fusion | flops 131072 | bytes 524288 | tf_op jit(solution)/shard_map/jvp()/mul | solution.py:41
  14.5 0.7 %iota_compare_fusion = pred[2,2,18]{1,2,0:T(8,128)(4,1)S(1)} fusion(s32[2,2]{1,0:T(2,128)} %param.11), kind=kLoop, calls=%fused_computation.460 | loop fusion | flops 72 | bytes 88 | tf_op jit(solution)/shard_map/jvp()/eq | solution.py:68
  15.4 0.9 %convolution_bitcast_fusion.3 = f32[64,256]{1,0:T(8,128)S(1)} fusion(f32[4,64]{1,0:T(4,128)} %param.14, s32[256]{0:T(256)} %param.10), kind=kOutput, calls=%fused_computation.42 | convolution fusion | flops 787456 | bytes 67584 | tf_op jit(solution)/shard_map/dot_general | solution.py:117
  16.5 1.9 %collective-permute-start.2 = (f32[3,2,4,128]{3,2,1,0:T(4,128)S(1)}, f32[3,2,4,128]{3,2,1,0:T(4,128)S(1)}, u32[]{:S(2)}, u32[]{:S(2)}) collective-permute-start(f32[3,2,4,128]{3,2,1,0:T(4,128)S(1)} %get-tuple-element.55), channel_id=1, source_target_pairs={{0,1},{1,2},{2,3},{3,4},{4,5},{5,6},{6,7},{7,8},{8,9},{9,10},{10,1... | collective-permute-start | bytes 36872 | tf_op jit(solution)/shard_map/ppermute | solution.py:83
  18.6 9.3 %collective-permute-start.3 = (f32[3,2,4,128]{3,2,1,0:T(4,128)S(1)}, f32[3,2,4,128]{3,2,1,0:T(4,128)S(1)}, u32[]{:S(2)}, u32[]{:S(2)}) collective-permute-start(f32[3,2,4,128]{3,2,1,0:T(4,128)S(1)} %get-tuple-element.54), channel_id=1, source_target_pairs={{1,0},{2,1},{3,2},{4,3},{5,4},{6,5},{7,6},{8,7},{9,8},{10,9},{11,1... | collective-permute-start | bytes 36872 | tf_op jit(solution)/shard_map/ppermute | solution.py:84
  28.0 0.8 %collective-permute-done.3 = f32[3,2,4,128]{3,2,1,0:T(4,128)S(1)} collective-permute-done((f32[3,2,4,128]{3,2,1,0:T(4,128)S(1)}, f32[3,2,4,128]{3,2,1,0:T(4,128)S(1)}, u32[]{:S(2)}, u32[]{:S(2)}) %collective-permute-start.3) | collective-permute-done | bytes 12320 | tf_op jit(solution)/shard_map/ppermute | solution.py:84
  32.1 0.5 fusion.236
  33.0 0.5 fusion.237
  34.2 0.5 convolution_add_fusion.1
  35.1 0.5 convolution_add_fusion
  39.3 0.5 convolution_convert_fusion
  40.4 0.9 %fusion.2 = (f32[9,128,128]{2,1,0:T(8,128)S(1)}, f32[4,128,128]{2,1,0:T(8,128)S(1)}, f32[4,128,128]{2,1,0:T(8,128)S(1)}, f32[9,128,128]{2,1,0:T(8,128)S(1)}) fusion(bf16[4,9,128,128]{3,2,1,0:T(8,128)(2,1)S(1)} %bitcast.778, f32[128,128]{1,0:T(8,128)S(1)} %get-tuple-element.42, f32[4,128,128]{2,1,0:T(8,128)S(1)} %get-tuple-element.81, ...), kind=kLoop, calls=%fused_computation.3 | loop fusion | flops 6651904 | bytes 5898240 | tf_op jit(solution)/shard_map/transpose(jvp())/reduce_sum | solution.py:41
  41.5 0.9 %fusion.10 = (f32[9,128,128]{2,1,0:T(8,128)S(1)}, f32[4,128,128]{2,1,0:T(8,128)S(1)}, f32[4,128,128]{2,1,0:T(8,128)S(1)}, f32[9,128,128]{2,1,0:T(8,128)S(1)}) fusion(bf16[4,9,128,128]{3,2,1,0:T(8,128)(2,1)S(1)} %bitcast.776, f32[128,128]{1,0:T(8,128)S(1)} %get-tuple-element.43, f32[4,128,128]{2,1,0:T(8,128)S(1)} %get-tuple-element.83, ...), kind=kLoop, calls=%fused_computation.13 | loop fusion | flops 6651904 | bytes 5898240 | tf_op jit(solution)/shard_map/transpose(jvp())/reduce_sum | solution.py:41
  44.9 3.3 %collective-permute-start.5 = (f32[3,2,3,128]{3,1,2,0:T(2,128)S(1)}, f32[3,2,3,128]{3,1,2,0:T(2,128)S(1)}, u32[]{:S(2)}, u32[]{:S(2)}) collective-permute-start(f32[3,2,3,128]{3,1,2,0:T(2,128)S(1)} %copy.46), channel_id=1, source_target_pairs={{96,0},{192,96},{288,192},{384,288},{480,384},{576,480},{672,576},... | collective-permute-start | bytes 27656 | tf_op jit(solution)/shard_map/ppermute | solution.py:81
  48.3 0.6 maximum_bitcast_fusion.4
  49.0 0.7 %collective-permute-done.4 = f32[3,2,3,128]{3,1,2,0:T(2,128)S(1)} collective-permute-done((f32[3,2,3,128]{3,1,2,0:T(2,128)S(1)}, f32[3,2,3,128]{3,1,2,0:T(2,128)S(1)}, u32[]{:S(2)}, u32[]{:S(2)}) %collective-permute-start.4) | collective-permute-done | bytes 9248 | tf_op jit(solution)/shard_map/ppermute | solution.py:80
  49.7 1.9 %collective-permute-start.6 = (f32[3,2,3,128]{3,0,1,2:T(4,128)S(1)}, f32[3,2,3,128]{3,0,1,2:T(4,128)S(1)}, u32[]{:S(2)}, u32[]{:S(2)}) collective-permute-start(f32[3,2,3,128]{3,0,1,2:T(4,128)S(1)} %get-tuple-element.61), channel_id=1, source_target_pairs={{0,1},{1,2},{2,3},{3,4},{4,5},{5,6},{6,7},{7,8},{8,9},{9,10},{10,1... | collective-permute-start | bytes 27656 | tf_op jit(solution)/shard_map/ppermute | solution.py:83
  51.6 7.0 %collective-permute-start.7 = (f32[3,2,3,128]{3,0,1,2:T(4,128)S(1)}, f32[3,2,3,128]{3,0,1,2:T(4,128)S(1)}, u32[]{:S(2)}, u32[]{:S(2)}) collective-permute-start(f32[3,2,3,128]{3,0,1,2:T(4,128)S(1)} %get-tuple-element.60), channel_id=1, source_target_pairs={{1,0},{2,1},{3,2},{4,3},{5,4},{6,5},{7,6},{8,7},{9,8},{10,9},{11,1... | collective-permute-start | bytes 27656 | tf_op jit(solution)/shard_map/ppermute | solution.py:84
  58.7 0.8 %collective-permute-done.7 = f32[3,2,3,128]{3,0,1,2:T(4,128)S(1)} collective-permute-done((f32[3,2,3,128]{3,0,1,2:T(4,128)S(1)}, f32[3,2,3,128]{3,0,1,2:T(4,128)S(1)}, u32[]{:S(2)}, u32[]{:S(2)}) %collective-permute-start.7) | collective-permute-done | bytes 9248 | tf_op jit(solution)/shard_map/ppermute | solution.py:84
  59.8 0.6 copy.81
  (173 shorter events, 11.8 us)
Async XLA Ops:
  0.6 35.5 %copy-start = (f32[192,64]{0,1:T(8,128)S(1)}, f32[192,64]{0,1:T(8,128)}, u32[]{:S(2)}) copy-start(f32[192,64]{0,1:T(8,128)} %param.16) | copy-start | bytes 147460
  0.6 17.9 %copy-start.2 = (f32[4,64]{1,0:T(4,128)S(1)}, f32[4,64]{1,0:T(4,128)}, u32[]{:S(2)}) copy-start(f32[4,64]{1,0:T(4,128)} %param.15) | copy-start | bytes 3076
  3.0 13.4 %collective-permute-start.1 = (f32[3,2,4,128]{3,0,2,1:T(4,128)S(1)}, f32[3,2,4,128]{3,0,2,1:T(4,128)S(1)}, u32[]{:S(2)}, u32[]{:S(2)}) collective-permute-start(f32[3,2,4,128]{3,0,2,1:T(4,128)S(1)} %get-tuple-element.57), channel_id=1, source_target_pairs={{96,0},{192,96},{288,192},{384,288},{480,384},{576,480},{672,576},... | collective-permute-start | bytes 36872 | tf_op jit(solution)/shard_map/ppermute | solution.py:81
  13.5 2.9 %collective-permute-start = (f32[3,2,4,128]{3,2,1,0:T(4,128)S(1)}, f32[3,2,4,128]{3,2,1,0:T(4,128)S(1)}, u32[]{:S(2)}, u32[]{:S(2)}) collective-permute-start(f32[3,2,4,128]{3,2,1,0:T(4,128)S(1)} %copy.65), channel_id=1, source_target_pairs={{0,96},{96,192},{192,288},{288,384},{384,480},{480,576},{576,672},... | collective-permute-start | bytes 36872 | tf_op jit(solution)/shard_map/ppermute | solution.py:80
  16.5 11.5 %collective-permute-start.2 = (f32[3,2,4,128]{3,2,1,0:T(4,128)S(1)}, f32[3,2,4,128]{3,2,1,0:T(4,128)S(1)}, u32[]{:S(2)}, u32[]{:S(2)}) collective-permute-start(f32[3,2,4,128]{3,2,1,0:T(4,128)S(1)} %get-tuple-element.55), channel_id=1, source_target_pairs={{0,1},{1,2},{2,3},{3,4},{4,5},{5,6},{6,7},{7,8},{8,9},{9,10},{10,1... | collective-permute-start | bytes 36872 | tf_op jit(solution)/shard_map/ppermute | solution.py:83
  18.6 10.1 %collective-permute-start.3 = (f32[3,2,4,128]{3,2,1,0:T(4,128)S(1)}, f32[3,2,4,128]{3,2,1,0:T(4,128)S(1)}, u32[]{:S(2)}, u32[]{:S(2)}) collective-permute-start(f32[3,2,4,128]{3,2,1,0:T(4,128)S(1)} %get-tuple-element.54), channel_id=1, source_target_pairs={{1,0},{2,1},{3,2},{4,3},{5,4},{6,5},{7,6},{8,7},{9,8},{10,9},{11,1... | collective-permute-start | bytes 36872 | tf_op jit(solution)/shard_map/ppermute | solution.py:84
  29.2 0.7 %copy-start.1 = (f32[4,64]{1,0:T(4,128)S(1)}, f32[4,64]{1,0:T(4,128)}, u32[]{:S(2)}) copy-start(f32[4,64]{1,0:T(4,128)} %param.14) | copy-start | bytes 3076
  35.6 0.7 %copy-start.4 = (f32[64]{0:T(128)S(1)}, f32[64]{0:T(128)}, u32[]{:S(2)}) copy-start(f32[64]{0:T(128)} %param.17) | copy-start | bytes 772
  44.2 15.4 %copy-start.3 = (s32[1,1,8,2]{2,3,1,0:T(2,128)S(1)}, s32[1,1,8,2]{2,3,1,0:T(2,128)}, u32[]{:S(2)}) copy-start(s32[1,1,8,2]{2,3,1,0:T(2,128)} %param.13) | copy-start | bytes 196
  44.9 4.8 %collective-permute-start.5 = (f32[3,2,3,128]{3,1,2,0:T(2,128)S(1)}, f32[3,2,3,128]{3,1,2,0:T(2,128)S(1)}, u32[]{:S(2)}, u32[]{:S(2)}) collective-permute-start(f32[3,2,3,128]{3,1,2,0:T(2,128)S(1)} %copy.46), channel_id=1, source_target_pairs={{96,0},{192,96},{288,192},{384,288},{480,384},{576,480},{672,576},... | collective-permute-start | bytes 27656 | tf_op jit(solution)/shard_map/ppermute | solution.py:81
  48.3 1.4 %collective-permute-start.4 = (f32[3,2,3,128]{3,1,2,0:T(2,128)S(1)}, f32[3,2,3,128]{3,1,2,0:T(2,128)S(1)}, u32[]{:S(2)}, u32[]{:S(2)}) collective-permute-start(f32[3,2,3,128]{3,1,2,0:T(2,128)S(1)} %copy.40), channel_id=1, source_target_pairs={{0,96},{96,192},{192,288},{288,384},{384,480},{480,576},{576,672},... | collective-permute-start | bytes 27656 | tf_op jit(solution)/shard_map/ppermute | solution.py:80
  49.7 9.0 %collective-permute-start.6 = (f32[3,2,3,128]{3,0,1,2:T(4,128)S(1)}, f32[3,2,3,128]{3,0,1,2:T(4,128)S(1)}, u32[]{:S(2)}, u32[]{:S(2)}) collective-permute-start(f32[3,2,3,128]{3,0,1,2:T(4,128)S(1)} %get-tuple-element.61), channel_id=1, source_target_pairs={{0,1},{1,2},{2,3},{3,4},{4,5},{5,6},{6,7},{7,8},{8,9},{9,10},{10,1... | collective-permute-start | bytes 27656 | tf_op jit(solution)/shard_map/ppermute | solution.py:83
  51.6 7.9 %collective-permute-start.7 = (f32[3,2,3,128]{3,0,1,2:T(4,128)S(1)}, f32[3,2,3,128]{3,0,1,2:T(4,128)S(1)}, u32[]{:S(2)}, u32[]{:S(2)}) collective-permute-start(f32[3,2,3,128]{3,0,1,2:T(4,128)S(1)} %get-tuple-element.60), channel_id=1, source_target_pairs={{1,0},{2,1},{3,2},{4,3},{5,4},{6,5},{7,6},{8,7},{9,8},{10,9},{11,1... | collective-permute-start | bytes 27656 | tf_op jit(solution)/shard_map/ppermute | solution.py:84

commit v4 on v3

--- a/solution.py
+++ b/solution.py
@@ -29,38 +29,28 @@
     )
 
 
-def tile_terms(own_pos, other_pos, other_feat, pair_mask, listed, count):
-    atoms = own_pos.shape[1]
+def block_energies(own_pos, others_pos, others_feat, masks, radial, readin, readout):
+    count = radial.shape[0]
+    atoms = own_pos.shape[2]
+    listed = others_pos.shape[1]
     centres = 0.5 + jnp.arange(count).astype(jnp.float32)
-    rel = other_pos[:, None, :] - own_pos[:, :, None]
-    dist = jnp.sqrt(jnp.sum(rel * rel, axis=0) + 0.25)
-    offset = dist[None] - centres[:, None, None]
+    rel = others_pos[:, :, :, None, :] - own_pos[:, None, :, :, None]
+    dist = jnp.sqrt(jnp.sum(rel * rel, axis=2) + 0.25)
+    offset = dist[:, :, None] - centres[:, None, None]
     basis = jnp.exp(-0.5 * offset * offset)
-    angular = harmonics(rel, dist)
-    weight = pair_mask.astype(jnp.float32) * (1.0 / math.sqrt(listed * atoms))
-    tiles = (basis[:, None] * angular[None] * weight[None, None]).reshape(count * 9, atoms, atoms)
-    return jnp.einsum(
-        "qij,cj->qci", tiles.astype(jnp.bfloat16), other_feat, preferred_element_type=jnp.float32
-    )
-
-
-def atom_energy(own_pos, others_pos, others_feat, masks, radial, readin, readout):
-    count = radial.shape[0]
-    width = others_feat.shape[1]
-    atoms = own_pos.shape[1]
-    listed = others_pos.shape[0]
-    total = jnp.zeros((count * 9, width, atoms), jnp.float32)
-    for slot in range(listed):
-        total = total + tile_terms(
-            own_pos, others_pos[slot], others_feat[slot], masks[slot], listed, count
-        )
-    proj = total.reshape(count, 9, width, atoms)
-    message = jnp.sum(radial[:, None, :, None] * proj, axis=0)
-    first = jnp.sum(message[1:4] * message[1:4], axis=0)
-    second = jnp.sum(message[4:9] * message[4:9], axis=0)
-    invariants = jnp.concatenate([message[0], first, second], axis=0)
-    hidden = jax.nn.silu(jnp.dot(readin.T, invariants, precision=HIGHEST))
-    return jnp.dot(readout, hidden, precision=HIGHEST)
+    angular = harmonics(jnp.moveaxis(rel, 2, 0), dist)
+    angular = jnp.moveaxis(angular, 0, 2)
+    weight = masks.astype(jnp.float32) * (1.0 / math.sqrt(listed * atoms))
+    tiles = basis[:, :, :, None] * angular[:, :, None] * weight[:, :, None, None]
+    tiles = tiles.reshape(tiles.shape[:2] + (count * 9, atoms, atoms)).astype(jnp.bfloat16)
+    proj = jnp.einsum("bnqij,bncj->bqci", tiles, others_feat, preferred_element_type=jnp.float32)
+    proj = proj.reshape((proj.shape[0], count, 9) + proj.shape[2:])
+    message = jnp.sum(radial[None, :, None, :, None] * proj, axis=1)
+    first = jnp.sum(message[:, 1:4] * message[:, 1:4], axis=1)
+    second = jnp.sum(message[:, 4:9] * message[:, 4:9], axis=1)
+    invariants = jnp.concatenate([message[:, 0], first, second], axis=1)
+    hidden = jax.nn.silu(jnp.einsum("fh,bfi->bhi", readin, invariants, precision=HIGHEST))
+    return jnp.einsum("h,bhi->bi", readout, hidden, precision=HIGHEST)
 
 
 def select_slots(table, chosen):
@@ -126,19 +116,8 @@
         table_feat = jnp.concatenate([own_feats32, ghost_feats32], axis=0)
         others_pos = select_slots(table_pos, neighbours)
         others_feat = select_slots(table_feat, neighbours).astype(jnp.bfloat16)
-        return jnp.stack(
-            [
-                atom_energy(
-                    own_now[block],
-                    others_pos[block],
-                    others_feat[block],
-                    pair_masks[block],
-                    radial,
-                    readin,
-                    readout,
-                )
-                for block in range(blocks)
-            ]
+        return block_energies(
+            own_now, others_pos, others_feat, pair_masks, radial, readin, readout
         )
 
     energy, pullback = jax.vjp(energies_of, own_pos, ghost_pos)

time: 61 us -> 72.8 us (1.19)
  waiting for transfers between devices: 2.26 us -> 7.8 us
  matrix products: 8.15 us -> 11.3 us
  other arithmetic: 11.8 us -> 14.2 us
  local copies, waits for them, and re-layouts: 2.34 us -> 3.54 us
    ppermute x2, waiting for transfers between devices: 0.01 us -> 5.81 us  [halo(): from_left_y = lax.ppermute(rows[:, 2], 'gy', up_y)]
    reduce_sum x12 -> x7, other arithmetic: 3.54 us -> 7.26 us  [the longest x1 5.87 us: block_energies(): basis[:, :, :, None] * angular[:, :, None] * weight[:, :, None, None]]
    ppermute x2, starting transfers between devices: 13.9 us -> 10.4 us  [halo(): from_right_x = lax.ppermute(grid[0], 'gx', down_x)]
    dot_general x14 -> x5, matrix products: 5.71 us -> 8.86 us  [the longest x2 7.5 us: block_energies(): jnp.einsum('bnqij,bncj->bqci', tiles, others_feat, preferred_element_type...]
    ppermute x2, starting transfers between devices: 0.02 us -> 2.61 us  [halo(): from_left_x = lax.ppermute(grid[2], 'gx', up_x)]
    convert_element_type x4 -> x0, other arithmetic: 1.39 us -> none  [tile_terms(): tiles.astype(jnp.bfloat16)]
    ppermute x2, waiting for transfers between devices: 0.01 us -> 1.16 us  [halo(): from_right_x = lax.ppermute(grid[0], 'gx', down_x)]
    mul x10 -> x5, other arithmetic: 2.01 us -> 2.87 us  [the longest x1 1.32 us: block_energies(): basis[:, :, :, None] * angular[:, :, None] * weight[:, :, None, None]]
  transfers between devices with their start and end apart: 8 -> 8, of which waited for: 3 -> 4; matrix products, arithmetic and copies ran while one was open for 6% -> 5% of each run, Pallas kernels for 0% -> 0%
where the time goes in v4:
time: 72.8 us; the launch traced here: 71.7 us
  starting transfers between devices  33.6 us (46%)
  other arithmetic  14.2 us (20%)
  matrix products  11.3 us (16%)
  waiting for transfers between devices  7.8 us (11%)
  local copies, waits for them, and re-layouts  3.54 us (5%)
  between operations  1.27 us (2%)
    ppermute x2, starting transfers between devices, halo(): from_right_y = lax.ppermute(rows[:, 0], 'gy', down_y)  16.7 us
    ppermute x2, starting transfers between devices, halo(): from_right_x = lax.ppermute(grid[0], 'gx', down_x)  10.4 us
    dot_general x2, matrix products, block_energies(): jnp.einsum('bnqij,bncj->bqci', tiles, others_feat, preferred_element_type...  7.5 us
    reduce_sum x1, other arithmetic, block_energies(): basis[:, :, :, None] * angular[:, :, None] * weight[:, :, None, None]  5.87 us
    ppermute x2, waiting for transfers between devices, halo(): from_left_y = lax.ppermute(rows[:, 2], 'gy', up_y)  5.81 us
    ppermute x2, starting transfers between devices, halo(): from_left_y = lax.ppermute(rows[:, 2], 'gy', up_y)  3.84 us
    ppermute x2, starting transfers between devices, halo(): from_left_x = lax.ppermute(grid[2], 'gx', up_x)  2.61 us
  transfers between devices with their start and end apart: 8, of which 4 were waited for; matrix products, arithmetic and copies ran while one was open for 5% of the time, Pallas kernels for 0%

profile of v4, /device:TPU:1, one launch (start us, length us, event | category | flops | bytes accessed | tf_op | source)
XLA Modules:
  0.0 71.7 jit_solution(13241253433270276745)
XLA Ops:
  0.7 0.7 %convert_bitcast_fusion = f32[2,1,128]{2,0,1:T(2,128)S(1)} fusion(s32[256]{0:T(256)} %param.10), kind=kLoop, calls=%fused_computation.203 | loop fusion | flops 256 | bytes 2048 | tf_op jit(solution)/shard_map/convert_element_type | solution.py:96
  1.4 0.7 reshape.174
  2.1 0.9 %fusion.96 = f32[8,2,4,128]{3,0,2,1:T(8,128)S(1)} fusion(f32[2,1,128]{2,0,1:T(2,128)S(1)} %convert_bitcast_fusion, f32[2,3,128]{2,0,1:T(2,128)S(1)} %bitcast.359, s32[8,2]{0,1:T(2,128)} %bitcast.380), kind=kOutput, calls=%fused_computation.192 | convolution fusion | flops 197664 | bytes 36928 | tf_op jit(solution)/shard_map/dgb,bra->dgra/dot_general | solution.py:100
  3.0 2.6 %collective-permute-start = (f32[3,2,4,128]{3,2,1,0:T(4,128)S(1)}, f32[3,2,4,128]{3,2,1,0:T(4,128)S(1)}, u32[]{:S(2)}, u32[]{:S(2)}) collective-permute-start(f32[3,2,4,128]{3,2,1,0:T(4,128)S(1)} %copy.129), channel_id=1, source_target_pairs={{0,96},{96,192},{192,288},{288,384},{384,480},{480,576},{576,672},... | collective-permute-start | bytes 36872 | tf_op jit(solution)/shard_map/ppermute | solution.py:70
  5.6 7.9 %collective-permute-start.1 = (f32[3,2,4,128]{3,0,2,1:T(4,128)S(1)}, f32[3,2,4,128]{3,0,2,1:T(4,128)S(1)}, u32[]{:S(2)}, u32[]{:S(2)}) collective-permute-start(f32[3,2,4,128]{3,0,2,1:T(4,128)S(1)} %get-tuple-element.18), channel_id=1, source_target_pairs={{96,0},{192,96},{288,192},{384,288},{480,384},{576,480},{672,576},... | collective-permute-start | bytes 36872 | tf_op jit(solution)/shard_map/ppermute | solution.py:71
  13.7 0.7 iota_compare_fusion
  14.4 0.9 %convolution_bitcast_fusion.2 = f32[64,256]{1,0:T(8,128)S(1)} fusion(f32[4,64]{1,0:T(4,128)} %param.14, s32[256]{0:T(256)} %param.10), kind=kOutput, calls=%fused_computation.21 | convolution fusion | flops 787456 | bytes 67584 | tf_op jit(solution)/shard_map/dot_general | solution.py:107
  15.4 1.0 %convert_multiply_fusion = f32[2,2,128,128]{3,2,1,0:T(8,128)S(1)} fusion(s32[2,2,128,128]{3,2,1,0:T(8,128)} %param.12), kind=kLoop, calls=%fused_computation.116 | loop fusion | flops 131072 | bytes 524288 | tf_op jit(solution)/shard_map/jvp()/mul | solution.py:43
  16.5 1.9 %collective-permute-start.2 = (f32[3,2,4,128]{3,2,1,0:T(4,128)S(1)}, f32[3,2,4,128]{3,2,1,0:T(4,128)S(1)}, u32[]{:S(2)}, u32[]{:S(2)}) collective-permute-start(f32[3,2,4,128]{3,2,1,0:T(4,128)S(1)} %get-tuple-element.16), channel_id=1, source_target_pairs={{0,1},{1,2},{2,3},{3,4},{4,5},{5,6},{6,7},{7,8},{8,9},{9,10},{10,1... | collective-permute-start | bytes 36872 | tf_op jit(solution)/shard_map/ppermute | solution.py:73
  18.5 0.7 mul.356
  19.3 9.5 %collective-permute-start.3 = (f32[3,2,4,128]{3,2,1,0:T(4,128)S(1)}, f32[3,2,4,128]{3,2,1,0:T(4,128)S(1)}, u32[]{:S(2)}, u32[]{:S(2)}) collective-permute-start(f32[3,2,4,128]{3,2,1,0:T(4,128)S(1)} %get-tuple-element.15), channel_id=1, source_target_pairs={{1,0},{2,1},{3,2},{4,3},{5,4},{6,5},{7,6},{8,7},{9,8},{10,9},{11,1... | collective-permute-start | bytes 36872 | tf_op jit(solution)/shard_map/ppermute | solution.py:74
  28.8 0.8 %collective-permute-done.3 = f32[3,2,4,128]{3,2,1,0:T(4,128)S(1)} collective-permute-done((f32[3,2,4,128]{3,2,1,0:T(4,128)S(1)}, f32[3,2,4,128]{3,2,1,0:T(4,128)S(1)}, u32[]{:S(2)}, u32[]{:S(2)}) %collective-permute-start.3) | collective-permute-done | bytes 12320 | tf_op jit(solution)/shard_map/ppermute | solution.py:74
  32.3 1.3 %broadcast_multiply_fusion = f32[2,2,4,9,128,128]{5,4,1,3,2,0:T(8,128)S(1)} fusion(f32[2,2,4,128,128]{4,3,1,2,0:T(8,128)S(1)} %fusion.11, f32[9,2,2,128,128]{4,3,2,1,0:T(8,128)S(1)} %fusion.16), kind=kLoop, calls=%fused_computation.6 | loop fusion | flops 2359296 | bytes 12845056 | tf_op jit(solution)/shard_map/jvp()/mul | solution.py:44
  33.7 1.5 %fusion = f32[2,64,36,128,1]{3,1,4,2,0:T(8,128)S(1)} fusion(f32[2,2,36,128,128]{4,3,1,2,0:T(8,128)S(1)} %bitcast.351, f32[2,2,128,128]{3,2,1,0:T(8,128)S(1)} %convert_multiply_fusion, bf16[2,2,64,128]{3,2,1,0:T(8,128)(2,1)S(1)} %select_reduce_fusion), kind=kOutput, calls=%fused_computation.3 | convolution fusion | flops 306708480 | bytes 12124160 | tf_op jit(solution)/shard_map/jvp(bnqij,bncj->bqci)/dot_general | solution.py:46
  35.9 0.7 %fusion.84 = f32[1,2,128]{2,0,1:T(1,128)} fusion(f32[2,128,64]{1,2,0:T(8,128)S(1)} %fusion.61, f32[64]{0:T(128)S(1)} %copy-done.8), kind=kOutput, calls=%fused_computation.157 | convolution fusion | flops 262144 | bytes 66816 | tf_op jit(solution)/shard_map/jvp(h,bhi->bi)/dot_general | solution.py:53
  37.6 6.0 %convert_convert_fusion = f32[2,36,128,2,128]{4,2,3,1,0:T(8,128)} fusion(f32[2,36,64,128]{3,2,1,0:T(8,128)S(1)} %bitcast.355, f32[36,64]{1,0:T(8,128)S(1)} %mul.357, bf16[2,2,64,128]{3,2,1,0:T(8,128)(2,1)S(1)} %select_reduce_fusion), kind=kOutput, calls=%fused_computation.4 | convolution fusion | flops 307298304 | bytes 11871232 | tf_op jit(solution)/shard_map/transpose(jvp(bnqij,bncj->bqci))/dot_general | solution.py:46
  43.5 5.9 %multiply_reduce_fusion.1 = (f32[2,2,9,128,128]{4,3,1,2,0:T(8,128)S(1)}, f32[2,2,4,128,128]{4,3,1,2,0:T(8,128)S(1)}) fusion(f32[2,2,4,9,128,128]{5,4,1,3,2,0:T(8,128)} %bitcast.350, f32[2,2,128,128]{3,2,1,0:T(8,128)S(1)} %copy-done.2, f32[2,2,4,128,128]{4,3,1,2,0:T(8,128)S(1)} %fusion.11, f32[9,2,2,128,128]{4,3,2,1,0:T(8,128)S(1)} %fusion.16), kind=kLoop, calls=%fused_computation.1 | loop fusion | flops 10944512 | bytes 16515072 | tf_op jit(solution)/shard_map/transpose(jvp())/reduce_sum | solution.py:44
  50.8 0.5 fusion.31
  52.0 2.5 %collective-permute-start.5 = (f32[3,2,3,128]{3,1,2,0:T(2,128)S(1)}, f32[3,2,3,128]{3,1,2,0:T(2,128)S(1)}, u32[]{:S(2)}, u32[]{:S(2)}) collective-permute-start(f32[3,2,3,128]{3,1,2,0:T(2,128)S(1)} %copy.112), channel_id=1, source_target_pairs={{96,0},{192,96},{288,192},{384,288},{480,384},{576,480},{672,576},... | collective-permute-start | bytes 27656 | tf_op jit(solution)/shard_map/ppermute | solution.py:71
  54.6 1.2 %collective-permute-done.5 = f32[3,2,3,128]{3,1,2,0:T(2,128)S(1)} collective-permute-done((f32[3,2,3,128]{3,1,2,0:T(2,128)S(1)}, f32[3,2,3,128]{3,1,2,0:T(2,128)S(1)}, u32[]{:S(2)}, u32[]{:S(2)}) %collective-permute-start.5) | collective-permute-done | bytes 9248 | tf_op jit(solution)/shard_map/ppermute | solution.py:71
  55.8 7.2 %collective-permute-start.7 = (f32[3,2,3,128]{3,0,1,2:T(4,128)S(1)}, f32[3,2,3,128]{3,0,1,2:T(4,128)S(1)}, u32[]{:S(2)}, u32[]{:S(2)}) collective-permute-start(f32[3,2,3,128]{3,0,1,2:T(4,128)S(1)} %get-tuple-element.21), channel_id=1, source_target_pairs={{1,0},{2,1},{3,2},{4,3},{5,4},{6,5},{7,6},{8,7},{9,8},{10,9},{11,1... | collective-permute-start | bytes 27656 | tf_op jit(solution)/shard_map/ppermute | solution.py:74
  63.0 1.9 %collective-permute-start.6 = (f32[3,2,3,128]{3,0,1,2:T(4,128)S(1)}, f32[3,2,3,128]{3,0,1,2:T(4,128)S(1)}, u32[]{:S(2)}, u32[]{:S(2)}) collective-permute-start(f32[3,2,3,128]{3,0,1,2:T(4,128)S(1)} %get-tuple-element.22), channel_id=1, source_target_pairs={{0,1},{1,2},{2,3},{3,4},{4,5},{5,6},{6,7},{7,8},{8,9},{9,10},{10,1... | collective-permute-start | bytes 27656 | tf_op jit(solution)/shard_map/ppermute | solution.py:73
  65.0 5.8 %collective-permute-done.6 = f32[3,2,3,128]{3,0,1,2:T(4,128)S(1)} collective-permute-done((f32[3,2,3,128]{3,0,1,2:T(4,128)S(1)}, f32[3,2,3,128]{3,0,1,2:T(4,128)S(1)}, u32[]{:S(2)}, u32[]{:S(2)}) %collective-permute-start.6) | collective-permute-done | bytes 9248 | tf_op jit(solution)/shard_map/ppermute | solution.py:73
  71.1 0.6 copy.165
  (102 shorter events, 7.0 us)
Async XLA Ops:
  0.6 35.0 %copy-start = (f32[192,64]{0,1:T(8,128)S(1)}, f32[192,64]{0,1:T(8,128)}, u32[]{:S(2)}) copy-start(f32[192,64]{0,1:T(8,128)} %param.16) | copy-start | bytes 147460
  0.6 29.6 %copy-start.5 = (f32[4,64]{1,0:T(4,128)S(1)}, f32[4,64]{1,0:T(4,128)}, u32[]{:S(2)}) copy-start(f32[4,64]{1,0:T(4,128)} %param.14) | copy-start | bytes 3076
  3.0 13.4 %collective-permute-start = (f32[3,2,4,128]{3,2,1,0:T(4,128)S(1)}, f32[3,2,4,128]{3,2,1,0:T(4,128)S(1)}, u32[]{:S(2)}, u32[]{:S(2)}) collective-permute-start(f32[3,2,4,128]{3,2,1,0:T(4,128)S(1)} %copy.129), channel_id=1, source_target_pairs={{0,96},{96,192},{192,288},{288,384},{384,480},{480,576},{576,672},... | collective-permute-start | bytes 36872 | tf_op jit(solution)/shard_map/ppermute | solution.py:70
  5.6 10.8 %collective-permute-start.1 = (f32[3,2,4,128]{3,0,2,1:T(4,128)S(1)}, f32[3,2,4,128]{3,0,2,1:T(4,128)S(1)}, u32[]{:S(2)}, u32[]{:S(2)}) collective-permute-start(f32[3,2,4,128]{3,0,2,1:T(4,128)S(1)} %get-tuple-element.18), channel_id=1, source_target_pairs={{96,0},{192,96},{288,192},{384,288},{480,384},{576,480},{672,576},... | collective-permute-start | bytes 36872 | tf_op jit(solution)/shard_map/ppermute | solution.py:71
  16.3 17.3 %copy-start.1 = (f32[2,2,128,128]{3,2,1,0:T(8,128)}, f32[2,2,128,128]{3,2,1,0:T(8,128)S(1)}, u32[]{:S(2)}) copy-start(f32[2,2,128,128]{3,2,1,0:T(8,128)S(1)} %convert_multiply_fusion) | copy-start | bytes 786436
  16.5 12.3 %collective-permute-start.2 = (f32[3,2,4,128]{3,2,1,0:T(4,128)S(1)}, f32[3,2,4,128]{3,2,1,0:T(4,128)S(1)}, u32[]{:S(2)}, u32[]{:S(2)}) collective-permute-start(f32[3,2,4,128]{3,2,1,0:T(4,128)S(1)} %get-tuple-element.16), channel_id=1, source_target_pairs={{0,1},{1,2},{2,3},{3,4},{4,5},{5,6},{6,7},{7,8},{8,9},{9,10},{10,1... | collective-permute-start | bytes 36872 | tf_op jit(solution)/shard_map/ppermute | solution.py:73
  19.3 10.4 %collective-permute-start.3 = (f32[3,2,4,128]{3,2,1,0:T(4,128)S(1)}, f32[3,2,4,128]{3,2,1,0:T(4,128)S(1)}, u32[]{:S(2)}, u32[]{:S(2)}) collective-permute-start(f32[3,2,4,128]{3,2,1,0:T(4,128)S(1)} %get-tuple-element.15), channel_id=1, source_target_pairs={{1,0},{2,1},{3,2},{4,3},{5,4},{6,5},{7,6},{8,7},{9,8},{10,9},{11,1... | collective-permute-start | bytes 36872 | tf_op jit(solution)/shard_map/ppermute | solution.py:74
  30.3 1.8 %copy-start.3 = (f32[2,2,128,128]{3,2,1,0:T(8,128)}, f32[2,2,128,128]{3,2,1,0:T(8,128)S(1)}, u32[]{:S(2)}) copy-start(f32[2,2,128,128]{3,2,1,0:T(8,128)S(1)} %add_sqrt_fusion) | copy-start | bytes 786436
  33.7 1.6 %copy-start.6 = (f32[4,64]{1,0:T(4,128)S(1)}, f32[4,64]{1,0:T(4,128)}, u32[]{:S(2)}) copy-start(f32[4,64]{1,0:T(4,128)} %param.15) | copy-start | bytes 3076
  35.2 0.7 copy-start.8
  37.5 6.0 %copy-start.2 = (f32[2,2,128,128]{3,2,1,0:T(8,128)S(1)}, f32[2,2,128,128]{3,2,1,0:T(8,128)}, u32[]{:S(2)}) copy-start(f32[2,2,128,128]{3,2,1,0:T(8,128)} %copy-done.1) | copy-start | bytes 786436
  49.4 1.0 %copy-start.4 = (f32[2,2,128,128]{3,2,1,0:T(8,128)S(1)}, f32[2,2,128,128]{3,2,1,0:T(8,128)}, u32[]{:S(2)}) copy-start(f32[2,2,128,128]{3,2,1,0:T(8,128)} %copy-done.3) | copy-start | bytes 786436
  50.8 20.0 %copy-start.7 = (s32[1,1,8,2]{2,3,1,0:T(2,128)S(1)}, s32[1,1,8,2]{2,3,1,0:T(2,128)}, u32[]{:S(2)}) copy-start(s32[1,1,8,2]{2,3,1,0:T(2,128)} %param.13) | copy-start | bytes 196
  52.0 3.7 %collective-permute-start.5 = (f32[3,2,3,128]{3,1,2,0:T(2,128)S(1)}, f32[3,2,3,128]{3,1,2,0:T(2,128)S(1)}, u32[]{:S(2)}, u32[]{:S(2)}) collective-permute-start(f32[3,2,3,128]{3,1,2,0:T(2,128)S(1)} %copy.112), channel_id=1, source_target_pairs={{96,0},{192,96},{288,192},{384,288},{480,384},{576,480},{672,576},... | collective-permute-start | bytes 27656 | tf_op jit(solution)/shard_map/ppermute | solution.py:71
  54.5 1.3 %collective-permute-start.4 = (f32[3,2,3,128]{3,1,2,0:T(2,128)S(1)}, f32[3,2,3,128]{3,1,2,0:T(2,128)S(1)}, u32[]{:S(2)}, u32[]{:S(2)}) collective-permute-start(f32[3,2,3,128]{3,1,2,0:T(2,128)S(1)} %copy.106), channel_id=1, source_target_pairs={{0,96},{96,192},{192,288},{288,384},{384,480},{480,576},{576,672},... | collective-permute-start | bytes 27656 | tf_op jit(solution)/shard_map/ppermute | solution.py:70
  55.8 9.1 %collective-permute-start.7 = (f32[3,2,3,128]{3,0,1,2:T(4,128)S(1)}, f32[3,2,3,128]{3,0,1,2:T(4,128)S(1)}, u32[]{:S(2)}, u32[]{:S(2)}) collective-permute-start(f32[3,2,3,128]{3,0,1,2:T(4,128)S(1)} %get-tuple-element.21), channel_id=1, source_target_pairs={{1,0},{2,1},{3,2},{4,3},{5,4},{6,5},{7,6},{8,7},{9,8},{10,9},{11,1... | collective-permute-start | bytes 27656 | tf_op jit(solution)/shard_map/ppermute | solution.py:74
  63.0 7.8 %collective-permute-start.6 = (f32[3,2,3,128]{3,0,1,2:T(4,128)S(1)}, f32[3,2,3,128]{3,0,1,2:T(4,128)S(1)}, u32[]{:S(2)}, u32[]{:S(2)}) collective-permute-start(f32[3,2,3,128]{3,0,1,2:T(4,128)S(1)} %get-tuple-element.22), channel_id=1, source_target_pairs={{0,1},{1,2},{2,3},{3,4},{4,5},{5,6},{6,7},{7,8},{8,9},{9,10},{10,1... | collective-permute-start | bytes 27656 | tf_op jit(solution)/shard_map/ppermute | solution.py:73

commit v5 on v4

--- a/solution.py
+++ b/solution.py
@@ -32,18 +32,17 @@
 def block_energies(own_pos, others_pos, others_feat, masks, radial, readin, readout):
     count = radial.shape[0]
     atoms = own_pos.shape[2]
-    listed = others_pos.shape[1]
+    listed = others_pos.shape[2] // atoms
     centres = 0.5 + jnp.arange(count).astype(jnp.float32)
-    rel = others_pos[:, :, :, None, :] - own_pos[:, None, :, :, None]
-    dist = jnp.sqrt(jnp.sum(rel * rel, axis=2) + 0.25)
-    offset = dist[:, :, None] - centres[:, None, None]
+    rel = others_pos[:, :, None, :] - own_pos[:, :, :, None]
+    dist = jnp.sqrt(jnp.sum(rel * rel, axis=1) + 0.25)
+    offset = dist[:, None] - centres[:, None, None]
     basis = jnp.exp(-0.5 * offset * offset)
-    angular = harmonics(jnp.moveaxis(rel, 2, 0), dist)
-    angular = jnp.moveaxis(angular, 0, 2)
+    angular = jnp.moveaxis(harmonics(jnp.moveaxis(rel, 1, 0), dist), 0, 1)
     weight = masks.astype(jnp.float32) * (1.0 / math.sqrt(listed * atoms))
-    tiles = basis[:, :, :, None] * angular[:, :, None] * weight[:, :, None, None]
-    tiles = tiles.reshape(tiles.shape[:2] + (count * 9, atoms, atoms)).astype(jnp.bfloat16)
-    proj = jnp.einsum("bnqij,bncj->bqci", tiles, others_feat, preferred_element_type=jnp.float32)
+    tiles = basis[:, :, None] * angular[:, None] * weight[:, None, None]
+    tiles = tiles.reshape((tiles.shape[0], count * 9) + tiles.shape[3:]).astype(jnp.bfloat16)
+    proj = jnp.einsum("bqij,bcj->bqci", tiles, others_feat, preferred_element_type=jnp.float32)
     proj = proj.reshape((proj.shape[0], count, 9) + proj.shape[2:])
     message = jnp.sum(radial[None, :, None, :, None] * proj, axis=1)
     first = jnp.sum(message[:, 1:4] * message[:, 1:4], axis=1)
@@ -51,6 +50,10 @@
     invariants = jnp.concatenate([message[:, 0], first, second], axis=1)
     hidden = jax.nn.silu(jnp.einsum("fh,bfi->bhi", readin, invariants, precision=HIGHEST))
     return jnp.einsum("h,bhi->bi", readout, hidden, precision=HIGHEST)
+
+
+def end_to_end(x):
+    return jnp.swapaxes(x, 1, 2).reshape(x.shape[0], x.shape[2], x.shape[1] * x.shape[3])
 
 
 def select_slots(table, chosen):
@@ -111,14 +114,14 @@
         features(ghost_kind.reshape(-1)).reshape(-1, 8 * sends, atoms).transpose(1, 0, 2)
     )
 
+    masks_joined = end_to_end(pair_masks)
+
     def energies_of(own_now, ghost_now):
         table_pos = jnp.concatenate([own_now, ghost_now], axis=0)
         table_feat = jnp.concatenate([own_feats32, ghost_feats32], axis=0)
-        others_pos = select_slots(table_pos, neighbours)
-        others_feat = select_slots(table_feat, neighbours).astype(jnp.bfloat16)
-        return block_energies(
-            own_now, others_pos, others_feat, pair_masks, radial, readin, readout
-        )
+        others_pos = end_to_end(select_slots(table_pos, neighbours))
+        others_feat = end_to_end(select_slots(table_feat, neighbours).astype(jnp.bfloat16))
+        return block_energies(own_now, others_pos, others_feat, masks_joined, radial, readin, readout)
 
     energy, pullback = jax.vjp(energies_of, own_pos, ghost_pos)
     grad_own, grad_ghost = pullback(jnp.ones_like(energy))

time: 72.8 us -> 73.8 us (1.014)
  the two profiles are of different devices: /device:TPU:1 before, /device:TPU:7 now
where the time goes in v5:
time: 73.8 us; the launch traced here: 73.3 us
  starting transfers between devices  32.9 us (45%)
  other arithmetic  11.8 us (16%)
  waiting for transfers between devices  10.8 us (15%)
  local copies, waits for them, and re-layouts  8.79 us (12%)
  matrix products  7.71 us (10%)
  between operations  1.33 us (2%)
    ppermute x2, starting transfers between devices, halo(): from_right_y = lax.ppermute(rows[:, 0], 'gy', down_y)  17.6 us
    ppermute x2, starting transfers between devices, halo(): from_left_x = lax.ppermute(grid[2], 'gx', up_x)  10.8 us
    ppermute x2, waiting for transfers between devices, halo(): from_left_y = lax.ppermute(rows[:, 2], 'gy', up_y)  5.81 us
    ppermute x2, waiting for transfers between devices, halo(): from_right_x = lax.ppermute(grid[0], 'gx', down_x)  4.21 us
    dot_general x2, matrix products, block_energies(): jnp.einsum('bqij,bcj->bqci', tiles, others_feat, preferred_element_type=j...  3.89 us
    ppermute x2, starting transfers between devices, halo(): from_left_y = lax.ppermute(rows[:, 2], 'gy', up_y)  3.84 us
    unnamed x52, local copies, waits for them, and re-layouts  2.94 us
    reduce_sum x1, other arithmetic, block_energies(): tiles = basis[:, :, None] * angular[:, None] * weight[:, None, None]  1.92 us
  transfers between devices with their start and end apart: 8, of which 3 were waited for; matrix products, arithmetic and copies ran while one was open for 9% of the time, Pallas kernels for 0%

profile of v5, /device:TPU:7, one launch (start us, length us, event | category | flops | bytes accessed | tf_op | source)
XLA Modules:
  0.0 73.3 jit_solution(17430966992185960458)
XLA Ops:
  0.7 0.7 %reshape.191 = f32[3,2,128]{2,1,0:T(2,128)S(1)} reshape(f32[3,256]{1,0:T(4,128)} %param.9) | data formatting | bytes 6144 | tf_op jit(solution)/shard_map/reshape | solution.py:98
  2.1 0.9 %fusion.98 = f32[8,2,4,128]{3,0,2,1:T(8,128)S(1)} fusion(f32[2,1,128]{2,0,1:T(2,128)S(1)} %convert_bitcast_fusion.1, f32[2,3,128]{2,0,1:T(2,128)S(1)} %bitcast.363, s32[8,2]{0,1:T(2,128)} %bitcast.386), kind=kOutput, calls=%fused_computation.194 | convolution fusion | flops 197664 | bytes 36928 | tf_op jit(solution)/shard_map/dgb,bra->dgra/dot_general | solution.py:103
  3.7 9.1 %collective-permute-start = (f32[3,2,4,128]{3,2,1,0:T(4,128)S(1)}, f32[3,2,4,128]{3,2,1,0:T(4,128)S(1)}, u32[]{:S(2)}, u32[]{:S(2)}) collective-permute-start(f32[3,2,4,128]{3,2,1,0:T(4,128)S(1)} %copy.173), channel_id=1, source_target_pairs={{0,96},{96,192},{192,288},{288,384},{384,480},{480,576},{576,672},... | collective-permute-start | bytes 36872 | tf_op jit(solution)/shard_map/ppermute | solution.py:73
  13.0 0.7 iota_compare_fusion
  13.7 0.9 %convolution_bitcast_fusion.2 = f32[64,256]{1,0:T(8,128)S(1)} fusion(f32[4,64]{1,0:T(4,128)} %param.14, s32[256]{0:T(256)} %param.10), kind=kOutput, calls=%fused_computation.24 | convolution fusion | flops 787456 | bytes 67584 | tf_op jit(solution)/shard_map/dot_general | solution.py:110
  14.6 1.1 %copy.134 = s32[2,2,128,128]{2,3,1,0:T(8,128)S(1)} copy(s32[2,2,128,128]{3,2,1,0:T(8,128)} %param.12) | data formatting | bytes 524288 | tf_op args[3]
  16.4 1.9 %collective-permute-start.2 = (f32[3,2,4,128]{3,2,1,0:T(4,128)S(1)}, f32[3,2,4,128]{3,2,1,0:T(4,128)S(1)}, u32[]{:S(2)}, u32[]{:S(2)}) collective-permute-start(f32[3,2,4,128]{3,2,1,0:T(4,128)S(1)} %get-tuple-element.16), channel_id=1, source_target_pairs={{0,1},{1,2},{2,3},{3,4},{4,5},{5,6},{6,7},{7,8},{8,9},{9,10},{10,1... | collective-permute-start | bytes 36872 | tf_op jit(solution)/shard_map/ppermute | solution.py:76
  19.6 0.8 %copy.135 = f32[2,128,256]{2,1,0:T(8,128)} copy(f32[2,128,256]{1,2,0:T(8,128)S(1)} %bitcast.360) | data formatting | bytes 524288 | tf_op jit(solution)/shard_map/jvp()/mul | solution.py:42
  21.0 10.4 %collective-permute-start.3 = (f32[3,2,4,128]{3,2,1,0:T(4,128)S(1)}, f32[3,2,4,128]{3,2,1,0:T(4,128)S(1)}, u32[]{:S(2)}, u32[]{:S(2)}) collective-permute-start(f32[3,2,4,128]{3,2,1,0:T(4,128)S(1)} %get-tuple-element.15), channel_id=1, source_target_pairs={{1,0},{2,1},{3,2},{4,3},{5,4},{6,5},{7,6},{8,7},{9,8},{10,9},{11,1... | collective-permute-start | bytes 36872 | tf_op jit(solution)/shard_map/ppermute | solution.py:77
  31.4 0.8 %collective-permute-done.3 = f32[3,2,4,128]{3,2,1,0:T(4,128)S(1)} collective-permute-done((f32[3,2,4,128]{3,2,1,0:T(4,128)S(1)}, f32[3,2,4,128]{3,2,1,0:T(4,128)S(1)}, u32[]{:S(2)}, u32[]{:S(2)}) %collective-permute-start.3) | collective-permute-done | bytes 12320 | tf_op jit(solution)/shard_map/ppermute | solution.py:77
  33.4 0.8 %add_sqrt_fusion = f32[2,128,256]{2,1,0:T(8,128)} fusion(f32[2,128,256]{2,1,0:T(8,128)S(1)} %fusion.17), kind=kLoop, calls=%fused_computation.125 | loop fusion | flops 65536 | bytes 524288 | tf_op jit(solution)/shard_map/jvp()/sqrt | solution.py:38
  36.0 0.7 copy.130
  36.7 0.9 %reshape.205 = bf16[2,64,256,1]{2,1,0,3:T(8,128)(2,1)S(1)} reshape(bf16[2,64,2,128]{3,2,1,0:T(2,128)(2,1)} %copy.130) | data formatting | bytes 131072 | tf_op jit(solution)/shard_map/jvp()/reshape | solution.py:56
  37.6 1.2 %fusion.15 = f32[2,4,128,256]{3,2,1,0:T(8,128)S(1)} fusion(f32[4]{0:T(128)} %broadcast_add_fusion, f32[2,128,256]{2,1,0:T(8,128)} %add_sqrt_fusion), kind=kLoop, calls=%fused_computation.31 | loop fusion | flops 786432 | bytes 1310736 | tf_op jit(solution)/shard_map/jvp()/exp | solution.py:40
  38.8 1.1 %broadcast_multiply_fusion = f32[2,4,9,128,256]{4,3,2,1,0:T(8,128)S(1)} fusion(f32[2,4,128,256]{3,2,1,0:T(8,128)S(1)} %fusion.15, f32[9,2,128,256]{3,2,1,0:T(8,128)S(1)} %fusion.20), kind=kLoop, calls=%fused_computation.8 | loop fusion | flops 2359296 | bytes 12845056 | tf_op jit(solution)/shard_map/jvp()/mul | solution.py:43
  40.0 1.6 %fusion.4 = f32[2,64,36,128]{3,1,2,0:T(8,128)S(1)} fusion(f32[2,36,128,256]{3,2,1,0:T(8,128)S(1)} %bitcast.352, f32[2,128,256]{2,1,0:T(8,128)S(1)} %copy-done.1, bf16[2,64,256,1]{2,1,0,3:T(8,128)(2,1)S(1)} %reshape.205), kind=kOutput, calls=%fused_computation.6 | convolution fusion | flops 306708480 | bytes 12124160 | tf_op jit(solution)/shard_map/jvp(bqij,bcj->bqci)/dot_general | solution.py:45
  43.7 2.3 %convolution_convert_fusion = bf16[2,36,128,256]{3,2,1,0:T(8,128)(2,1)S(1)} fusion(f32[2,36,64,128]{3,2,1,0:T(8,128)S(1)} %bitcast.357, f32[36,64]{1,0:T(8,128)S(1)} %copy-done.3, bf16[2,64,256,1]{2,1,0,3:T(8,128)(2,1)S(1)} %reshape.205), kind=kOutput, calls=%fused_computation.9 | convolution fusion | flops 304939008 | bytes 7152640 | tf_op jit(solution)/shard_map/transpose(jvp(bqij,bcj->bqci))/dot_general | solution.py:45
  46.0 1.9 %fusion.2 = (f32[2,9,128,256]{3,2,1,0:T(8,128)S(1)}, f32[2,4,128,256]{3,2,1,0:T(8,128)S(1)}) fusion(bf16[2,4,9,128,256]{4,3,2,1,0:T(8,128)(2,1)S(1)} %bitcast.356, f32[2,128,256]{2,1,0:T(8,128)S(1)} %copy-done.1, f32[2,4,128,256]{3,2,1,0:T(8,128)S(1)} %fusion.15, f32[9,2,128,256]{3,2,1,0:T(8,128)S(1)} %fusion.20), kind=kLoop, calls=%fused_computation.3 | loop fusion | flops 13303808 | bytes 11796480 | tf_op jit(solution)/shard_map/transpose(jvp())/reduce_sum | solution.py:43
  50.6 0.7 %fusion.88 = f32[1,2,128]{2,0,1:T(1,128)} fusion(f32[2,128,64]{1,2,0:T(8,128)S(1)} %copy-done.7, f32[64]{0:T(128)S(1)} %copy-done.18), kind=kOutput, calls=%fused_computation.161 | convolution fusion | flops 262144 | bytes 66816 | tf_op jit(solution)/shard_map/jvp(h,bhi->bi)/dot_general | solution.py:52
  51.4 1.6 %collective-permute-start.4 = (f32[3,2,3,128]{3,1,2,0:T(2,128)S(1)}, f32[3,2,3,128]{3,1,2,0:T(2,128)S(1)}, u32[]{:S(2)}, u32[]{:S(2)}) collective-permute-start(f32[3,2,3,128]{3,1,2,0:T(2,128)S(1)} %copy.152), channel_id=1, source_target_pairs={{0,96},{96,192},{192,288},{288,384},{384,480},{480,576},{576,672},... | collective-permute-start | bytes 27656 | tf_op jit(solution)/shard_map/ppermute | solution.py:73
  53.1 4.2 %collective-permute-done.5 = f32[3,2,3,128]{3,1,2,0:T(2,128)S(1)} collective-permute-done((f32[3,2,3,128]{3,1,2,0:T(2,128)S(1)}, f32[3,2,3,128]{3,1,2,0:T(2,128)S(1)}, u32[]{:S(2)}, u32[]{:S(2)}) %collective-permute-start.5) | collective-permute-done | bytes 9248 | tf_op jit(solution)/shard_map/ppermute | solution.py:74
  57.4 7.2 %collective-permute-start.7 = (f32[3,2,3,128]{3,0,1,2:T(4,128)S(1)}, f32[3,2,3,128]{3,0,1,2:T(4,128)S(1)}, u32[]{:S(2)}, u32[]{:S(2)}) collective-permute-start(f32[3,2,3,128]{3,0,1,2:T(4,128)S(1)} %get-tuple-element.21), channel_id=1, source_target_pairs={{1,0},{2,1},{3,2},{4,3},{5,4},{6,5},{7,6},{8,7},{9,8},{10,9},{11,1... | collective-permute-start | bytes 27656 | tf_op jit(solution)/shard_map/ppermute | solution.py:77
  64.6 1.9 %collective-permute-start.6 = (f32[3,2,3,128]{3,0,1,2:T(4,128)S(1)}, f32[3,2,3,128]{3,0,1,2:T(4,128)S(1)}, u32[]{:S(2)}, u32[]{:S(2)}) collective-permute-start(f32[3,2,3,128]{3,0,1,2:T(4,128)S(1)} %get-tuple-element.22), channel_id=1, source_target_pairs={{0,1},{1,2},{2,3},{3,4},{4,5},{5,6},{6,7},{7,8},{8,9},{9,10},{10,1... | collective-permute-start | bytes 27656 | tf_op jit(solution)/shard_map/ppermute | solution.py:76
  66.6 5.8 %collective-permute-done.6 = f32[3,2,3,128]{3,0,1,2:T(4,128)S(1)} collective-permute-done((f32[3,2,3,128]{3,0,1,2:T(4,128)S(1)}, f32[3,2,3,128]{3,0,1,2:T(4,128)S(1)}, u32[]{:S(2)}, u32[]{:S(2)}) %collective-permute-start.6) | collective-permute-done | bytes 9248 | tf_op jit(solution)/shard_map/ppermute | solution.py:76
  (129 shorter events, 12.6 us)
Async XLA Ops:
  0.6 41.3 %copy-start = (f32[192,64]{0,1:T(8,128)S(1)}, f32[192,64]{0,1:T(8,128)}, u32[]{:S(2)}) copy-start(f32[192,64]{0,1:T(8,128)} %param.16) | copy-start | bytes 147460
  0.6 19.8 %copy-start.10 = (f32[4,64]{1,0:T(4,128)S(1)}, f32[4,64]{1,0:T(4,128)}, u32[]{:S(2)}) copy-start(f32[4,64]{1,0:T(4,128)} %param.15) | copy-start | bytes 3076
  3.0 13.4 %collective-permute-start.1 = (f32[3,2,4,128]{3,0,2,1:T(4,128)S(1)}, f32[3,2,4,128]{3,0,2,1:T(4,128)S(1)}, u32[]{:S(2)}, u32[]{:S(2)}) collective-permute-start(f32[3,2,4,128]{3,0,2,1:T(4,128)S(1)} %get-tuple-element.18), channel_id=1, source_target_pairs={{96,0},{192,96},{288,192},{384,288},{480,384},{576,480},{672,576},... | collective-permute-start | bytes 36872 | tf_op jit(solution)/shard_map/ppermute | solution.py:74
  3.7 12.7 %collective-permute-start = (f32[3,2,4,128]{3,2,1,0:T(4,128)S(1)}, f32[3,2,4,128]{3,2,1,0:T(4,128)S(1)}, u32[]{:S(2)}, u32[]{:S(2)}) collective-permute-start(f32[3,2,4,128]{3,2,1,0:T(4,128)S(1)} %copy.173), channel_id=1, source_target_pairs={{0,96},{96,192},{192,288},{288,384},{384,480},{480,576},{576,672},... | collective-permute-start | bytes 36872 | tf_op jit(solution)/shard_map/ppermute | solution.py:73
  13.0 20.0 %copy-start.13 = (f32[3]{0:T(128)}, f32[3]{0:T(128)S(1)}, u32[]{:S(2)}) copy-start(f32[3]{0:T(128)S(1)} %slice.217) | copy-start | bytes 40
  13.7 19.5 %copy-start.4 = (pred[2,2,18]{1,2,0:T(8,128)(4,1)}, pred[2,2,18]{1,2,0:T(8,128)(4,1)S(1)}, u32[]{:S(2)}) copy-start(pred[2,2,18]{1,2,0:T(8,128)(4,1)S(1)} %iota_compare_fusion) | copy-start | bytes 220
  16.4 15.0 %collective-permute-start.2 = (f32[3,2,4,128]{3,2,1,0:T(4,128)S(1)}, f32[3,2,4,128]{3,2,1,0:T(4,128)S(1)}, u32[]{:S(2)}, u32[]{:S(2)}) collective-permute-start(f32[3,2,4,128]{3,2,1,0:T(4,128)S(1)} %get-tuple-element.16), channel_id=1, source_target_pairs={{0,1},{1,2},{2,3},{3,4},{4,5},{5,6},{6,7},{7,8},{8,9},{9,10},{10,1... | collective-permute-start | bytes 36872 | tf_op jit(solution)/shard_map/ppermute | solution.py:76
  21.0 11.2 %collective-permute-start.3 = (f32[3,2,4,128]{3,2,1,0:T(4,128)S(1)}, f32[3,2,4,128]{3,2,1,0:T(4,128)S(1)}, u32[]{:S(2)}, u32[]{:S(2)}) collective-permute-start(f32[3,2,4,128]{3,2,1,0:T(4,128)S(1)} %get-tuple-element.15), channel_id=1, source_target_pairs={{1,0},{2,1},{3,2},{4,3},{5,4},{6,5},{7,6},{8,7},{9,8},{10,9},{11,1... | collective-permute-start | bytes 36872 | tf_op jit(solution)/shard_map/ppermute | solution.py:77
  34.3 0.7 copy-start.8
  34.3 0.7 copy-start.9
  34.9 0.8 %copy-start.11 = (pred[2,2,18]{2,1,0:T(4,128)(4,1)S(1)}, pred[2,2,18]{2,1,0:T(4,128)(4,1)}, u32[]{:S(2)}) copy-start(pred[2,2,18]{2,1,0:T(4,128)(4,1)} %copy.124) | copy-start | bytes 220
  38.8 1.2 %copy-start.1 = (f32[2,128,256]{2,1,0:T(8,128)S(1)}, f32[2,128,256]{2,1,0:T(8,128)}, u32[]{:S(2)}) copy-start(f32[2,128,256]{2,1,0:T(8,128)} %copy.135) | copy-start | bytes 786436
  43.0 0.7 copy-start.3
  48.0 1.0 %copy-start.2 = (f32[2,128,256]{2,1,0:T(8,128)S(1)}, f32[2,128,256]{2,1,0:T(8,128)}, u32[]{:S(2)}) copy-start(f32[2,128,256]{2,1,0:T(8,128)} %add_sqrt_fusion) | copy-start | bytes 786436
  48.0 0.9 %copy-start.15 = (f32[4]{0:T(128)S(1)}, f32[4]{0:T(128)}, u32[]{:S(2)}) copy-start(f32[4]{0:T(128)} %broadcast_add_fusion) | copy-start | bytes 52
  49.4 1.0 %copy-start.5 = (pred[2,2,18]{1,2,0:T(8,128)(4,1)S(1)}, pred[2,2,18]{1,2,0:T(8,128)(4,1)}, u32[]{:S(2)}) copy-start(pred[2,2,18]{1,2,0:T(8,128)(4,1)} %copy-done.4) | copy-start | bytes 220
  49.4 1.2 %copy-start.7 = (f32[2,128,64]{1,2,0:T(8,128)S(1)}, f32[2,128,64]{1,2,0:T(8,128)}, u32[]{:S(2)}) copy-start(f32[2,128,64]{1,2,0:T(8,128)} %copy-done.6) | copy-start | bytes 196612
  49.4 1.2 %copy-start.18 = (f32[64]{0:T(128)S(1)}, f32[64]{0:T(128)}, u32[]{:S(2)}) copy-start(f32[64]{0:T(128)} %param.17) | copy-start | bytes 772
  49.4 3.6 %copy-start.14 = (f32[3]{0:T(128)S(1)}, f32[3]{0:T(128)}, u32[]{:S(2)}) copy-start(f32[3]{0:T(128)} %copy-done.13) | copy-start | bytes 40
  49.4 23.0 %copy-start.12 = (s32[1,1,8,2]{2,3,1,0:T(2,128)S(1)}, s32[1,1,8,2]{2,3,1,0:T(2,128)}, u32[]{:S(2)}) copy-start(s32[1,1,8,2]{2,3,1,0:T(2,128)} %param.13) | copy-start | bytes 196
  51.4 5.9 %collective-permute-start.4 = (f32[3,2,3,128]{3,1,2,0:T(2,128)S(1)}, f32[3,2,3,128]{3,1,2,0:T(2,128)S(1)}, u32[]{:S(2)}, u32[]{:S(2)}) collective-permute-start(f32[3,2,3,128]{3,1,2,0:T(2,128)S(1)} %copy.152), channel_id=1, source_target_pairs={{0,96},{96,192},{192,288},{288,384},{384,480},{480,576},{576,672},... | collective-permute-start | bytes 27656 | tf_op jit(solution)/shard_map/ppermute | solution.py:73
  53.0 4.3 %collective-permute-start.5 = (f32[3,2,3,128]{3,1,2,0:T(2,128)S(1)}, f32[3,2,3,128]{3,1,2,0:T(2,128)S(1)}, u32[]{:S(2)}, u32[]{:S(2)}) collective-permute-start(f32[3,2,3,128]{3,1,2,0:T(2,128)S(1)} %copy.158), channel_id=1, source_target_pairs={{96,0},{192,96},{288,192},{384,288},{480,384},{576,480},{672,576},... | collective-permute-start | bytes 27656 | tf_op jit(solution)/shard_map/ppermute | solution.py:74
  57.4 9.2 %collective-permute-start.7 = (f32[3,2,3,128]{3,0,1,2:T(4,128)S(1)}, f32[3,2,3,128]{3,0,1,2:T(4,128)S(1)}, u32[]{:S(2)}, u32[]{:S(2)}) collective-permute-start(f32[3,2,3,128]{3,0,1,2:T(4,128)S(1)} %get-tuple-element.21), channel_id=1, source_target_pairs={{1,0},{2,1},{3,2},{4,3},{5,4},{6,5},{7,6},{8,7},{9,8},{10,9},{11,1... | collective-permute-start | bytes 27656 | tf_op jit(solution)/shard_map/ppermute | solution.py:77
  64.6 7.8 %collective-permute-start.6 = (f32[3,2,3,128]{3,0,1,2:T(4,128)S(1)}, f32[3,2,3,128]{3,0,1,2:T(4,128)S(1)}, u32[]{:S(2)}, u32[]{:S(2)}) collective-permute-start(f32[3,2,3,128]{3,0,1,2:T(4,128)S(1)} %get-tuple-element.22), channel_id=1, source_target_pairs={{0,1},{1,2},{2,3},{3,4},{4,5},{5,6},{6,7},{7,8},{8,9},{9,10},{10,1... | collective-permute-start | bytes 27656 | tf_op jit(solution)/shard_map/ppermute | solution.py:76
  (3 other events, 2.0 us)

commit v6 on v3

--- a/solution.py
+++ b/solution.py
@@ -40,7 +40,7 @@
     weight = pair_mask.astype(jnp.float32) * (1.0 / math.sqrt(listed * atoms))
     tiles = (basis[:, None] * angular[None] * weight[None, None]).reshape(count * 9, atoms, atoms)
     return jnp.einsum(
-        "qij,cj->qci", tiles.astype(jnp.bfloat16), other_feat, preferred_element_type=jnp.float32
+        "qij,cj->qic", tiles.astype(jnp.bfloat16), other_feat, preferred_element_type=jnp.float32
     )
 
 
@@ -49,18 +49,18 @@
     width = others_feat.shape[1]
     atoms = own_pos.shape[1]
     listed = others_pos.shape[0]
-    total = jnp.zeros((count * 9, width, atoms), jnp.float32)
+    total = jnp.zeros((count * 9, atoms, width), jnp.float32)
     for slot in range(listed):
         total = total + tile_terms(
             own_pos, others_pos[slot], others_feat[slot], masks[slot], listed, count
         )
-    proj = total.reshape(count, 9, width, atoms)
-    message = jnp.sum(radial[:, None, :, None] * proj, axis=0)
+    proj = total.reshape(count, 9, atoms, width)
+    message = jnp.sum(radial[:, None, None, :] * proj, axis=0)
     first = jnp.sum(message[1:4] * message[1:4], axis=0)
     second = jnp.sum(message[4:9] * message[4:9], axis=0)
-    invariants = jnp.concatenate([message[0], first, second], axis=0)
-    hidden = jax.nn.silu(jnp.dot(readin.T, invariants, precision=HIGHEST))
-    return jnp.dot(readout, hidden, precision=HIGHEST)
+    invariants = jnp.concatenate([message[0], first, second], axis=1)
+    hidden = jax.nn.silu(jnp.dot(invariants, readin, precision=HIGHEST))
+    return jnp.dot(hidden, readout, precision=HIGHEST)
 
 
 def select_slots(table, chosen):

time: 61 us -> 61 us (level)
  no operation moved by 1% of the time
where the time goes in v6:
time: 61 us; the launch traced here: 60.4 us
  starting transfers between devices  34.1 us (56%)
  other arithmetic  11.7 us (19%)
  matrix products  8.15 us (13%)
  local copies, waits for them, and re-layouts  2.47 us (4%)
  waiting for transfers between devices  2.25 us (4%)
  between operations  1.73 us (3%)
    ppermute x2, starting transfers between devices, halo(): from_right_y = lax.ppermute(rows[:, 0], 'gy', down_y)  16.4 us
    ppermute x2, starting transfers between devices, halo(): from_right_x = lax.ppermute(grid[0], 'gx', down_x)  13.9 us
    dot_general x8, matrix products, tile_terms(): jnp.einsum('qij,cj->qic', tiles.astype(jnp.bfloat16), other_feat, preferr...  4.2 us
    ppermute x2, starting transfers between devices, halo(): from_left_y = lax.ppermute(rows[:, 2], 'gy', up_y)  3.84 us
    reduce_sum x2, other arithmetic, tile_terms(): basis[:, None] * angular[None] * weight[None, None]  1.88 us
    ppermute x2, waiting for transfers between devices, halo(): from_right_y = lax.ppermute(rows[:, 0], 'gy', down_y)  1.56 us
    convert_element_type x4, other arithmetic, tile_terms(): tiles.astype(jnp.bfloat16)  1.39 us
    dot_general x2, matrix products, features(): return jnp.dot(embedding.T, onehot, precision=HIGHEST)  1.36 us
  transfers between devices with their start and end apart: 8, of which 3 were waited for; matrix products, arithmetic and copies ran while one was open for 6% of the time, Pallas kernels for 0%

profile of v6, /device:TPU:1, one launch (start us, length us, event | category | flops | bytes accessed | tf_op | source)
XLA Modules:
  0.0 60.4 jit_solution(10976933617195031655)
XLA Ops:
  0.6 0.7 %convert_bitcast_fusion = f32[2,1,128]{2,0,1:T(2,128)S(1)} fusion(s32[256]{0:T(256)} %param.10), kind=kLoop, calls=%fused_computation.510 | loop fusion | flops 256 | bytes 2048 | tf_op jit(solution)/shard_map/convert_element_type | solution.py:106
  1.4 0.7 %reshape.566 = f32[3,2,128]{2,1,0:T(2,128)S(1)} reshape(f32[3,256]{1,0:T(4,128)} %param.9) | data formatting | bytes 6144 | tf_op jit(solution)/shard_map/reshape | solution.py:105
  2.1 0.9 %fusion.241 = f32[8,2,4,128]{3,0,2,1:T(8,128)S(1)} fusion(f32[2,1,128]{2,0,1:T(2,128)S(1)} %convert_bitcast_fusion, f32[2,3,128]{2,0,1:T(2,128)S(1)} %bitcast.770, s32[8,2]{0,1:T(2,128)} %bitcast.798), kind=kOutput, calls=%fused_computation.488 | convolution fusion | flops 197664 | bytes 36928 | tf_op jit(solution)/shard_map/dgb,bra->dgra/dot_general | solution.py:110
  3.0 10.5 %collective-permute-start.1 = (f32[3,2,4,128]{3,0,2,1:T(4,128)S(1)}, f32[3,2,4,128]{3,0,2,1:T(4,128)S(1)}, u32[]{:S(2)}, u32[]{:S(2)}) collective-permute-start(f32[3,2,4,128]{3,0,2,1:T(4,128)S(1)} %get-tuple-element.57), channel_id=1, source_target_pairs={{96,0},{192,96},{288,192},{384,288},{480,384},{576,480},{672,576},... | collective-permute-start | bytes 36872 | tf_op jit(solution)/shard_map/ppermute | solution.py:81
  13.6 1.0 %multiply_bitcast_fusion = (f32[128,128]{1,0:T(8,128)S(1)}, f32[128,128]{1,0:T(8,128)S(1)}, f32[128,128]{1,0:T(8,128)S(1)}, f32[128,128]{1,0:T(8,128)S(1)}) fusion(s32[2,2,128,128]{3,2,1,0:T(8,128)} %param.12), kind=kLoop, calls=%fused_computation.412 | loop fusion | flops 131072 | bytes 524288 | tf_op jit(solution)/shard_map/jvp()/mul | solution.py:41
  14.5 0.7 %iota_compare_fusion = pred[2,2,18]{1,2,0:T(8,128)(4,1)S(1)} fusion(s32[2,2]{1,0:T(2,128)} %param.11), kind=kLoop, calls=%fused_computation.456 | loop fusion | flops 72 | bytes 88 | tf_op jit(solution)/shard_map/jvp()/eq | solution.py:68
  15.4 0.9 %convolution_bitcast_fusion.1 = f32[64,256]{1,0:T(8,128)S(1)} fusion(f32[4,64]{1,0:T(4,128)} %param.14, s32[256]{0:T(256)} %param.10), kind=kOutput, calls=%fused_computation.34 | convolution fusion | flops 787456 | bytes 67584 | tf_op jit(solution)/shard_map/dot_general | solution.py:117
  16.4 1.9 %collective-permute-start.2 = (f32[3,2,4,128]{3,2,1,0:T(4,128)S(1)}, f32[3,2,4,128]{3,2,1,0:T(4,128)S(1)}, u32[]{:S(2)}, u32[]{:S(2)}) collective-permute-start(f32[3,2,4,128]{3,2,1,0:T(4,128)S(1)} %get-tuple-element.55), channel_id=1, source_target_pairs={{0,1},{1,2},{2,3},{3,4},{4,5},{5,6},{6,7},{7,8},{8,9},{9,10},{10,1... | collective-permute-start | bytes 36872 | tf_op jit(solution)/shard_map/ppermute | solution.py:83
  18.6 9.3 %collective-permute-start.3 = (f32[3,2,4,128]{3,2,1,0:T(4,128)S(1)}, f32[3,2,4,128]{3,2,1,0:T(4,128)S(1)}, u32[]{:S(2)}, u32[]{:S(2)}) collective-permute-start(f32[3,2,4,128]{3,2,1,0:T(4,128)S(1)} %get-tuple-element.54), channel_id=1, source_target_pairs={{1,0},{2,1},{3,2},{4,3},{5,4},{6,5},{7,6},{8,7},{9,8},{10,9},{11,1... | collective-permute-start | bytes 36872 | tf_op jit(solution)/shard_map/ppermute | solution.py:84
  27.9 0.8 %collective-permute-done.3 = f32[3,2,4,128]{3,2,1,0:T(4,128)S(1)} collective-permute-done((f32[3,2,4,128]{3,2,1,0:T(4,128)S(1)}, f32[3,2,4,128]{3,2,1,0:T(4,128)S(1)}, u32[]{:S(2)}, u32[]{:S(2)}) %collective-permute-start.3) | collective-permute-done | bytes 12320 | tf_op jit(solution)/shard_map/ppermute | solution.py:84
  32.1 0.5 fusion.236
  33.0 0.5 fusion.237
  34.2 0.5 convolution_add_fusion.1
  35.1 0.5 convolution_add_fusion
  38.3 0.5 convolution_convert_fusion.2
  40.4 0.9 %fusion.2 = (f32[9,128,128]{2,1,0:T(8,128)S(1)}, f32[4,128,128]{2,1,0:T(8,128)S(1)}, f32[4,128,128]{2,1,0:T(8,128)S(1)}, f32[9,128,128]{2,1,0:T(8,128)S(1)}) fusion(bf16[4,9,128,128]{3,2,1,0:T(8,128)(2,1)S(1)} %bitcast.762, f32[128,128]{1,0:T(8,128)S(1)} %get-tuple-element.42, f32[4,128,128]{2,1,0:T(8,128)S(1)} %get-tuple-element.81, ...), kind=kLoop, calls=%fused_computation.3 | loop fusion | flops 6651904 | bytes 5898240 | tf_op jit(solution)/shard_map/transpose(jvp())/reduce_sum | solution.py:41
  41.5 0.9 %fusion.10 = (f32[9,128,128]{2,1,0:T(8,128)S(1)}, f32[4,128,128]{2,1,0:T(8,128)S(1)}, f32[4,128,128]{2,1,0:T(8,128)S(1)}, f32[9,128,128]{2,1,0:T(8,128)S(1)}) fusion(bf16[4,9,128,128]{3,2,1,0:T(8,128)(2,1)S(1)} %bitcast.760, f32[128,128]{1,0:T(8,128)S(1)} %get-tuple-element.43, f32[4,128,128]{2,1,0:T(8,128)S(1)} %get-tuple-element.83, ...), kind=kLoop, calls=%fused_computation.13 | loop fusion | flops 6651904 | bytes 5898240 | tf_op jit(solution)/shard_map/transpose(jvp())/reduce_sum | solution.py:41
  45.0 3.3 %collective-permute-start.5 = (f32[3,2,3,128]{3,1,2,0:T(2,128)S(1)}, f32[3,2,3,128]{3,1,2,0:T(2,128)S(1)}, u32[]{:S(2)}, u32[]{:S(2)}) collective-permute-start(f32[3,2,3,128]{3,1,2,0:T(2,128)S(1)} %copy.46), channel_id=1, source_target_pairs={{96,0},{192,96},{288,192},{384,288},{480,384},{576,480},{672,576},... | collective-permute-start | bytes 27656 | tf_op jit(solution)/shard_map/ppermute | solution.py:81
  48.4 0.6 maximum_bitcast_fusion.4
  49.0 0.7 %collective-permute-done.4 = f32[3,2,3,128]{3,1,2,0:T(2,128)S(1)} collective-permute-done((f32[3,2,3,128]{3,1,2,0:T(2,128)S(1)}, f32[3,2,3,128]{3,1,2,0:T(2,128)S(1)}, u32[]{:S(2)}, u32[]{:S(2)}) %collective-permute-start.4) | collective-permute-done | bytes 9248 | tf_op jit(solution)/shard_map/ppermute | solution.py:80
  49.7 1.9 %collective-permute-start.6 = (f32[3,2,3,128]{3,0,1,2:T(4,128)S(1)}, f32[3,2,3,128]{3,0,1,2:T(4,128)S(1)}, u32[]{:S(2)}, u32[]{:S(2)}) collective-permute-start(f32[3,2,3,128]{3,0,1,2:T(4,128)S(1)} %get-tuple-element.61), channel_id=1, source_target_pairs={{0,1},{1,2},{2,3},{3,4},{4,5},{5,6},{6,7},{7,8},{8,9},{9,10},{10,1... | collective-permute-start | bytes 27656 | tf_op jit(solution)/shard_map/ppermute | solution.py:83
  51.7 7.0 %collective-permute-start.7 = (f32[3,2,3,128]{3,0,1,2:T(4,128)S(1)}, f32[3,2,3,128]{3,0,1,2:T(4,128)S(1)}, u32[]{:S(2)}, u32[]{:S(2)}) collective-permute-start(f32[3,2,3,128]{3,0,1,2:T(4,128)S(1)} %get-tuple-element.60), channel_id=1, source_target_pairs={{1,0},{2,1},{3,2},{4,3},{5,4},{6,5},{7,6},{8,7},{9,8},{10,9},{11,1... | collective-permute-start | bytes 27656 | tf_op jit(solution)/shard_map/ppermute | solution.py:84
  58.8 0.8 %collective-permute-done.7 = f32[3,2,3,128]{3,0,1,2:T(4,128)S(1)} collective-permute-done((f32[3,2,3,128]{3,0,1,2:T(4,128)S(1)}, f32[3,2,3,128]{3,0,1,2:T(4,128)S(1)}, u32[]{:S(2)}, u32[]{:S(2)}) %collective-permute-start.7) | collective-permute-done | bytes 9248 | tf_op jit(solution)/shard_map/ppermute | solution.py:84
  59.8 0.6 copy.81
  (171 shorter events, 11.8 us)
Async XLA Ops:
  0.6 35.6 %copy-start = (f32[192,64]{0,1:T(8,128)S(1)}, f32[192,64]{0,1:T(8,128)}, u32[]{:S(2)}) copy-start(f32[192,64]{0,1:T(8,128)} %param.16) | copy-start | bytes 147460
  3.0 13.4 %collective-permute-start.1 = (f32[3,2,4,128]{3,0,2,1:T(4,128)S(1)}, f32[3,2,4,128]{3,0,2,1:T(4,128)S(1)}, u32[]{:S(2)}, u32[]{:S(2)}) collective-permute-start(f32[3,2,4,128]{3,0,2,1:T(4,128)S(1)} %get-tuple-element.57), channel_id=1, source_target_pairs={{96,0},{192,96},{288,192},{384,288},{480,384},{576,480},{672,576},... | collective-permute-start | bytes 36872 | tf_op jit(solution)/shard_map/ppermute | solution.py:81
  13.5 2.9 %collective-permute-start = (f32[3,2,4,128]{3,2,1,0:T(4,128)S(1)}, f32[3,2,4,128]{3,2,1,0:T(4,128)S(1)}, u32[]{:S(2)}, u32[]{:S(2)}) collective-permute-start(f32[3,2,4,128]{3,2,1,0:T(4,128)S(1)} %copy.65), channel_id=1, source_target_pairs={{0,96},{96,192},{192,288},{288,384},{384,480},{480,576},{576,672},... | collective-permute-start | bytes 36872 | tf_op jit(solution)/shard_map/ppermute | solution.py:80
  16.4 11.5 %collective-permute-start.2 = (f32[3,2,4,128]{3,2,1,0:T(4,128)S(1)}, f32[3,2,4,128]{3,2,1,0:T(4,128)S(1)}, u32[]{:S(2)}, u32[]{:S(2)}) collective-permute-start(f32[3,2,4,128]{3,2,1,0:T(4,128)S(1)} %get-tuple-element.55), channel_id=1, source_target_pairs={{0,1},{1,2},{2,3},{3,4},{4,5},{5,6},{6,7},{7,8},{8,9},{9,10},{10,1... | collective-permute-start | bytes 36872 | tf_op jit(solution)/shard_map/ppermute | solution.py:83
  18.6 10.1 %collective-permute-start.3 = (f32[3,2,4,128]{3,2,1,0:T(4,128)S(1)}, f32[3,2,4,128]{3,2,1,0:T(4,128)S(1)}, u32[]{:S(2)}, u32[]{:S(2)}) collective-permute-start(f32[3,2,4,128]{3,2,1,0:T(4,128)S(1)} %get-tuple-element.54), channel_id=1, source_target_pairs={{1,0},{2,1},{3,2},{4,3},{5,4},{6,5},{7,6},{8,7},{9,8},{10,9},{11,1... | collective-permute-start | bytes 36872 | tf_op jit(solution)/shard_map/ppermute | solution.py:84
  29.2 0.7 %copy-start.1 = (f32[4,64]{1,0:T(4,128)S(1)}, f32[4,64]{1,0:T(4,128)}, u32[]{:S(2)}) copy-start(f32[4,64]{1,0:T(4,128)} %param.14) | copy-start | bytes 3076
  35.1 0.7 %copy-start.2 = (f32[4,64]{1,0:T(4,128)S(1)}, f32[4,64]{1,0:T(4,128)}, u32[]{:S(2)}) copy-start(f32[4,64]{1,0:T(4,128)} %param.15) | copy-start | bytes 3076
  35.7 0.7 %copy-start.4 = (f32[64]{0:T(128)S(1)}, f32[64]{0:T(128)}, u32[]{:S(2)}) copy-start(f32[64]{0:T(128)} %param.17) | copy-start | bytes 772
  44.2 15.4 %copy-start.3 = (s32[1,1,8,2]{2,3,1,0:T(2,128)S(1)}, s32[1,1,8,2]{2,3,1,0:T(2,128)}, u32[]{:S(2)}) copy-start(s32[1,1,8,2]{2,3,1,0:T(2,128)} %param.13) | copy-start | bytes 196
  45.0 4.7 %collective-permute-start.5 = (f32[3,2,3,128]{3,1,2,0:T(2,128)S(1)}, f32[3,2,3,128]{3,1,2,0:T(2,128)S(1)}, u32[]{:S(2)}, u32[]{:S(2)}) collective-permute-start(f32[3,2,3,128]{3,1,2,0:T(2,128)S(1)} %copy.46), channel_id=1, source_target_pairs={{96,0},{192,96},{288,192},{384,288},{480,384},{576,480},{672,576},... | collective-permute-start | bytes 27656 | tf_op jit(solution)/shard_map/ppermute | solution.py:81
  48.3 1.4 %collective-permute-start.4 = (f32[3,2,3,128]{3,1,2,0:T(2,128)S(1)}, f32[3,2,3,128]{3,1,2,0:T(2,128)S(1)}, u32[]{:S(2)}, u32[]{:S(2)}) collective-permute-start(f32[3,2,3,128]{3,1,2,0:T(2,128)S(1)} %copy.40), channel_id=1, source_target_pairs={{0,96},{96,192},{192,288},{288,384},{384,480},{480,576},{576,672},... | collective-permute-start | bytes 27656 | tf_op jit(solution)/shard_map/ppermute | solution.py:80
  49.7 9.0 %collective-permute-start.6 = (f32[3,2,3,128]{3,0,1,2:T(4,128)S(1)}, f32[3,2,3,128]{3,0,1,2:T(4,128)S(1)}, u32[]{:S(2)}, u32[]{:S(2)}) collective-permute-start(f32[3,2,3,128]{3,0,1,2:T(4,128)S(1)} %get-tuple-element.61), channel_id=1, source_target_pairs={{0,1},{1,2},{2,3},{3,4},{4,5},{5,6},{6,7},{7,8},{8,9},{9,10},{10,1... | collective-permute-start | bytes 27656 | tf_op jit(solution)/shard_map/ppermute | solution.py:83
  51.7 7.9 %collective-permute-start.7 = (f32[3,2,3,128]{3,0,1,2:T(4,128)S(1)}, f32[3,2,3,128]{3,0,1,2:T(4,128)S(1)}, u32[]{:S(2)}, u32[]{:S(2)}) collective-permute-start(f32[3,2,3,128]{3,0,1,2:T(4,128)S(1)} %get-tuple-element.60), channel_id=1, source_target_pairs={{1,0},{2,1},{3,2},{4,3},{5,4},{6,5},{7,6},{8,7},{9,8},{10,9},{11,1... | collective-permute-start | bytes 27656 | tf_op jit(solution)/shard_map/ppermute | solution.py:84

commit v7 on v6

--- a/solution.py
+++ b/solution.py
@@ -77,12 +77,12 @@
     down_x = [((i + 1) % count_x, i) for i in range(count_x)]
     up_y = [(i, (i + 1) % count_y) for i in range(count_y)]
     down_y = [((i + 1) % count_y, i) for i in range(count_y)]
-    from_left_x = lax.ppermute(grid[2], "gx", up_x)
-    from_right_x = lax.ppermute(grid[0], "gx", down_x)
-    rows = jnp.stack([from_left_x, grid[1], from_right_x], axis=0)
-    from_left_y = lax.ppermute(rows[:, 2], "gy", up_y)
-    from_right_y = lax.ppermute(rows[:, 0], "gy", down_y)
-    return jnp.stack([from_left_y, rows[:, 1], from_right_y], axis=1)
+    from_left_y = lax.ppermute(grid[:, 2], "gy", up_y)
+    from_right_y = lax.ppermute(grid[:, 0], "gy", down_y)
+    columns = jnp.stack([from_left_y, grid[:, 1], from_right_y], axis=1)
+    from_left_x = lax.ppermute(columns[2], "gx", up_x)
+    from_right_x = lax.ppermute(columns[0], "gx", down_x)
+    return jnp.stack([from_left_x, columns[1], from_right_x], axis=0)
 
 
 def place(parts):

time: 61 us -> 68 us (1.11)
  waiting for transfers between devices: 2.25 us -> 15.1 us
  starting transfers between devices: 34.1 us -> 29.8 us
  matrix products: 8.15 us -> 7.45 us
    ppermute x8, waiting for transfers between devices: 2.25 us -> 15.1 us  [the longest x2 8.82 us: halo(): from_left_y = lax.ppermute(grid[:, 2], 'gy', up_y)]
    ppermute x8, starting transfers between devices: 34.1 us -> 29.8 us  [the longest x2 20 us: halo(): from_right_y = lax.ppermute(grid[:, 0], 'gy', down_y)]
    dot_general x2, matrix products: 1.36 us -> 0.67 us  [features(): return jnp.dot(embedding.T, onehot, precision=HIGHEST)]
    eq x1, other arithmetic: 0.69 us -> 0.01 us  [select_slots(): hit = chosen[..., None] == jnp.arange(slots, dtype=chosen.dtype)]
  transfers between devices with their start and end apart: 8 -> 8, of which waited for: 3 -> 6; matrix products, arithmetic and copies ran while one was open for 6% -> 3% of each run, Pallas kernels for 0% -> 0%
where the time goes in v7:
time: 68 us; the launch traced here: 67.4 us
  starting transfers between devices  29.8 us (44%)
  waiting for transfers between devices  15.1 us (22%)
  other arithmetic  11.1 us (16%)
  matrix products  7.45 us (11%)
  local copies, waits for them, and re-layouts  2.21 us (3%)
  between operations  1.71 us (3%)
    ppermute x2, starting transfers between devices, halo(): from_right_y = lax.ppermute(grid[:, 0], 'gy', down_y)  20 us
    ppermute x2, waiting for transfers between devices, halo(): from_left_y = lax.ppermute(grid[:, 2], 'gy', up_y)  8.82 us
    ppermute x2, waiting for transfers between devices, halo(): from_right_x = lax.ppermute(columns[0], 'gx', down_x)  5.56 us
    ppermute x2, starting transfers between devices, halo(): from_left_y = lax.ppermute(grid[:, 2], 'gy', up_y)  5.28 us
    ppermute x2, starting transfers between devices, halo(): from_left_x = lax.ppermute(columns[2], 'gx', up_x)  4.41 us
    dot_general x8, matrix products, tile_terms(): jnp.einsum('qij,cj->qic', tiles.astype(jnp.bfloat16), other_feat, preferr...  4.18 us
    reduce_sum x2, other arithmetic, tile_terms(): basis[:, None] * angular[None] * weight[None, None]  1.88 us
    convert_element_type x4, other arithmetic, tile_terms(): tiles.astype(jnp.bfloat16)  1.39 us
  transfers between devices with their start and end apart: 8, of which 6 were waited for; matrix products, arithmetic and copies ran while one was open for 3% of the time, Pallas kernels for 0%

profile of v7, /device:TPU:1, one launch (start us, length us, event | category | flops | bytes accessed | tf_op | source)
XLA Modules:
  0.0 67.4 jit_solution(8393524933467848674)
XLA Ops:
  0.7 0.7 %convert_bitcast_fusion = f32[2,1,128]{2,0,1:T(2,128)S(1)} fusion(s32[256]{0:T(256)} %param.10), kind=kLoop, calls=%fused_computation.515 | loop fusion | flops 256 | bytes 2048 | tf_op jit(solution)/shard_map/convert_element_type | solution.py:106
  1.4 0.7 %reshape.542 = f32[3,2,128]{2,1,0:T(2,128)S(1)} reshape(f32[3,256]{1,0:T(4,128)} %param.9) | data formatting | bytes 6144 | tf_op jit(solution)/shard_map/reshape | solution.py:105
  2.1 0.9 %fusion.240 = f32[8,2,4,128]{3,0,2,1:T(8,128)S(1)} fusion(f32[2,1,128]{2,0,1:T(2,128)S(1)} %convert_bitcast_fusion, f32[2,3,128]{2,0,1:T(2,128)S(1)} %bitcast.820, s32[8,2]{0,1:T(2,128)} %bitcast.855), kind=kOutput, calls=%fused_computation.495 | convolution fusion | flops 197664 | bytes 36928 | tf_op jit(solution)/shard_map/dgb,bra->dgra/dot_general | solution.py:110
  3.2 18.0 %collective-permute-start.1 = (f32[3,2,4,128]{3,2,1,0:T(4,128)S(1)}, f32[3,2,4,128]{3,2,1,0:T(4,128)S(1)}, u32[]{:S(2)}, u32[]{:S(2)}) collective-permute-start(f32[3,2,4,128]{3,2,1,0:T(4,128)S(1)} %get-tuple-element.55), channel_id=1, source_target_pairs={{1,0},{2,1},{3,2},{4,3},{5,4},{6,5},{7,6},{8,7},{9,8},{10,9},{11,1... | collective-permute-start | bytes 36872 | tf_op jit(solution)/shard_map/ppermute | solution.py:81
  21.2 1.9 %collective-permute-start = (f32[3,2,4,128]{3,2,1,0:T(4,128)S(1)}, f32[3,2,4,128]{3,2,1,0:T(4,128)S(1)}, u32[]{:S(2)}, u32[]{:S(2)}) collective-permute-start(f32[3,2,4,128]{3,2,1,0:T(4,128)S(1)} %get-tuple-element.54), channel_id=1, source_target_pairs={{0,1},{1,2},{2,3},{3,4},{4,5},{5,6},{6,7},{7,8},{8,9},{9,10},{10,1... | collective-permute-start | bytes 36872 | tf_op jit(solution)/shard_map/ppermute | solution.py:80
  23.2 1.0 %multiply_bitcast_fusion = (f32[128,128]{1,0:T(8,128)S(1)}, f32[128,128]{1,0:T(8,128)S(1)}, f32[128,128]{1,0:T(8,128)S(1)}, f32[128,128]{1,0:T(8,128)S(1)}) fusion(s32[2,2,128,128]{3,2,1,0:T(8,128)} %param.12), kind=kLoop, calls=%fused_computation.413 | loop fusion | flops 131072 | bytes 524288 | tf_op jit(solution)/shard_map/jvp()/mul | solution.py:41
  24.5 4.5 %collective-permute-done = f32[3,2,4,128]{3,2,1,0:T(4,128)S(1)} collective-permute-done((f32[3,2,4,128]{3,2,1,0:T(4,128)S(1)}, f32[3,2,4,128]{3,2,1,0:T(4,128)S(1)}, u32[]{:S(2)}, u32[]{:S(2)}) %collective-permute-start) | collective-permute-done | bytes 12320 | tf_op jit(solution)/shard_map/ppermute | solution.py:80
  29.0 3.2 %collective-permute-start.2 = (f32[3,2,4,128]{3,2,1,0:T(4,128)S(1)}, f32[3,2,4,128]{3,2,1,0:T(4,128)S(1)}, u32[]{:S(2)}, u32[]{:S(2)}) collective-permute-start(f32[3,2,4,128]{3,2,1,0:T(4,128)S(1)} %get-tuple-element.53), channel_id=1, source_target_pairs={{0,96},{96,192},{192,288},{288,384},{384,480},{480,576},{576,672},... | collective-permute-start | bytes 36872 | tf_op jit(solution)/shard_map/ppermute | solution.py:83
  32.4 0.7 collective-permute-done.2
  33.1 2.4 %collective-permute-done.3 = f32[3,2,4,128]{3,2,1,0:T(4,128)S(1)} collective-permute-done((f32[3,2,4,128]{3,2,1,0:T(4,128)S(1)}, f32[3,2,4,128]{3,2,1,0:T(4,128)S(1)}, u32[]{:S(2)}, u32[]{:S(2)}) %collective-permute-start.3) | collective-permute-done | bytes 12320 | tf_op jit(solution)/shard_map/ppermute | solution.py:84
  38.7 0.5 fusion.236
  39.6 0.5 fusion.237
  40.8 0.5 convolution_add_fusion.1
  41.7 0.5 convolution_add_fusion
  44.9 0.5 convolution_convert_fusion.2
  47.0 0.9 %fusion.2 = (f32[9,128,128]{2,1,0:T(8,128)S(1)}, f32[4,128,128]{2,1,0:T(8,128)S(1)}, f32[4,128,128]{2,1,0:T(8,128)S(1)}, f32[9,128,128]{2,1,0:T(8,128)S(1)}) fusion(bf16[4,9,128,128]{3,2,1,0:T(8,128)(2,1)S(1)} %bitcast.810, f32[128,128]{1,0:T(8,128)S(1)} %get-tuple-element.42, f32[4,128,128]{2,1,0:T(8,128)S(1)} %get-tuple-element.83, ...), kind=kLoop, calls=%fused_computation.3 | loop fusion | flops 6651904 | bytes 5898240 | tf_op jit(solution)/shard_map/transpose(jvp())/reduce_sum | solution.py:41
  48.1 0.9 %fusion.10 = (f32[9,128,128]{2,1,0:T(8,128)S(1)}, f32[4,128,128]{2,1,0:T(8,128)S(1)}, f32[4,128,128]{2,1,0:T(8,128)S(1)}, f32[9,128,128]{2,1,0:T(8,128)S(1)}) fusion(bf16[4,9,128,128]{3,2,1,0:T(8,128)(2,1)S(1)} %bitcast.808, f32[128,128]{1,0:T(8,128)S(1)} %get-tuple-element.43, f32[4,128,128]{2,1,0:T(8,128)S(1)} %get-tuple-element.85, ...), kind=kLoop, calls=%fused_computation.13 | loop fusion | flops 6651904 | bytes 5898240 | tf_op jit(solution)/shard_map/transpose(jvp())/reduce_sum | solution.py:41
  51.7 1.9 %collective-permute-start.5 = (f32[3,2,3,128]{3,1,2,0:T(2,128)S(1)}, f32[3,2,3,128]{3,1,2,0:T(2,128)S(1)}, u32[]{:S(2)}, u32[]{:S(2)}) collective-permute-start(f32[3,2,3,128]{3,1,2,0:T(2,128)S(1)} %get-tuple-element.63), channel_id=1, source_target_pairs={{1,0},{2,1},{3,2},{4,3},{5,4},{6,5},{7,6},{8,7},{9,8},{10,9},{11,1... | collective-permute-start | bytes 27656 | tf_op jit(solution)/shard_map/ppermute | solution.py:81
  53.6 3.4 %collective-permute-start.4 = (f32[3,2,3,128]{3,1,2,0:T(2,128)S(1)}, f32[3,2,3,128]{3,1,2,0:T(2,128)S(1)}, u32[]{:S(2)}, u32[]{:S(2)}) collective-permute-start(f32[3,2,3,128]{3,1,2,0:T(2,128)S(1)} %get-tuple-element.61), channel_id=1, source_target_pairs={{0,1},{1,2},{2,3},{3,4},{4,5},{5,6},{6,7},{7,8},{8,9},{9,10},{10,1... | collective-permute-start | bytes 27656 | tf_op jit(solution)/shard_map/ppermute | solution.py:80
  57.0 4.3 %collective-permute-done.4 = f32[3,2,3,128]{3,1,2,0:T(2,128)S(1)} collective-permute-done((f32[3,2,3,128]{3,1,2,0:T(2,128)S(1)}, f32[3,2,3,128]{3,1,2,0:T(2,128)S(1)}, u32[]{:S(2)}, u32[]{:S(2)}) %collective-permute-start.4) | collective-permute-done | bytes 9248 | tf_op jit(solution)/shard_map/ppermute | solution.py:80
  61.3 1.2 %collective-permute-start.6 = (f32[3,2,3,128]{3,1,2,0:T(2,128)S(1)}, f32[3,2,3,128]{3,1,2,0:T(2,128)S(1)}, u32[]{:S(2)}, u32[]{:S(2)}) collective-permute-start(f32[3,2,3,128]{3,1,2,0:T(2,128)S(1)} %get-tuple-element.60), channel_id=1, source_target_pairs={{0,96},{96,192},{192,288},{288,384},{384,480},{480,576},{576,672},... | collective-permute-start | bytes 27656 | tf_op jit(solution)/shard_map/ppermute | solution.py:83
  62.5 0.6 maximum_bitcast_fusion.4
  63.4 3.2 %collective-permute-done.7 = f32[3,2,3,128]{3,1,2,0:T(2,128)S(1)} collective-permute-done((f32[3,2,3,128]{3,1,2,0:T(2,128)S(1)}, f32[3,2,3,128]{3,1,2,0:T(2,128)S(1)}, u32[]{:S(2)}, u32[]{:S(2)}) %collective-permute-start.7) | collective-permute-done | bytes 9248 | tf_op jit(solution)/shard_map/ppermute | solution.py:84
  66.8 0.6 copy.92
  (170 shorter events, 12.0 us)
Async XLA Ops:
  0.6 42.2 %copy-start = (f32[192,64]{0,1:T(8,128)S(1)}, f32[192,64]{0,1:T(8,128)}, u32[]{:S(2)}) copy-start(f32[192,64]{0,1:T(8,128)} %param.16) | copy-start | bytes 147460
  0.6 23.6 %copy-start.3 = (s32[256]{0:T(256)S(1)}, s32[256]{0:T(256)}, u32[]{:S(2)}) copy-start(s32[256]{0:T(256)} %param.10) | copy-start | bytes 3076
  0.7 23.5 %copy-start.6 = (s32[2,2]{1,0:T(2,128)S(1)}, s32[2,2]{1,0:T(2,128)}, u32[]{:S(2)}) copy-start(s32[2,2]{1,0:T(2,128)} %param.11) | copy-start | bytes 52
  0.7 23.6 %copy-start.1 = (f32[4,64]{1,0:T(4,128)S(1)}, f32[4,64]{1,0:T(4,128)}, u32[]{:S(2)}) copy-start(f32[4,64]{1,0:T(4,128)} %param.14) | copy-start | bytes 3076
  3.2 21.3 %collective-permute-start.1 = (f32[3,2,4,128]{3,2,1,0:T(4,128)S(1)}, f32[3,2,4,128]{3,2,1,0:T(4,128)S(1)}, u32[]{:S(2)}, u32[]{:S(2)}) collective-permute-start(f32[3,2,4,128]{3,2,1,0:T(4,128)S(1)} %get-tuple-element.55), channel_id=1, source_target_pairs={{1,0},{2,1},{3,2},{4,3},{5,4},{6,5},{7,6},{8,7},{9,8},{10,9},{11,1... | collective-permute-start | bytes 36872 | tf_op jit(solution)/shard_map/ppermute | solution.py:81
  21.2 7.8 %collective-permute-start = (f32[3,2,4,128]{3,2,1,0:T(4,128)S(1)}, f32[3,2,4,128]{3,2,1,0:T(4,128)S(1)}, u32[]{:S(2)}, u32[]{:S(2)}) collective-permute-start(f32[3,2,4,128]{3,2,1,0:T(4,128)S(1)} %get-tuple-element.54), channel_id=1, source_target_pairs={{0,1},{1,2},{2,3},{3,4},{4,5},{5,6},{6,7},{7,8},{8,9},{9,10},{10,1... | collective-permute-start | bytes 36872 | tf_op jit(solution)/shard_map/ppermute | solution.py:80
  29.0 4.0 %collective-permute-start.2 = (f32[3,2,4,128]{3,2,1,0:T(4,128)S(1)}, f32[3,2,4,128]{3,2,1,0:T(4,128)S(1)}, u32[]{:S(2)}, u32[]{:S(2)}) collective-permute-start(f32[3,2,4,128]{3,2,1,0:T(4,128)S(1)} %get-tuple-element.53), channel_id=1, source_target_pairs={{0,96},{96,192},{192,288},{288,384},{384,480},{480,576},{576,672},... | collective-permute-start | bytes 36872 | tf_op jit(solution)/shard_map/ppermute | solution.py:83
  32.4 3.1 %collective-permute-start.3 = (f32[3,2,4,128]{3,2,1,0:T(4,128)S(1)}, f32[3,2,4,128]{3,2,1,0:T(4,128)S(1)}, u32[]{:S(2)}, u32[]{:S(2)}) collective-permute-start(f32[3,2,4,128]{3,2,1,0:T(4,128)S(1)} %get-tuple-element.52), channel_id=1, source_target_pairs={{96,0},{192,96},{288,192},{384,288},{480,384},{576,480},{672,576},... | collective-permute-start | bytes 36872 | tf_op jit(solution)/shard_map/ppermute | solution.py:84
  41.7 0.7 %copy-start.2 = (f32[4,64]{1,0:T(4,128)S(1)}, f32[4,64]{1,0:T(4,128)}, u32[]{:S(2)}) copy-start(f32[4,64]{1,0:T(4,128)} %param.15) | copy-start | bytes 3076
  42.4 0.7 %copy-start.5 = (f32[64]{0:T(128)S(1)}, f32[64]{0:T(128)}, u32[]{:S(2)}) copy-start(f32[64]{0:T(128)} %param.17) | copy-start | bytes 772
  50.8 15.7 %copy-start.4 = (s32[1,1,8,2]{2,3,1,0:T(2,128)S(1)}, s32[1,1,8,2]{2,3,1,0:T(2,128)}, u32[]{:S(2)}) copy-start(s32[1,1,8,2]{2,3,1,0:T(2,128)} %param.13) | copy-start | bytes 196
  51.7 5.3 %collective-permute-start.5 = (f32[3,2,3,128]{3,1,2,0:T(2,128)S(1)}, f32[3,2,3,128]{3,1,2,0:T(2,128)S(1)}, u32[]{:S(2)}, u32[]{:S(2)}) collective-permute-start(f32[3,2,3,128]{3,1,2,0:T(2,128)S(1)} %get-tuple-element.63), channel_id=1, source_target_pairs={{1,0},{2,1},{3,2},{4,3},{5,4},{6,5},{7,6},{8,7},{9,8},{10,9},{11,1... | collective-permute-start | bytes 27656 | tf_op jit(solution)/shard_map/ppermute | solution.py:81
  53.6 7.7 %collective-permute-start.4 = (f32[3,2,3,128]{3,1,2,0:T(2,128)S(1)}, f32[3,2,3,128]{3,1,2,0:T(2,128)S(1)}, u32[]{:S(2)}, u32[]{:S(2)}) collective-permute-start(f32[3,2,3,128]{3,1,2,0:T(2,128)S(1)} %get-tuple-element.61), channel_id=1, source_target_pairs={{0,1},{1,2},{2,3},{3,4},{4,5},{5,6},{6,7},{7,8},{8,9},{9,10},{10,1... | collective-permute-start | bytes 27656 | tf_op jit(solution)/shard_map/ppermute | solution.py:80
  61.3 2.0 %collective-permute-start.6 = (f32[3,2,3,128]{3,1,2,0:T(2,128)S(1)}, f32[3,2,3,128]{3,1,2,0:T(2,128)S(1)}, u32[]{:S(2)}, u32[]{:S(2)}) collective-permute-start(f32[3,2,3,128]{3,1,2,0:T(2,128)S(1)} %get-tuple-element.60), channel_id=1, source_target_pairs={{0,96},{96,192},{192,288},{288,384},{384,480},{480,576},{576,672},... | collective-permute-start | bytes 27656 | tf_op jit(solution)/shard_map/ppermute | solution.py:83
  63.1 3.4 %collective-permute-start.7 = (f32[3,2,3,128]{3,1,2,0:T(2,128)S(1)}, f32[3,2,3,128]{3,1,2,0:T(2,128)S(1)}, u32[]{:S(2)}, u32[]{:S(2)}) collective-permute-start(f32[3,2,3,128]{3,1,2,0:T(2,128)S(1)} %get-tuple-element.59), channel_id=1, source_target_pairs={{96,0},{192,96},{288,192},{384,288},{480,384},{576,480},{672,576},... | collective-permute-start | bytes 27656 | tf_op jit(solution)/shard_map/ppermute | solution.py:84

commit v8 on v4

--- a/solution.py
+++ b/solution.py
@@ -1,8 +1,10 @@
 import math
+from functools import partial
 
 import jax
 import jax.numpy as jnp
 from jax import lax
+from jax.experimental import pallas as pl
 from jax.sharding import PartitionSpec as P
 
 OFFSETS = ((-1, -1), (-1, 0), (-1, 1), (0, -1), (0, 1), (1, -1), (1, 0), (1, 1))
@@ -29,21 +31,99 @@
     )
 
 
-def block_energies(own_pos, others_pos, others_feat, masks, radial, readin, readout):
+def pair_kernel(own_ref, other_ref, weight_ref, feat_ref, out_ref):
+    slot = pl.program_id(1)
+    count = out_ref.shape[1] // 9
+    rel = [other_ref[0, 0, d : d + 1, :] - own_ref[0, :, d : d + 1] for d in range(3)]
+    dist = jnp.sqrt((rel[0] * rel[0] + rel[1] * rel[1] + rel[2] * rel[2]) + 0.25)
+    angular = harmonics(rel, dist)
+    weight = weight_ref[0, 0]
+    feat = feat_ref[0, 0]
+    for k in range(count):
+        offset = dist - (0.5 + k)
+        basis = jnp.exp(-0.5 * offset * offset)
+        for m in range(9):
+            tile = ((basis * angular[m]) * weight).astype(jnp.bfloat16)
+            part = lax.dot_general(
+                feat, tile, (((1,), (1,)), ((), ())), preferred_element_type=jnp.float32
+            )
+            q = k * 9 + m
+
+            @pl.when(slot == 0)
+            def _():
+                out_ref[0, q] = part
+
+            @pl.when(slot > 0)
+            def _():
+                out_ref[0, q] = out_ref[0, q] + part
+
+
+def fused_proj(own_pos, others_pos, others_feat, weights, count):
+    blocks, atoms = own_pos.shape[0], own_pos.shape[2]
+    listed, width = others_pos.shape[1], others_feat.shape[2]
+    return pl.pallas_call(
+        pair_kernel,
+        grid=(blocks, listed),
+        in_specs=[
+            pl.BlockSpec((1, atoms, 3), lambda b, n: (b, 0, 0)),
+            pl.BlockSpec((1, 1, 3, atoms), lambda b, n: (b, n, 0, 0)),
+            pl.BlockSpec((1, 1, atoms, atoms), lambda b, n: (b, n, 0, 0)),
+            pl.BlockSpec((1, 1, width, atoms), lambda b, n: (b, n, 0, 0)),
+        ],
+        out_specs=pl.BlockSpec((1, count * 9, width, atoms), lambda b, n: (b, 0, 0, 0)),
+        out_shape=jax.ShapeDtypeStruct((blocks, count * 9, width, atoms), jnp.float32),
+    )(jnp.swapaxes(own_pos, 1, 2), others_pos, weights, others_feat)
+
+
+def plain_proj(own_pos, others_pos, others_feat, weights, count):
+    centres = 0.5 + jnp.arange(count).astype(jnp.float32)
+    atoms = own_pos.shape[2]
+    result = []
+    for block in range(own_pos.shape[0]):
+        total = 0.0
+        for slot in range(others_pos.shape[1]):
+            rel = others_pos[block, slot][:, None, :] - own_pos[block][:, :, None]
+            dist = jnp.sqrt(jnp.sum(rel * rel, axis=0) + 0.25)
+            offset = dist[None] - centres[:, None, None]
+            basis = jnp.exp(-0.5 * offset * offset)
+            angular = harmonics(rel, dist)
+            tiles = basis[:, None] * angular[None] * weights[block, slot][None, None]
+            tiles = tiles.reshape(count * 9, atoms, atoms).astype(jnp.bfloat16)
+            total = total + jnp.einsum(
+                "qij,cj->qci", tiles, others_feat[block, slot], preferred_element_type=jnp.float32
+            )
+        result.append(total)
+    return jnp.stack(result)
+
+
+@partial(jax.custom_vjp, nondiff_argnums=(4,))
+def pair_proj(own_pos, others_pos, others_feat, weights, count):
+    return fused_proj(own_pos, others_pos, others_feat, weights, count)
+
+
+def pair_proj_fwd(own_pos, others_pos, others_feat, weights, count):
+    return pair_proj(own_pos, others_pos, others_feat, weights, count), (
+        own_pos,
+        others_pos,
+        others_feat,
+        weights,
+    )
+
+
+def pair_proj_bwd(count, saved, grad):
+    own_pos, others_pos, others_feat, weights = saved
+    _, pullback = jax.vjp(
+        lambda a, b: plain_proj(a, b, others_feat, weights, count), own_pos, others_pos
+    )
+    grad_own, grad_others = pullback(grad)
+    return grad_own, grad_others, jnp.zeros_like(others_feat), jnp.zeros_like(weights)
+
+
+pair_proj.defvjp(pair_proj_fwd, pair_proj_bwd)
+
+
+def block_energies(proj, radial, readin, readout):
     count = radial.shape[0]
-    atoms = own_pos.shape[2]
-    listed = others_pos.shape[1]
-    centres = 0.5 + jnp.arange(count).astype(jnp.float32)
-    rel = others_pos[:, :, :, None, :] - own_pos[:, None, :, :, None]
-    dist = jnp.sqrt(jnp.sum(rel * rel, axis=2) + 0.25)
-    offset = dist[:, :, None] - centres[:, None, None]
-    basis = jnp.exp(-0.5 * offset * offset)
-    angular = harmonics(jnp.moveaxis(rel, 2, 0), dist)
-    angular = jnp.moveaxis(angular, 0, 2)
-    weight = masks.astype(jnp.float32) * (1.0 / math.sqrt(listed * atoms))
-    tiles = basis[:, :, :, None] * angular[:, :, None] * weight[:, :, None, None]
-    tiles = tiles.reshape(tiles.shape[:2] + (count * 9, atoms, atoms)).astype(jnp.bfloat16)
-    proj = jnp.einsum("bnqij,bncj->bqci", tiles, others_feat, preferred_element_type=jnp.float32)
     proj = proj.reshape((proj.shape[0], count, 9) + proj.shape[2:])
     message = jnp.sum(radial[None, :, None, :, None] * proj, axis=1)
     first = jnp.sum(message[:, 1:4] * message[:, 1:4], axis=1)
@@ -111,14 +191,16 @@
         features(ghost_kind.reshape(-1)).reshape(-1, 8 * sends, atoms).transpose(1, 0, 2)
     )
 
+    listed = neighbours.shape[1]
+    weights = pair_masks.astype(jnp.float32) * (1.0 / math.sqrt(listed * atoms))
+
     def energies_of(own_now, ghost_now):
         table_pos = jnp.concatenate([own_now, ghost_now], axis=0)
         table_feat = jnp.concatenate([own_feats32, ghost_feats32], axis=0)
         others_pos = select_slots(table_pos, neighbours)
         others_feat = select_slots(table_feat, neighbours).astype(jnp.bfloat16)
-        return block_energies(
-            own_now, others_pos, others_feat, pair_masks, radial, readin, readout
-        )
+        proj = pair_proj(own_now, others_pos, others_feat, weights, radial.shape[0])
+        return block_energies(proj, radial, readin, readout)
 
     energy, pullback = jax.vjp(energies_of, own_pos, ghost_pos)
     grad_own, grad_ghost = pullback(jnp.ones_like(energy))

time: 72.8 us -> 88.9 us (1.22)
  the two profiles are of different devices: /device:TPU:1 before, /device:TPU:7 now
where the time goes in v8:
time: 88.9 us; the launch traced here: 88.4 us
  starting transfers between devices  33.4 us (38%)
  Pallas kernels  25.6 us (29%)
  other arithmetic  12.2 us (14%)
  matrix products  5.97 us (7%)
  waiting for transfers between devices  5.76 us (6%)
  local copies, waits for them, and re-layouts  3.78 us (4%)
  between operations  1.7 us (2%)
    pallas_call x1, Pallas kernels, fused_proj(): pl.pallas_call(pair_kernel, grid=(blocks, listed), in_specs=[pl.BlockSpec...  25.6 us
    ppermute x2, starting transfers between devices, halo(): from_right_y = lax.ppermute(rows[:, 0], 'gy', down_y)  17.6 us
    ppermute x2, starting transfers between devices, halo(): from_left_x = lax.ppermute(grid[2], 'gx', up_x)  11.3 us
    ppermute x2, starting transfers between devices, halo(): from_left_y = lax.ppermute(rows[:, 2], 'gy', up_y)  3.84 us
    ppermute x2, waiting for transfers between devices, halo(): from_right_x = lax.ppermute(grid[0], 'gx', down_x)  3.59 us
    reduce_sum x7, other arithmetic, energies_of(): proj = pair_proj(own_now, others_pos, others_feat, weights, radial.shape[0])  3.16 us
    reduce_sum x1, other arithmetic, block_energies(): message = jnp.sum(radial[None, :, None, :, None] * proj, axis=1)  2.11 us
    dot_general x4, matrix products, energies_of(): proj = pair_proj(own_now, others_pos, others_feat, weights, radial.shape[0])  2.07 us
  transfers between devices with their start and end apart: 8, of which 4 were waited for; matrix products, arithmetic and copies ran while one was open for 4% of the time, Pallas kernels for 0%

profile of v8, /device:TPU:7, one launch (start us, length us, event | category | flops | bytes accessed | tf_op | source)
XLA Modules:
  0.0 88.4 jit_solution(17129875405411907978)
XLA Ops:
  0.7 0.9 copy.64
  1.5 0.7 convert_bitcast_fusion
  2.6 0.9 %fusion.225 = f32[8,2,4,128]{3,0,2,1:T(8,128)S(1)} fusion(f32[2,4,128]{2,0,1:T(2,128)S(1)} %copy.66, s32[8,2]{0,1:T(2,128)} %bitcast.789), kind=kOutput, calls=%fused_computation.464 | convolution fusion | flops 196640 | bytes 36928 | tf_op jit(solution)/shard_map/dgb,bra->dgra/dot_general | solution.py:180
  3.5 0.7 collective-permute-start.1
  4.2 9.1 %collective-permute-start = (f32[3,2,4,128]{3,2,1,0:T(4,128)S(1)}, f32[3,2,4,128]{3,2,1,0:T(4,128)S(1)}, u32[]{:S(2)}, u32[]{:S(2)}) collective-permute-start(f32[3,2,4,128]{3,2,1,0:T(4,128)S(1)} %copy.107), channel_id=1, source_target_pairs={{0,96},{96,192},{192,288},{288,384},{384,480},{480,576},{576,672},... | collective-permute-start | bytes 36872 | tf_op jit(solution)/shard_map/ppermute | solution.py:150
  13.4 0.7 iota_compare_fusion
  14.2 1.0 %convert_multiply_fusion.4.weight_ref = f32[2,2,128,128]{3,2,1,0:T(8,128)S(1)} fusion(s32[2,2,128,128]{3,2,1,0:T(8,128)} %param.12), kind=kLoop, calls=%fused_computation.75 | loop fusion | flops 131072 | bytes 524288 | tf_op jit(solution)/shard_map/mul | solution.py:195
  15.2 1.0 %convolution_bitcast_fusion.2 = f32[64,256]{1,0:T(8,128)S(1)} fusion(f32[4,64]{1,0:T(4,128)} %param.14, s32[256]{0:T(256)} %param.10), kind=kOutput, calls=%fused_computation.29 | convolution fusion | flops 787456 | bytes 67584 | tf_op jit(solution)/shard_map/dot_general | solution.py:187
  16.4 1.9 %collective-permute-start.2 = (f32[3,2,4,128]{3,2,1,0:T(4,128)S(1)}, f32[3,2,4,128]{3,2,1,0:T(4,128)S(1)}, u32[]{:S(2)}, u32[]{:S(2)}) collective-permute-start(f32[3,2,4,128]{3,2,1,0:T(4,128)S(1)} %get-tuple-element.54), channel_id=1, source_target_pairs={{0,1},{1,2},{2,3},{3,4},{4,5},{5,6},{6,7},{7,8},{8,9},{9,10},{10,1... | collective-permute-start | bytes 36872 | tf_op jit(solution)/shard_map/ppermute | solution.py:153
  18.7 10.4 %collective-permute-start.3 = (f32[3,2,4,128]{3,2,1,0:T(4,128)S(1)}, f32[3,2,4,128]{3,2,1,0:T(4,128)S(1)}, u32[]{:S(2)}, u32[]{:S(2)}) collective-permute-start(f32[3,2,4,128]{3,2,1,0:T(4,128)S(1)} %get-tuple-element.53), channel_id=1, source_target_pairs={{1,0},{2,1},{3,2},{4,3},{5,4},{6,5},{7,6},{8,7},{9,8},{10,9},{11,1... | collective-permute-start | bytes 36872 | tf_op jit(solution)/shard_map/ppermute | solution.py:154
  29.1 0.8 collective-permute-done.3
  31.5 0.8 select_reduce_fusion.feat_ref
  32.3 25.6 %jvp__.1 = f32[2,36,64,128]{3,2,1,0:T(8,128)} custom-call(f32[2,128,3]{2,1,0:T(8,128)} %bitcast.761, f32[2,2,3,128]{3,2,1,0:T(4,128)} %copy.74.other_ref, f32[2,2,128,128]{3,2,1,0:T(8,128)} %copy-done.2, bf16[2,2,64,128]{3,2,1,0:T(8,128)(2,1)} %select_reduce_fusion.feat_ref), custom_call_target="tpu_custom_call" | custom-call | tf_op jit(solution)/shard_map/jvp()/pallas_call | solution.py:64
  57.9 2.1 %multiply_reduce_fusion = f32[2,9,64,128]{3,2,1,0:T(8,128)S(1)} fusion(f32[2,4,9,64,128]{4,3,2,1,0:T(8,128)} %bitcast.741, f32[4,64]{1,0:T(4,128)S(1)} %copy-done.5), kind=kLoop, calls=%fused_computation.20 | loop fusion | flops 1032192 | bytes 2950144 | tf_op jit(solution)/shard_map/jvp()/reduce_sum | solution.py:128
  60.4 0.7 fusion.207
  66.5 0.9 %fusion.2 = (f32[9,128,128]{2,1,0:T(8,128)S(1)}, f32[4,128,128]{2,1,0:T(8,128)S(1)}, f32[4,128,128]{2,1,0:T(8,128)S(1)}, f32[9,128,128]{2,1,0:T(8,128)S(1)}) fusion(bf16[4,9,128,128]{3,2,1,0:T(8,128)(2,1)S(1)} %bitcast.756, f32[128,128]{1,0:T(8,128)S(1)} %get-tuple-element.40, f32[4,128,128]{2,1,0:T(8,128)S(1)} %get-tuple-element.75, ...), kind=kLoop, calls=%fused_computation.3 | loop fusion | flops 6651904 | bytes 5898240 | tf_op jit(solution)/shard_map/transpose(jvp(transpose(jvp())))/reduce_sum | solution.py:202
  67.6 0.9 %fusion.10 = (f32[9,128,128]{2,1,0:T(8,128)S(1)}, f32[4,128,128]{2,1,0:T(8,128)S(1)}, f32[4,128,128]{2,1,0:T(8,128)S(1)}, f32[9,128,128]{2,1,0:T(8,128)S(1)}) fusion(bf16[4,9,128,128]{3,2,1,0:T(8,128)(2,1)S(1)} %bitcast.754, f32[128,128]{1,0:T(8,128)S(1)} %get-tuple-element.42, f32[4,128,128]{2,1,0:T(8,128)S(1)} %get-tuple-element.77, ...), kind=kLoop, calls=%fused_computation.13 | loop fusion | flops 6651904 | bytes 5898240 | tf_op jit(solution)/shard_map/transpose(jvp(transpose(jvp())))/reduce_sum | solution.py:202
  71.0 2.1 %collective-permute-start.4 = (f32[3,2,3,128]{3,1,2,0:T(2,128)S(1)}, f32[3,2,3,128]{3,1,2,0:T(2,128)S(1)}, u32[]{:S(2)}, u32[]{:S(2)}) collective-permute-start(f32[3,2,3,128]{3,1,2,0:T(2,128)S(1)} %copy.83), channel_id=1, source_target_pairs={{0,96},{96,192},{192,288},{288,384},{384,480},{480,576},{576,672},... | collective-permute-start | bytes 27656 | tf_op jit(solution)/shard_map/ppermute | solution.py:150
  73.3 0.6 collective-permute-done.4
  73.9 3.6 %collective-permute-done.5 = f32[3,2,3,128]{3,1,2,0:T(2,128)S(1)} collective-permute-done((f32[3,2,3,128]{3,1,2,0:T(2,128)S(1)}, f32[3,2,3,128]{3,1,2,0:T(2,128)S(1)}, u32[]{:S(2)}, u32[]{:S(2)}) %collective-permute-start.5) | collective-permute-done | bytes 9248 | tf_op jit(solution)/shard_map/ppermute | solution.py:151
  77.5 1.9 %collective-permute-start.6 = (f32[3,2,3,128]{3,0,1,2:T(4,128)S(1)}, f32[3,2,3,128]{3,0,1,2:T(4,128)S(1)}, u32[]{:S(2)}, u32[]{:S(2)}) collective-permute-start(f32[3,2,3,128]{3,0,1,2:T(4,128)S(1)} %get-tuple-element.60), channel_id=1, source_target_pairs={{0,1},{1,2},{2,3},{3,4},{4,5},{5,6},{6,7},{7,8},{8,9},{9,10},{10,1... | collective-permute-start | bytes 27656 | tf_op jit(solution)/shard_map/ppermute | solution.py:153
  79.5 7.2 %collective-permute-start.7 = (f32[3,2,3,128]{3,0,1,2:T(4,128)S(1)}, f32[3,2,3,128]{3,0,1,2:T(4,128)S(1)}, u32[]{:S(2)}, u32[]{:S(2)}) collective-permute-start(f32[3,2,3,128]{3,0,1,2:T(4,128)S(1)} %get-tuple-element.59), channel_id=1, source_target_pairs={{1,0},{2,1},{3,2},{4,3},{5,4},{6,5},{7,6},{8,7},{9,8},{10,9},{11,1... | collective-permute-start | bytes 27656 | tf_op jit(solution)/shard_map/ppermute | solution.py:154
  86.8 0.8 collective-permute-done.7
  87.8 0.6 copy.130
  (166 shorter events, 10.7 us)
Async XLA Ops:
  0.6 59.5 %copy-start = (f32[192,64]{0,1:T(8,128)S(1)}, f32[192,64]{0,1:T(8,128)}, u32[]{:S(2)}) copy-start(f32[192,64]{0,1:T(8,128)} %param.16) | copy-start | bytes 147460
  0.6 30.0 %copy-start.4 = (f32[4,64]{1,0:T(4,128)S(1)}, f32[4,64]{1,0:T(4,128)}, u32[]{:S(2)}) copy-start(f32[4,64]{1,0:T(4,128)} %param.14) | copy-start | bytes 3076
  1.5 29.7 %copy-start.1 = (f32[3,256]{0,1:T(8,128)}, f32[3,256]{0,1:T(8,128)S(1)}, u32[]{:S(2)}) copy-start(f32[3,256]{0,1:T(8,128)S(1)} %copy.64) | copy-start | bytes 9220
  3.5 12.8 %collective-permute-start.1 = (f32[3,2,4,128]{3,0,2,1:T(4,128)S(1)}, f32[3,2,4,128]{3,0,2,1:T(4,128)S(1)}, u32[]{:S(2)}, u32[]{:S(2)}) collective-permute-start(f32[3,2,4,128]{3,0,2,1:T(4,128)S(1)} %get-tuple-element.56), channel_id=1, source_target_pairs={{96,0},{192,96},{288,192},{384,288},{480,384},{576,480},{672,576},... | collective-permute-start | bytes 36872 | tf_op jit(solution)/shard_map/ppermute | solution.py:151
  4.2 12.2 %collective-permute-start = (f32[3,2,4,128]{3,2,1,0:T(4,128)S(1)}, f32[3,2,4,128]{3,2,1,0:T(4,128)S(1)}, u32[]{:S(2)}, u32[]{:S(2)}) collective-permute-start(f32[3,2,4,128]{3,2,1,0:T(4,128)S(1)} %copy.107), channel_id=1, source_target_pairs={{0,96},{96,192},{192,288},{288,384},{384,480},{480,576},{576,672},... | collective-permute-start | bytes 36872 | tf_op jit(solution)/shard_map/ppermute | solution.py:150
  15.2 16.3 %copy-start.2 = (f32[2,2,128,128]{3,2,1,0:T(8,128)}, f32[2,2,128,128]{3,2,1,0:T(8,128)S(1)}, u32[]{:S(2)}) copy-start(f32[2,2,128,128]{3,2,1,0:T(8,128)S(1)} %convert_multiply_fusion.4.weight_ref) | copy-start | bytes 786436
  16.4 12.7 %collective-permute-start.2 = (f32[3,2,4,128]{3,2,1,0:T(4,128)S(1)}, f32[3,2,4,128]{3,2,1,0:T(4,128)S(1)}, u32[]{:S(2)}, u32[]{:S(2)}) collective-permute-start(f32[3,2,4,128]{3,2,1,0:T(4,128)S(1)} %get-tuple-element.54), channel_id=1, source_target_pairs={{0,1},{1,2},{2,3},{3,4},{4,5},{5,6},{6,7},{7,8},{8,9},{9,10},{10,1... | collective-permute-start | bytes 36872 | tf_op jit(solution)/shard_map/ppermute | solution.py:153
  18.7 11.2 %collective-permute-start.3 = (f32[3,2,4,128]{3,2,1,0:T(4,128)S(1)}, f32[3,2,4,128]{3,2,1,0:T(4,128)S(1)}, u32[]{:S(2)}, u32[]{:S(2)}) collective-permute-start(f32[3,2,4,128]{3,2,1,0:T(4,128)S(1)} %get-tuple-element.53), channel_id=1, source_target_pairs={{1,0},{2,1},{3,2},{4,3},{5,4},{6,5},{7,6},{8,7},{9,8},{10,9},{11,1... | collective-permute-start | bytes 36872 | tf_op jit(solution)/shard_map/ppermute | solution.py:154
  31.3 26.6 %copy-start.5 = (f32[4,64]{1,0:T(4,128)S(1)}, f32[4,64]{1,0:T(4,128)}, u32[]{:S(2)}) copy-start(f32[4,64]{1,0:T(4,128)} %param.15) | copy-start | bytes 3076
  57.9 2.5 %copy-start.7 = (f32[64]{0:T(128)S(1)}, f32[64]{0:T(128)}, u32[]{:S(2)}) copy-start(f32[64]{0:T(128)} %param.17) | copy-start | bytes 772
  61.6 0.8 copy-start.3
  69.9 17.7 %copy-start.6 = (s32[1,1,8,2]{2,3,1,0:T(2,128)S(1)}, s32[1,1,8,2]{2,3,1,0:T(2,128)}, u32[]{:S(2)}) copy-start(s32[1,1,8,2]{2,3,1,0:T(2,128)} %param.13) | copy-start | bytes 196
  71.0 2.9 %collective-permute-start.4 = (f32[3,2,3,128]{3,1,2,0:T(2,128)S(1)}, f32[3,2,3,128]{3,1,2,0:T(2,128)S(1)}, u32[]{:S(2)}, u32[]{:S(2)}) collective-permute-start(f32[3,2,3,128]{3,1,2,0:T(2,128)S(1)} %copy.83), channel_id=1, source_target_pairs={{0,96},{96,192},{192,288},{288,384},{384,480},{480,576},{576,672},... | collective-permute-start | bytes 27656 | tf_op jit(solution)/shard_map/ppermute | solution.py:150
  73.2 4.3 %collective-permute-start.5 = (f32[3,2,3,128]{3,1,2,0:T(2,128)S(1)}, f32[3,2,3,128]{3,1,2,0:T(2,128)S(1)}, u32[]{:S(2)}, u32[]{:S(2)}) collective-permute-start(f32[3,2,3,128]{3,1,2,0:T(2,128)S(1)} %copy.89), channel_id=1, source_target_pairs={{96,0},{192,96},{288,192},{384,288},{480,384},{576,480},{672,576},... | collective-permute-start | bytes 27656 | tf_op jit(solution)/shard_map/ppermute | solution.py:151
  77.5 9.2 %collective-permute-start.6 = (f32[3,2,3,128]{3,0,1,2:T(4,128)S(1)}, f32[3,2,3,128]{3,0,1,2:T(4,128)S(1)}, u32[]{:S(2)}, u32[]{:S(2)}) collective-permute-start(f32[3,2,3,128]{3,0,1,2:T(4,128)S(1)} %get-tuple-element.60), channel_id=1, source_target_pairs={{0,1},{1,2},{2,3},{3,4},{4,5},{5,6},{6,7},{7,8},{8,9},{9,10},{10,1... | collective-permute-start | bytes 27656 | tf_op jit(solution)/shard_map/ppermute | solution.py:153
  79.5 8.1 %collective-permute-start.7 = (f32[3,2,3,128]{3,0,1,2:T(4,128)S(1)}, f32[3,2,3,128]{3,0,1,2:T(4,128)S(1)}, u32[]{:S(2)}, u32[]{:S(2)}) collective-permute-start(f32[3,2,3,128]{3,0,1,2:T(4,128)S(1)} %get-tuple-element.59), channel_id=1, source_target_pairs={{1,0},{2,1},{3,2},{4,3},{5,4},{6,5},{7,6},{8,7},{9,8},{10,9},{11,1... | collective-permute-start | bytes 27656 | tf_op jit(solution)/shard_map/ppermute | solution.py:154

commit v9 on v8

--- a/solution.py
+++ b/solution.py
@@ -32,30 +32,23 @@
 
 
 def pair_kernel(own_ref, other_ref, weight_ref, feat_ref, out_ref):
-    slot = pl.program_id(1)
     count = out_ref.shape[1] // 9
-    rel = [other_ref[0, 0, d : d + 1, :] - own_ref[0, :, d : d + 1] for d in range(3)]
-    dist = jnp.sqrt((rel[0] * rel[0] + rel[1] * rel[1] + rel[2] * rel[2]) + 0.25)
-    angular = harmonics(rel, dist)
-    weight = weight_ref[0, 0]
-    feat = feat_ref[0, 0]
-    for k in range(count):
-        offset = dist - (0.5 + k)
-        basis = jnp.exp(-0.5 * offset * offset)
-        for m in range(9):
-            tile = ((basis * angular[m]) * weight).astype(jnp.bfloat16)
-            part = lax.dot_general(
-                feat, tile, (((1,), (1,)), ((), ())), preferred_element_type=jnp.float32
-            )
-            q = k * 9 + m
-
-            @pl.when(slot == 0)
-            def _():
-                out_ref[0, q] = part
-
-            @pl.when(slot > 0)
-            def _():
-                out_ref[0, q] = out_ref[0, q] + part
+    for slot in range(other_ref.shape[1]):
+        rel = [other_ref[0, slot, d : d + 1, :] - own_ref[0, :, d : d + 1] for d in range(3)]
+        dist = jnp.sqrt((rel[0] * rel[0] + rel[1] * rel[1] + rel[2] * rel[2]) + 0.25)
+        angular = harmonics(rel, dist)
+        weight = weight_ref[0, slot]
+        feat = feat_ref[0, slot]
+        for k in range(count):
+            offset = dist - (0.5 + k)
+            basis = jnp.exp(-0.5 * offset * offset)
+            for m in range(9):
+                tile = ((basis * angular[m]) * weight).astype(jnp.bfloat16)
+                part = jnp.dot(tile, feat, preferred_element_type=jnp.float32)
+                if slot == 0:
+                    out_ref[0, k * 9 + m] = part
+                else:
+                    out_ref[0, k * 9 + m] = out_ref[0, k * 9 + m] + part
 
 
 def fused_proj(own_pos, others_pos, others_feat, weights, count):
@@ -63,16 +56,16 @@
     listed, width = others_pos.shape[1], others_feat.shape[2]
     return pl.pallas_call(
         pair_kernel,
-        grid=(blocks, listed),
+        grid=(blocks,),
         in_specs=[
-            pl.BlockSpec((1, atoms, 3), lambda b, n: (b, 0, 0)),
-            pl.BlockSpec((1, 1, 3, atoms), lambda b, n: (b, n, 0, 0)),
-            pl.BlockSpec((1, 1, atoms, atoms), lambda b, n: (b, n, 0, 0)),
-            pl.BlockSpec((1, 1, width, atoms), lambda b, n: (b, n, 0, 0)),
+            pl.BlockSpec((1, atoms, 3), lambda b: (b, 0, 0)),
+            pl.BlockSpec((1, listed, 3, atoms), lambda b: (b, 0, 0, 0)),
+            pl.BlockSpec((1, listed, atoms, atoms), lambda b: (b, 0, 0, 0)),
+            pl.BlockSpec((1, listed, atoms, width), lambda b: (b, 0, 0, 0)),
         ],
-        out_specs=pl.BlockSpec((1, count * 9, width, atoms), lambda b, n: (b, 0, 0, 0)),
-        out_shape=jax.ShapeDtypeStruct((blocks, count * 9, width, atoms), jnp.float32),
-    )(jnp.swapaxes(own_pos, 1, 2), others_pos, weights, others_feat)
+        out_specs=pl.BlockSpec((1, count * 9, atoms, width), lambda b: (b, 0, 0, 0)),
+        out_shape=jax.ShapeDtypeStruct((blocks, count * 9, atoms, width), jnp.float32),
+    )(jnp.swapaxes(own_pos, 1, 2), others_pos, weights, jnp.swapaxes(others_feat, 2, 3))
 
 
 def plain_proj(own_pos, others_pos, others_feat, weights, count):
@@ -90,7 +83,7 @@
             tiles = basis[:, None] * angular[None] * weights[block, slot][None, None]
             tiles = tiles.reshape(count * 9, atoms, atoms).astype(jnp.bfloat16)
             total = total + jnp.einsum(
-                "qij,cj->qci", tiles, others_feat[block, slot], preferred_element_type=jnp.float32
+                "qij,cj->qic", tiles, others_feat[block, slot], preferred_element_type=jnp.float32
             )
         result.append(total)
     return jnp.stack(result)
@@ -125,12 +118,12 @@
 def block_energies(proj, radial, readin, readout):
     count = radial.shape[0]
     proj = proj.reshape((proj.shape[0], count, 9) + proj.shape[2:])
-    message = jnp.sum(radial[None, :, None, :, None] * proj, axis=1)
+    message = jnp.sum(radial[None, :, None, None, :] * proj, axis=1)
     first = jnp.sum(message[:, 1:4] * message[:, 1:4], axis=1)
     second = jnp.sum(message[:, 4:9] * message[:, 4:9], axis=1)
-    invariants = jnp.concatenate([message[:, 0], first, second], axis=1)
-    hidden = jax.nn.silu(jnp.einsum("fh,bfi->bhi", readin, invariants, precision=HIGHEST))
-    return jnp.einsum("h,bhi->bi", readout, hidden, precision=HIGHEST)
+    invariants = jnp.concatenate([message[:, 0], first, second], axis=2)
+    hidden = jax.nn.silu(jnp.einsum("bif,fh->bih", invariants, readin, precision=HIGHEST))
+    return jnp.einsum("bih,h->bi", hidden, readout, precision=HIGHEST)
 
 
 def select_slots(table, chosen):

time: 88.9 us -> 70.5 us (0.79)
  Pallas kernels: 25.6 us -> 4.46 us
  local copies, waits for them, and re-layouts: 3.78 us -> 7.27 us
  starting transfers between devices: 33.4 us -> 32.2 us
    pallas_call x1, Pallas kernels: 25.6 us -> 4.46 us  [fused_proj(): pl.pallas_call(pair_kernel, grid=(blocks,), in_specs=[pl.BlockSpec((1, at...]
    unnamed x37 -> x44, local copies, waits for them, and re-layouts: 2.01 us -> 4.1 us
    ppermute x2, starting transfers between devices: 11.3 us -> 10.1 us  [halo(): from_left_x = lax.ppermute(grid[2], 'gx', up_x)]
    reduce_sum x1, other arithmetic: 2.11 us -> 3.04 us  [block_energies(): message = jnp.sum(radial[None, :, None, None, :] * proj, axis=1)]
  transfers between devices with their start and end apart: 8 -> 8, of which waited for: 4 -> 4; matrix products, arithmetic and copies ran while one was open for 4% -> 7% of each run, Pallas kernels for 0% -> 0%
where the time goes in v9:
time: 70.5 us; the launch traced here: 70 us
  starting transfers between devices  32.2 us (46%)
  other arithmetic  12.8 us (18%)
  local copies, waits for them, and re-layouts  7.27 us (10%)
  matrix products  5.79 us (8%)
  waiting for transfers between devices  5.76 us (8%)
  Pallas kernels  4.46 us (6%)
  between operations  1.75 us (2%)
    ppermute x2, starting transfers between devices, halo(): from_right_y = lax.ppermute(rows[:, 0], 'gy', down_y)  17.6 us
    ppermute x2, starting transfers between devices, halo(): from_left_x = lax.ppermute(grid[2], 'gx', up_x)  10.1 us
    pallas_call x1, Pallas kernels, fused_proj(): pl.pallas_call(pair_kernel, grid=(blocks,), in_specs=[pl.BlockSpec((1, at...  4.46 us
    unnamed x44, local copies, waits for them, and re-layouts  4.1 us
    ppermute x2, starting transfers between devices, halo(): from_left_y = lax.ppermute(rows[:, 2], 'gy', up_y)  3.84 us
    ppermute x2, waiting for transfers between devices, halo(): from_right_x = lax.ppermute(grid[0], 'gx', down_x)  3.59 us
    reduce_sum x7, other arithmetic, energies_of(): proj = pair_proj(own_now, others_pos, others_feat, weights, radial.shape[0])  3.16 us
    reduce_sum x1, other arithmetic, block_energies(): message = jnp.sum(radial[None, :, None, None, :] * proj, axis=1)  3.04 us
  transfers between devices with their start and end apart: 8, of which 4 were waited for; matrix products, arithmetic and copies ran while one was open for 7% of the time, Pallas kernels for 0%

profile of v9, /device:TPU:7, one launch (start us, length us, event | category | flops | bytes accessed | tf_op | source)
XLA Modules:
  0.0 70.0 jit_solution(15335483556075543815)
XLA Ops:
  0.7 0.9 %copy.82 = f32[3,256]{0,1:T(8,128)S(1)} copy(f32[3,256]{1,0:T(4,128)} %param.9) | data formatting | bytes 6144 | tf_op args[0]
  1.5 0.7 %convert_bitcast_fusion = f32[2,1,128]{2,0,1:T(2,128)S(1)} fusion(s32[256]{0:T(256)} %param.10), kind=kLoop, calls=%fused_computation.470 | loop fusion | flops 256 | bytes 2048 | tf_op jit(solution)/shard_map/convert_element_type | solution.py:169
  2.6 0.9 %fusion.220 = f32[8,2,4,128]{3,0,2,1:T(8,128)S(1)} fusion(f32[2,4,128]{2,0,1:T(2,128)S(1)} %copy.84, s32[8,2]{0,1:T(2,128)} %bitcast.775), kind=kOutput, calls=%fused_computation.456 | convolution fusion | flops 196640 | bytes 36928 | tf_op jit(solution)/shard_map/dgb,bra->dgra/dot_general | solution.py:173
  3.5 0.7 collective-permute-start.1
  4.2 9.1 %collective-permute-start = (f32[3,2,4,128]{3,2,1,0:T(4,128)S(1)}, f32[3,2,4,128]{3,2,1,0:T(4,128)S(1)}, u32[]{:S(2)}, u32[]{:S(2)}) collective-permute-start(f32[3,2,4,128]{3,2,1,0:T(4,128)S(1)} %copy.140), channel_id=1, source_target_pairs={{0,96},{96,192},{192,288},{288,384},{384,480},{480,576},{576,672},... | collective-permute-start | bytes 36872 | tf_op jit(solution)/shard_map/ppermute | solution.py:143
  13.3 0.6 constant_dynamic-update-slice_fusion.25
  13.9 0.6 constant_dynamic-update-slice_fusion.16
  14.6 0.7 iota_compare_fusion
  15.4 1.0 %convert_multiply_fusion.4.weight_ref = f32[2,2,128,128]{3,2,1,0:T(8,128)S(1)} fusion(s32[2,2,128,128]{3,2,1,0:T(8,128)} %param.12), kind=kLoop, calls=%fused_computation.73 | loop fusion | flops 131072 | bytes 524288 | tf_op jit(solution)/shard_map/mul | solution.py:188
  16.4 1.0 %convolution_bitcast_fusion.1 = f32[64,256]{1,0:T(8,128)S(1)} fusion(f32[4,64]{1,0:T(4,128)} %param.14, s32[256]{0:T(256)} %param.10), kind=kOutput, calls=%fused_computation.28 | convolution fusion | flops 787456 | bytes 67584 | tf_op jit(solution)/shard_map/dot_general | solution.py:180
  17.6 1.9 %collective-permute-start.2 = (f32[3,2,4,128]{3,2,1,0:T(4,128)S(1)}, f32[3,2,4,128]{3,2,1,0:T(4,128)S(1)}, u32[]{:S(2)}, u32[]{:S(2)}) collective-permute-start(f32[3,2,4,128]{3,2,1,0:T(4,128)S(1)} %get-tuple-element.54), channel_id=1, source_target_pairs={{0,1},{1,2},{2,3},{3,4},{4,5},{5,6},{6,7},{7,8},{8,9},{9,10},{10,1... | collective-permute-start | bytes 36872 | tf_op jit(solution)/shard_map/ppermute | solution.py:146
  19.9 10.4 %collective-permute-start.3 = (f32[3,2,4,128]{3,2,1,0:T(4,128)S(1)}, f32[3,2,4,128]{3,2,1,0:T(4,128)S(1)}, u32[]{:S(2)}, u32[]{:S(2)}) collective-permute-start(f32[3,2,4,128]{3,2,1,0:T(4,128)S(1)} %get-tuple-element.53), channel_id=1, source_target_pairs={{1,0},{2,1},{3,2},{4,3},{5,4},{6,5},{7,6},{8,7},{9,8},{10,9},{11,1... | collective-permute-start | bytes 36872 | tf_op jit(solution)/shard_map/ppermute | solution.py:147
  30.3 0.8 %collective-permute-done.3 = f32[3,2,4,128]{3,2,1,0:T(4,128)S(1)} collective-permute-done((f32[3,2,4,128]{3,2,1,0:T(4,128)S(1)}, f32[3,2,4,128]{3,2,1,0:T(4,128)S(1)}, u32[]{:S(2)}, u32[]{:S(2)}) %collective-permute-start.3) | collective-permute-done | bytes 12320 | tf_op jit(solution)/shard_map/ppermute | solution.py:147
  32.9 0.8 %copy.92 = bf16[2,2,64,128]{2,3,1,0:T(8,128)(2,1)} copy(bf16[2,2,64,128]{3,2,1,0:T(8,128)(2,1)S(1)} %select_reduce_fusion) | data formatting | bytes 131072 | tf_op jit(solution)/shard_map/jvp()/reduce_sum | solution.py:133
  33.7 4.5 %jvp__.1 = f32[2,36,128,64]{3,2,1,0:T(8,128)} custom-call(f32[2,128,3]{2,1,0:T(8,128)} %bitcast.745, f32[2,2,3,128]{3,2,1,0:T(4,128)} %copy.93.other_ref, f32[2,2,128,128]{3,2,1,0:T(8,128)} %copy-done.2, bf16[2,2,128,64]{3,2,1,0:T(8,128)(2,1)} %bitcast.747), custom_call_target="tpu_custom_call" | custom-call | tf_op jit(solution)/shard_map/jvp()/pallas_call | solution.py:57
  38.1 3.0 %multiply_reduce_fusion = f32[2,9,128,64]{3,2,1,0:T(8,128)S(1)} fusion(f32[2,4,9,128,64]{4,3,2,1,0:T(8,128)} %bitcast.725, f32[4,64]{1,0:T(4,128)S(1)} %copy-done.6), kind=kLoop, calls=%fused_computation | loop fusion | flops 1032192 | bytes 2950144 | tf_op jit(solution)/shard_map/jvp()/reduce_sum | solution.py:121
  42.1 0.7 %fusion.201 = f32[1,2,128]{2,0,1:T(1,128)} fusion(f32[2,128,64]{1,2,0:T(8,128)S(1)} %fusion.39, f32[64]{0:T(128)S(1)} %copy-done.9), kind=kOutput, calls=%fused_computation.409 | convolution fusion | flops 262144 | bytes 66816 | tf_op jit(solution)/shard_map/jvp(bih,h->bi)/dot_general | solution.py:126
  49.3 0.9 %fusion.2 = (f32[9,128,128]{2,1,0:T(8,128)S(1)}, f32[4,128,128]{2,1,0:T(8,128)S(1)}, f32[4,128,128]{2,1,0:T(8,128)S(1)}, f32[9,128,128]{2,1,0:T(8,128)S(1)}) fusion(bf16[4,9,128,128]{3,2,1,0:T(8,128)(2,1)S(1)} %bitcast.740, f32[128,128]{1,0:T(8,128)S(1)} %get-tuple-element.40, f32[4,128,128]{2,1,0:T(8,128)S(1)} %get-tuple-element.75, ...), kind=kLoop, calls=%fused_computation.4 | loop fusion | flops 6651904 | bytes 5898240 | tf_op jit(solution)/shard_map/transpose(jvp(transpose(jvp())))/reduce_sum | solution.py:195
  50.4 0.9 %fusion.10 = (f32[9,128,128]{2,1,0:T(8,128)S(1)}, f32[4,128,128]{2,1,0:T(8,128)S(1)}, f32[4,128,128]{2,1,0:T(8,128)S(1)}, f32[9,128,128]{2,1,0:T(8,128)S(1)}) fusion(bf16[4,9,128,128]{3,2,1,0:T(8,128)(2,1)S(1)} %bitcast.738, f32[128,128]{1,0:T(8,128)S(1)} %get-tuple-element.42, f32[4,128,128]{2,1,0:T(8,128)S(1)} %get-tuple-element.77, ...), kind=kLoop, calls=%fused_computation.14 | loop fusion | flops 6651904 | bytes 5898240 | tf_op jit(solution)/shard_map/transpose(jvp(transpose(jvp())))/reduce_sum | solution.py:195
  53.8 0.9 %collective-permute-start.4 = (f32[3,2,3,128]{3,1,2,0:T(2,128)S(1)}, f32[3,2,3,128]{3,1,2,0:T(2,128)S(1)}, u32[]{:S(2)}, u32[]{:S(2)}) collective-permute-start(f32[3,2,3,128]{3,1,2,0:T(2,128)S(1)} %copy.108), channel_id=1, source_target_pairs={{0,96},{96,192},{192,288},{288,384},{384,480},{480,576},{576,672},... | collective-permute-start | bytes 27656 | tf_op jit(solution)/shard_map/ppermute | solution.py:143
  55.6 3.6 %collective-permute-done.5 = f32[3,2,3,128]{3,1,2,0:T(2,128)S(1)} collective-permute-done((f32[3,2,3,128]{3,1,2,0:T(2,128)S(1)}, f32[3,2,3,128]{3,1,2,0:T(2,128)S(1)}, u32[]{:S(2)}, u32[]{:S(2)}) %collective-permute-start.5) | collective-permute-done | bytes 9248 | tf_op jit(solution)/shard_map/ppermute | solution.py:144
  59.2 1.9 %collective-permute-start.6 = (f32[3,2,3,128]{3,0,1,2:T(4,128)S(1)}, f32[3,2,3,128]{3,0,1,2:T(4,128)S(1)}, u32[]{:S(2)}, u32[]{:S(2)}) collective-permute-start(f32[3,2,3,128]{3,0,1,2:T(4,128)S(1)} %get-tuple-element.60), channel_id=1, source_target_pairs={{0,1},{1,2},{2,3},{3,4},{4,5},{5,6},{6,7},{7,8},{8,9},{9,10},{10,1... | collective-permute-start | bytes 27656 | tf_op jit(solution)/shard_map/ppermute | solution.py:146
  61.1 7.2 %collective-permute-start.7 = (f32[3,2,3,128]{3,0,1,2:T(4,128)S(1)}, f32[3,2,3,128]{3,0,1,2:T(4,128)S(1)}, u32[]{:S(2)}, u32[]{:S(2)}) collective-permute-start(f32[3,2,3,128]{3,0,1,2:T(4,128)S(1)} %get-tuple-element.59), channel_id=1, source_target_pairs={{1,0},{2,1},{3,2},{4,3},{5,4},{6,5},{7,6},{8,7},{9,8},{10,9},{11,1... | collective-permute-start | bytes 27656 | tf_op jit(solution)/shard_map/ppermute | solution.py:147
  68.4 0.8 %collective-permute-done.7 = f32[3,2,3,128]{3,0,1,2:T(4,128)S(1)} collective-permute-done((f32[3,2,3,128]{3,0,1,2:T(4,128)S(1)}, f32[3,2,3,128]{3,0,1,2:T(4,128)S(1)}, u32[]{:S(2)}, u32[]{:S(2)}) %collective-permute-start.7) | collective-permute-done | bytes 9248 | tf_op jit(solution)/shard_map/ppermute | solution.py:147
  (178 shorter events, 13.8 us)
Async XLA Ops:
  0.6 41.2 %copy-start = (f32[192,64]{0,1:T(8,128)S(1)}, f32[192,64]{0,1:T(8,128)}, u32[]{:S(2)}) copy-start(f32[192,64]{0,1:T(8,128)} %param.16) | copy-start | bytes 147460
  0.6 31.2 %copy-start.7 = (f32[4,64]{1,0:T(4,128)S(1)}, f32[4,64]{1,0:T(4,128)}, u32[]{:S(2)}) copy-start(f32[4,64]{1,0:T(4,128)} %param.14) | copy-start | bytes 3076
  1.5 30.9 %copy-start.1 = (f32[3,256]{0,1:T(8,128)}, f32[3,256]{0,1:T(8,128)S(1)}, u32[]{:S(2)}) copy-start(f32[3,256]{0,1:T(8,128)S(1)} %copy.82) | copy-start | bytes 9220
  3.5 14.0 %collective-permute-start.1 = (f32[3,2,4,128]{3,0,2,1:T(4,128)S(1)}, f32[3,2,4,128]{3,0,2,1:T(4,128)S(1)}, u32[]{:S(2)}, u32[]{:S(2)}) collective-permute-start(f32[3,2,4,128]{3,0,2,1:T(4,128)S(1)} %get-tuple-element.56), channel_id=1, source_target_pairs={{96,0},{192,96},{288,192},{384,288},{480,384},{576,480},{672,576},... | collective-permute-start | bytes 36872 | tf_op jit(solution)/shard_map/ppermute | solution.py:144
  4.2 13.4 %collective-permute-start = (f32[3,2,4,128]{3,2,1,0:T(4,128)S(1)}, f32[3,2,4,128]{3,2,1,0:T(4,128)S(1)}, u32[]{:S(2)}, u32[]{:S(2)}) collective-permute-start(f32[3,2,4,128]{3,2,1,0:T(4,128)S(1)} %copy.140), channel_id=1, source_target_pairs={{0,96},{96,192},{192,288},{288,384},{384,480},{480,576},{576,672},... | collective-permute-start | bytes 36872 | tf_op jit(solution)/shard_map/ppermute | solution.py:143
  16.4 16.3 %copy-start.2 = (f32[2,2,128,128]{3,2,1,0:T(8,128)}, f32[2,2,128,128]{3,2,1,0:T(8,128)S(1)}, u32[]{:S(2)}) copy-start(f32[2,2,128,128]{3,2,1,0:T(8,128)S(1)} %convert_multiply_fusion.4.weight_ref) | copy-start | bytes 786436
  17.6 12.7 %collective-permute-start.2 = (f32[3,2,4,128]{3,2,1,0:T(4,128)S(1)}, f32[3,2,4,128]{3,2,1,0:T(4,128)S(1)}, u32[]{:S(2)}, u32[]{:S(2)}) collective-permute-start(f32[3,2,4,128]{3,2,1,0:T(4,128)S(1)} %get-tuple-element.54), channel_id=1, source_target_pairs={{0,1},{1,2},{2,3},{3,4},{4,5},{5,6},{6,7},{7,8},{8,9},{9,10},{10,1... | collective-permute-start | bytes 36872 | tf_op jit(solution)/shard_map/ppermute | solution.py:146
  19.9 11.2 %collective-permute-start.3 = (f32[3,2,4,128]{3,2,1,0:T(4,128)S(1)}, f32[3,2,4,128]{3,2,1,0:T(4,128)S(1)}, u32[]{:S(2)}, u32[]{:S(2)}) collective-permute-start(f32[3,2,4,128]{3,2,1,0:T(4,128)S(1)} %get-tuple-element.53), channel_id=1, source_target_pairs={{1,0},{2,1},{3,2},{4,3},{5,4},{6,5},{7,6},{8,7},{9,8},{10,9},{11,1... | collective-permute-start | bytes 36872 | tf_op jit(solution)/shard_map/ppermute | solution.py:147
  33.7 4.5 %copy-start.6 = (f32[4,64]{1,0:T(4,128)S(1)}, f32[4,64]{1,0:T(4,128)}, u32[]{:S(2)}) copy-start(f32[4,64]{1,0:T(4,128)} %param.15) | copy-start | bytes 3076
  41.2 0.9 %copy-start.9 = (f32[64]{0:T(128)S(1)}, f32[64]{0:T(128)}, u32[]{:S(2)}) copy-start(f32[64]{0:T(128)} %param.17) | copy-start | bytes 772
  44.3 0.9 %copy-start.3 = (bf16[2,2,64,128]{2,3,1,0:T(8,128)(2,1)S(1)}, bf16[2,2,64,128]{2,3,1,0:T(8,128)(2,1)}, u32[]{:S(2)}) copy-start(bf16[2,2,64,128]{2,3,1,0:T(8,128)(2,1)} %copy.92) | copy-start | bytes 196612
  46.7 1.1 %copy-start.5 = (f32[9,128,128]{2,1,0:T(8,128)S(1)}, f32[9,128,128]{2,1,0:T(8,128)}, u32[]{:S(2)}) copy-start(f32[9,128,128]{2,1,0:T(8,128)} %constant_dynamic-update-slice_fusion.25) | copy-start | bytes 1769476
  46.7 1.4 %copy-start.4 = (f32[9,128,128]{2,1,0:T(8,128)S(1)}, f32[9,128,128]{2,1,0:T(8,128)}, u32[]{:S(2)}) copy-start(f32[9,128,128]{2,1,0:T(8,128)} %constant_dynamic-update-slice_fusion.16) | copy-start | bytes 1769476
  52.8 16.5 %copy-start.8 = (s32[1,1,8,2]{2,3,1,0:T(2,128)S(1)}, s32[1,1,8,2]{2,3,1,0:T(2,128)}, u32[]{:S(2)}) copy-start(s32[1,1,8,2]{2,3,1,0:T(2,128)} %param.13) | copy-start | bytes 196
  53.8 1.7 %collective-permute-start.4 = (f32[3,2,3,128]{3,1,2,0:T(2,128)S(1)}, f32[3,2,3,128]{3,1,2,0:T(2,128)S(1)}, u32[]{:S(2)}, u32[]{:S(2)}) collective-permute-start(f32[3,2,3,128]{3,1,2,0:T(2,128)S(1)} %copy.108), channel_id=1, source_target_pairs={{0,96},{96,192},{192,288},{288,384},{384,480},{480,576},{576,672},... | collective-permute-start | bytes 27656 | tf_op jit(solution)/shard_map/ppermute | solution.py:143
  54.8 4.3 %collective-permute-start.5 = (f32[3,2,3,128]{3,1,2,0:T(2,128)S(1)}, f32[3,2,3,128]{3,1,2,0:T(2,128)S(1)}, u32[]{:S(2)}, u32[]{:S(2)}) collective-permute-start(f32[3,2,3,128]{3,1,2,0:T(2,128)S(1)} %copy.114), channel_id=1, source_target_pairs={{96,0},{192,96},{288,192},{384,288},{480,384},{576,480},{672,576},... | collective-permute-start | bytes 27656 | tf_op jit(solution)/shard_map/ppermute | solution.py:144
  59.2 9.2 %collective-permute-start.6 = (f32[3,2,3,128]{3,0,1,2:T(4,128)S(1)}, f32[3,2,3,128]{3,0,1,2:T(4,128)S(1)}, u32[]{:S(2)}, u32[]{:S(2)}) collective-permute-start(f32[3,2,3,128]{3,0,1,2:T(4,128)S(1)} %get-tuple-element.60), channel_id=1, source_target_pairs={{0,1},{1,2},{2,3},{3,4},{4,5},{5,6},{6,7},{7,8},{8,9},{9,10},{10,1... | collective-permute-start | bytes 27656 | tf_op jit(solution)/shard_map/ppermute | solution.py:146
  61.1 8.1 %collective-permute-start.7 = (f32[3,2,3,128]{3,0,1,2:T(4,128)S(1)}, f32[3,2,3,128]{3,0,1,2:T(4,128)S(1)}, u32[]{:S(2)}, u32[]{:S(2)}) collective-permute-start(f32[3,2,3,128]{3,0,1,2:T(4,128)S(1)} %get-tuple-element.59), channel_id=1, source_target_pairs={{1,0},{2,1},{3,2},{4,3},{5,4},{6,5},{7,6},{8,7},{9,8},{10,9},{11,1... | collective-permute-start | bytes 27656 | tf_op jit(solution)/shard_map/ppermute | solution.py:147

commit v10 on v3

--- a/solution.py
+++ b/solution.py
@@ -113,8 +113,8 @@
     ghost_kind = incoming[:, 3]
 
     def features(kind):
-        onehot = (kind[None, :] == jnp.arange(kinds).astype(kind.dtype)[:, None]).astype(jnp.float32)
-        return jnp.dot(embedding.T, onehot, precision=HIGHEST)
+        hit = kind[None, None, :] == jnp.arange(kinds).astype(kind.dtype)[:, None, None]
+        return jnp.sum(jnp.where(hit, embedding[:, :, None], 0.0), axis=0)
 
     own_feats32 = features(species).reshape(-1, blocks, atoms).transpose(1, 0, 2)
     ghost_feats32 = (
@@ -144,7 +144,9 @@
     energy, pullback = jax.vjp(energies_of, own_pos, ghost_pos)
     grad_own, grad_ghost = pullback(jnp.ones_like(energy))
     returned = collect(halo(place(grad_ghost.reshape(8, sends, 3, atoms))))
-    back = jnp.einsum("dgb,dgca->bca", pick, returned, precision=HIGHEST)
+    back = jnp.sum(
+        jnp.where(pick[:, :, :, None, None] > 0, returned[:, :, None], 0.0), axis=(0, 1)
+    )
     forces = -(grad_own + back)
     return (energy.reshape(blocks * atoms), forces.transpose(1, 0, 2).reshape(3, blocks * atoms))
 

time: 61 us -> 62.1 us (1.018)
  other arithmetic: 11.8 us -> 15 us
  waiting for transfers between devices: 2.26 us -> 4.08 us
  matrix products: 8.15 us -> 6.6 us
  starting transfers between devices: 34.1 us -> 32.7 us
  local copies, waits for them, and re-layouts: 2.34 us -> 1.6 us
    dot_general x3 -> x0, matrix products: 1.57 us -> none  [the longest x2 1.36 us: features(): return jnp.dot(embedding.T, onehot, precision=HIGHEST)]
    ppermute x2, starting transfers between devices: 13.9 us -> 12.6 us  [halo(): from_right_x = lax.ppermute(grid[0], 'gx', down_x)]
    reduce_sum x0 -> x3, other arithmetic: none -> 1.15 us  [the longest x2 1.06 us: features(): return jnp.sum(jnp.where(hit, embedding[:, :, None], 0.0), axis=0)]
    ppermute x2, waiting for transfers between devices: 0.01 us -> 0.95 us  [halo(): from_right_x = lax.ppermute(grid[0], 'gx', down_x)]
    ppermute x2, waiting for transfers between devices: 0.69 us -> 1.57 us  [halo(): from_left_x = lax.ppermute(grid[2], 'gx', up_x)]
    eq x0 -> x2, other arithmetic: none -> 0.77 us  [features(): kind[None, None, :] == jnp.arange(kinds).astype(kind.dtype)[:, None, None]]
    gt x0 -> x1, other arithmetic: none -> 0.69 us  [local(): pick[:, :, :, None, None] > 0]
    unnamed x32 -> x36, local copies, waits for them, and re-layouts: 1 us -> 0.35 us
  transfers between devices with their start and end apart: 8 -> 8, of which waited for: 3 -> 4; matrix products, arithmetic and copies ran while one was open for 6% -> 8% of each run, Pallas kernels for 0% -> 0%
where the time goes in v10:
time: 62.1 us; the launch traced here: 61.6 us
  starting transfers between devices  32.7 us (53%)
  other arithmetic  15 us (24%)
  matrix products  6.6 us (11%)
  waiting for transfers between devices  4.08 us (7%)
  between operations  1.67 us (3%)
  local copies, waits for them, and re-layouts  1.6 us (3%)
    ppermute x2, starting transfers between devices, halo(): from_right_y = lax.ppermute(rows[:, 0], 'gy', down_y)  16.2 us
    ppermute x2, starting transfers between devices, halo(): from_right_x = lax.ppermute(grid[0], 'gx', down_x)  12.6 us
    dot_general x8, matrix products, tile_terms(): jnp.einsum('qij,cj->qci', tiles.astype(jnp.bfloat16), other_feat, preferr...  4.21 us
    ppermute x2, starting transfers between devices, halo(): from_left_y = lax.ppermute(rows[:, 2], 'gy', up_y)  3.84 us
    reduce_sum x2, other arithmetic, tile_terms(): basis[:, None] * angular[None] * weight[None, None]  1.88 us
    ppermute x2, waiting for transfers between devices, halo(): from_left_x = lax.ppermute(grid[2], 'gx', up_x)  1.57 us
    ppermute x2, waiting for transfers between devices, halo(): from_right_y = lax.ppermute(rows[:, 0], 'gy', down_y)  1.55 us
    convert_element_type x4, other arithmetic, tile_terms(): tiles.astype(jnp.bfloat16)  1.39 us
  transfers between devices with their start and end apart: 8, of which 4 were waited for; matrix products, arithmetic and copies ran while one was open for 8% of the time, Pallas kernels for 0%

profile of v10, /device:TPU:1, one launch (start us, length us, event | category | flops | bytes accessed | tf_op | source)
XLA Modules:
  0.0 61.6 jit_solution(12477892163475934878)
XLA Ops:
  0.7 0.7 %convert_bitcast_fusion = f32[2,1,128]{2,0,1:T(2,128)S(1)} fusion(s32[256]{0:T(256)} %param.10), kind=kLoop, calls=%fused_computation.519 | loop fusion | flops 256 | bytes 2048 | tf_op jit(solution)/shard_map/convert_element_type | solution.py:106
  1.4 0.7 %reshape.564 = f32[3,2,128]{2,1,0:T(2,128)S(1)} reshape(f32[3,256]{1,0:T(4,128)} %param.9) | data formatting | bytes 6144 | tf_op jit(solution)/shard_map/reshape | solution.py:105
  2.1 0.9 %fusion.239 = f32[8,2,4,128]{3,0,2,1:T(8,128)S(1)} fusion(f32[2,1,128]{2,0,1:T(2,128)S(1)} %convert_bitcast_fusion, f32[2,3,128]{2,0,1:T(2,128)S(1)} %bitcast.774, s32[8,2]{0,1:T(2,128)} %bitcast.801), kind=kOutput, calls=%fused_computation.501 | convolution fusion | flops 197664 | bytes 36928 | tf_op jit(solution)/shard_map/dgb,bra->dgra/dot_general | solution.py:110
  3.0 10.5 %collective-permute-start.1 = (f32[3,2,4,128]{3,0,2,1:T(4,128)S(1)}, f32[3,2,4,128]{3,0,2,1:T(4,128)S(1)}, u32[]{:S(2)}, u32[]{:S(2)}) collective-permute-start(f32[3,2,4,128]{3,0,2,1:T(4,128)S(1)} %get-tuple-element.59), channel_id=1, source_target_pairs={{96,0},{192,96},{288,192},{384,288},{480,384},{576,480},{672,576},... | collective-permute-start | bytes 36872 | tf_op jit(solution)/shard_map/ppermute | solution.py:81
  13.5 0.7 %iota_compare_fusion.1 = pred[4,256]{1,0:T(4,128)(4,1)S(1)} fusion(s32[256]{0:T(256)} %param.10), kind=kLoop, calls=%fused_computation.504 | loop fusion | flops 1024 | bytes 2048 | tf_op jit(solution)/shard_map/eq | solution.py:116
  14.3 0.7 %convert_compare_fusion = pred[8,2,2]{0,2,1:T(4,128)(4,1)S(1)} fusion(s32[8,2]{0,1:T(2,128)} %bitcast.802), kind=kLoop, calls=%fused_computation.514 | loop fusion | flops 96 | bytes 96 | tf_op jit(solution)/shard_map/gt | solution.py:148
  15.0 1.0 %multiply_bitcast_fusion = (f32[128,128]{1,0:T(8,128)S(1)}, f32[128,128]{1,0:T(8,128)S(1)}, f32[128,128]{1,0:T(8,128)S(1)}, f32[128,128]{1,0:T(8,128)S(1)}) fusion(s32[2,2,128,128]{3,2,1,0:T(8,128)} %param.12), kind=kLoop, calls=%fused_computation.422 | loop fusion | flops 131072 | bytes 524288 | tf_op jit(solution)/shard_map/jvp()/mul | solution.py:41
  15.9 0.7 %iota_compare_fusion = pred[2,2,18]{1,2,0:T(8,128)(4,1)S(1)} fusion(s32[2,2]{1,0:T(2,128)} %param.11), kind=kLoop, calls=%fused_computation.464 | loop fusion | flops 72 | bytes 88 | tf_op jit(solution)/shard_map/jvp()/eq | solution.py:68
  16.8 0.8 %select_reduce_fusion.2 = f32[64,256]{1,0:T(8,128)S(1)} fusion(f32[4,64]{1,0:T(4,128)} %param.14, pred[4,256]{1,0:T(4,128)(4,1)S(1)} %iota_compare_fusion.1), kind=kLoop, calls=%fused_computation.85 | loop fusion | flops 114688 | bytes 67584 | tf_op jit(solution)/shard_map/reduce_sum | solution.py:117
  17.7 1.9 %collective-permute-start.2 = (f32[3,2,4,128]{3,2,1,0:T(4,128)S(1)}, f32[3,2,4,128]{3,2,1,0:T(4,128)S(1)}, u32[]{:S(2)}, u32[]{:S(2)}) collective-permute-start(f32[3,2,4,128]{3,2,1,0:T(4,128)S(1)} %get-tuple-element.57), channel_id=1, source_target_pairs={{0,1},{1,2},{2,3},{3,4},{4,5},{5,6},{6,7},{7,8},{8,9},{9,10},{10,1... | collective-permute-start | bytes 36872 | tf_op jit(solution)/shard_map/ppermute | solution.py:83
  19.8 9.3 %collective-permute-start.3 = (f32[3,2,4,128]{3,2,1,0:T(4,128)S(1)}, f32[3,2,4,128]{3,2,1,0:T(4,128)S(1)}, u32[]{:S(2)}, u32[]{:S(2)}) collective-permute-start(f32[3,2,4,128]{3,2,1,0:T(4,128)S(1)} %get-tuple-element.56), channel_id=1, source_target_pairs={{1,0},{2,1},{3,2},{4,3},{5,4},{6,5},{7,6},{8,7},{9,8},{10,9},{11,1... | collective-permute-start | bytes 36872 | tf_op jit(solution)/shard_map/ppermute | solution.py:84
  29.2 0.8 %collective-permute-done.3 = f32[3,2,4,128]{3,2,1,0:T(4,128)S(1)} collective-permute-done((f32[3,2,4,128]{3,2,1,0:T(4,128)S(1)}, f32[3,2,4,128]{3,2,1,0:T(4,128)S(1)}, u32[]{:S(2)}, u32[]{:S(2)}) %collective-permute-start.3) | collective-permute-done | bytes 12320 | tf_op jit(solution)/shard_map/ppermute | solution.py:84
  35.3 0.5 convolution_add_fusion.1
  36.2 0.5 convolution_add_fusion
  41.4 0.9 %fusion.2 = (f32[9,128,128]{2,1,0:T(8,128)S(1)}, f32[4,128,128]{2,1,0:T(8,128)S(1)}, f32[4,128,128]{2,1,0:T(8,128)S(1)}, f32[9,128,128]{2,1,0:T(8,128)S(1)}) fusion(bf16[4,9,128,128]{3,2,1,0:T(8,128)(2,1)S(1)} %bitcast.765, f32[128,128]{1,0:T(8,128)S(1)} %get-tuple-element.42, f32[4,128,128]{2,1,0:T(8,128)S(1)} %get-tuple-element.75, ...), kind=kLoop, calls=%fused_computation.3 | loop fusion | flops 6651904 | bytes 5898240 | tf_op jit(solution)/shard_map/transpose(jvp())/reduce_sum | solution.py:41
  42.5 0.9 %fusion.10 = (f32[9,128,128]{2,1,0:T(8,128)S(1)}, f32[4,128,128]{2,1,0:T(8,128)S(1)}, f32[4,128,128]{2,1,0:T(8,128)S(1)}, f32[9,128,128]{2,1,0:T(8,128)S(1)}) fusion(bf16[4,9,128,128]{3,2,1,0:T(8,128)(2,1)S(1)} %bitcast.763, f32[128,128]{1,0:T(8,128)S(1)} %get-tuple-element.43, f32[4,128,128]{2,1,0:T(8,128)S(1)} %get-tuple-element.77, ...), kind=kLoop, calls=%fused_computation.13 | loop fusion | flops 6651904 | bytes 5898240 | tf_op jit(solution)/shard_map/transpose(jvp())/reduce_sum | solution.py:41
  45.9 2.1 %collective-permute-start.5 = (f32[3,2,3,128]{3,2,1,0:T(4,128)S(1)}, f32[3,2,3,128]{3,2,1,0:T(4,128)S(1)}, u32[]{:S(2)}, u32[]{:S(2)}) collective-permute-start(f32[3,2,3,128]{3,2,1,0:T(4,128)S(1)} %bitcast.800), channel_id=1, source_target_pairs={{96,0},{192,96},{288,192},{384,288},{480,384},{576,480},{672,576},... | collective-permute-start | bytes 27656 | tf_op jit(solution)/shard_map/ppermute | solution.py:81
  48.1 0.9 %collective-permute-done.5 = f32[3,2,3,128]{3,2,1,0:T(4,128)S(1)} collective-permute-done((f32[3,2,3,128]{3,2,1,0:T(4,128)S(1)}, f32[3,2,3,128]{3,2,1,0:T(4,128)S(1)}, u32[]{:S(2)}, u32[]{:S(2)}) %collective-permute-start.5) | collective-permute-done | bytes 9248 | tf_op jit(solution)/shard_map/ppermute | solution.py:81
  49.1 1.6 %collective-permute-done.4 = f32[3,2,3,128]{3,2,1,0:T(4,128)S(1)} collective-permute-done((f32[3,2,3,128]{3,2,1,0:T(4,128)S(1)}, f32[3,2,3,128]{3,2,1,0:T(4,128)S(1)}, u32[]{:S(2)}, u32[]{:S(2)}) %collective-permute-start.4) | collective-permute-done | bytes 9248 | tf_op jit(solution)/shard_map/ppermute | solution.py:80
  50.7 1.9 %collective-permute-start.6 = (f32[3,2,3,128]{3,2,1,0:T(4,128)S(1)}, f32[3,2,3,128]{3,2,1,0:T(4,128)S(1)}, u32[]{:S(2)}, u32[]{:S(2)}) collective-permute-start(f32[3,2,3,128]{3,2,1,0:T(4,128)S(1)} %get-tuple-element.51), channel_id=1, source_target_pairs={{0,1},{1,2},{2,3},{3,4},{4,5},{5,6},{6,7},{7,8},{8,9},{9,10},{10,1... | collective-permute-start | bytes 27656 | tf_op jit(solution)/shard_map/ppermute | solution.py:83
  52.6 0.6 maximum_bitcast_fusion.4
  53.1 6.9 %collective-permute-start.7 = (f32[3,2,3,128]{3,2,1,0:T(4,128)S(1)}, f32[3,2,3,128]{3,2,1,0:T(4,128)S(1)}, u32[]{:S(2)}, u32[]{:S(2)}) collective-permute-start(f32[3,2,3,128]{3,2,1,0:T(4,128)S(1)} %get-tuple-element.50), channel_id=1, source_target_pairs={{1,0},{2,1},{3,2},{4,3},{5,4},{6,5},{7,6},{8,7},{9,8},{10,9},{11,1... | collective-permute-start | bytes 27656 | tf_op jit(solution)/shard_map/ppermute | solution.py:84
  60.1 0.8 %collective-permute-done.7 = f32[3,2,3,128]{3,2,1,0:T(4,128)S(1)} collective-permute-done((f32[3,2,3,128]{3,2,1,0:T(4,128)S(1)}, f32[3,2,3,128]{3,2,1,0:T(4,128)S(1)}, u32[]{:S(2)}, u32[]{:S(2)}) %collective-permute-start.7) | collective-permute-done | bytes 9248 | tf_op jit(solution)/shard_map/ppermute | solution.py:84
  61.0 0.6 fusion.238
  (171 shorter events, 13.0 us)
Async XLA Ops:
  0.6 36.5 %copy-start = (f32[192,64]{0,1:T(8,128)S(1)}, f32[192,64]{0,1:T(8,128)}, u32[]{:S(2)}) copy-start(f32[192,64]{0,1:T(8,128)} %param.16) | copy-start | bytes 147460
  0.6 19.2 %copy-start.2 = (f32[4,64]{1,0:T(4,128)S(1)}, f32[4,64]{1,0:T(4,128)}, u32[]{:S(2)}) copy-start(f32[4,64]{1,0:T(4,128)} %param.15) | copy-start | bytes 3076
  3.0 14.7 %collective-permute-start.1 = (f32[3,2,4,128]{3,0,2,1:T(4,128)S(1)}, f32[3,2,4,128]{3,0,2,1:T(4,128)S(1)}, u32[]{:S(2)}, u32[]{:S(2)}) collective-permute-start(f32[3,2,4,128]{3,0,2,1:T(4,128)S(1)} %get-tuple-element.59), channel_id=1, source_target_pairs={{96,0},{192,96},{288,192},{384,288},{480,384},{576,480},{672,576},... | collective-permute-start | bytes 36872 | tf_op jit(solution)/shard_map/ppermute | solution.py:81
  13.5 4.2 %collective-permute-start = (f32[3,2,4,128]{3,2,1,0:T(4,128)S(1)}, f32[3,2,4,128]{3,2,1,0:T(4,128)S(1)}, u32[]{:S(2)}, u32[]{:S(2)}) collective-permute-start(f32[3,2,4,128]{3,2,1,0:T(4,128)S(1)} %copy.50), channel_id=1, source_target_pairs={{0,96},{96,192},{192,288},{288,384},{384,480},{480,576},{576,672},... | collective-permute-start | bytes 36872 | tf_op jit(solution)/shard_map/ppermute | solution.py:80
  17.7 11.5 %collective-permute-start.2 = (f32[3,2,4,128]{3,2,1,0:T(4,128)S(1)}, f32[3,2,4,128]{3,2,1,0:T(4,128)S(1)}, u32[]{:S(2)}, u32[]{:S(2)}) collective-permute-start(f32[3,2,4,128]{3,2,1,0:T(4,128)S(1)} %get-tuple-element.57), channel_id=1, source_target_pairs={{0,1},{1,2},{2,3},{3,4},{4,5},{5,6},{6,7},{7,8},{8,9},{9,10},{10,1... | collective-permute-start | bytes 36872 | tf_op jit(solution)/shard_map/ppermute | solution.py:83
  19.8 10.1 %collective-permute-start.3 = (f32[3,2,4,128]{3,2,1,0:T(4,128)S(1)}, f32[3,2,4,128]{3,2,1,0:T(4,128)S(1)}, u32[]{:S(2)}, u32[]{:S(2)}) collective-permute-start(f32[3,2,4,128]{3,2,1,0:T(4,128)S(1)} %get-tuple-element.56), channel_id=1, source_target_pairs={{1,0},{2,1},{3,2},{4,3},{5,4},{6,5},{7,6},{8,7},{9,8},{10,9},{11,1... | collective-permute-start | bytes 36872 | tf_op jit(solution)/shard_map/ppermute | solution.py:84
  30.4 0.7 %copy-start.1 = (f32[4,64]{1,0:T(4,128)S(1)}, f32[4,64]{1,0:T(4,128)}, u32[]{:S(2)}) copy-start(f32[4,64]{1,0:T(4,128)} %param.14) | copy-start | bytes 3076
  36.7 0.7 %copy-start.3 = (f32[64]{0:T(128)S(1)}, f32[64]{0:T(128)}, u32[]{:S(2)}) copy-start(f32[64]{0:T(128)} %param.17) | copy-start | bytes 772
  45.9 3.1 %collective-permute-start.5 = (f32[3,2,3,128]{3,2,1,0:T(4,128)S(1)}, f32[3,2,3,128]{3,2,1,0:T(4,128)S(1)}, u32[]{:S(2)}, u32[]{:S(2)}) collective-permute-start(f32[3,2,3,128]{3,2,1,0:T(4,128)S(1)} %bitcast.800), channel_id=1, source_target_pairs={{96,0},{192,96},{288,192},{384,288},{480,384},{576,480},{672,576},... | collective-permute-start | bytes 27656 | tf_op jit(solution)/shard_map/ppermute | solution.py:81
  48.0 2.6 %collective-permute-start.4 = (f32[3,2,3,128]{3,2,1,0:T(4,128)S(1)}, f32[3,2,3,128]{3,2,1,0:T(4,128)S(1)}, u32[]{:S(2)}, u32[]{:S(2)}) collective-permute-start(f32[3,2,3,128]{3,2,1,0:T(4,128)S(1)} %bitcast.799), channel_id=1, source_target_pairs={{0,96},{96,192},{192,288},{288,384},{384,480},{480,576},{576,672},... | collective-permute-start | bytes 27656 | tf_op jit(solution)/shard_map/ppermute | solution.py:80
  50.7 9.4 %collective-permute-start.6 = (f32[3,2,3,128]{3,2,1,0:T(4,128)S(1)}, f32[3,2,3,128]{3,2,1,0:T(4,128)S(1)}, u32[]{:S(2)}, u32[]{:S(2)}) collective-permute-start(f32[3,2,3,128]{3,2,1,0:T(4,128)S(1)} %get-tuple-element.51), channel_id=1, source_target_pairs={{0,1},{1,2},{2,3},{3,4},{4,5},{5,6},{6,7},{7,8},{8,9},{9,10},{10,1... | collective-permute-start | bytes 27656 | tf_op jit(solution)/shard_map/ppermute | solution.py:83
  53.1 7.7 %collective-permute-start.7 = (f32[3,2,3,128]{3,2,1,0:T(4,128)S(1)}, f32[3,2,3,128]{3,2,1,0:T(4,128)S(1)}, u32[]{:S(2)}, u32[]{:S(2)}) collective-permute-start(f32[3,2,3,128]{3,2,1,0:T(4,128)S(1)} %get-tuple-element.50), channel_id=1, source_target_pairs={{1,0},{2,1},{3,2},{4,3},{5,4},{6,5},{7,6},{8,7},{9,8},{10,9},{11,1... | collective-permute-start | bytes 27656 | tf_op jit(solution)/shard_map/ppermute | solution.py:84

commit v11 on v3

--- a/solution.py
+++ b/solution.py
@@ -70,6 +70,21 @@
     return jnp.sum(jnp.where(hit, table, jnp.zeros((), table.dtype)), axis=2)
 
 
+def neighbourhood(own):
+    count_x = lax.axis_size("gx")
+    count_y = lax.axis_size("gy")
+    up_x = [(i, (i + 1) % count_x) for i in range(count_x)]
+    down_x = [((i + 1) % count_x, i) for i in range(count_x)]
+    up_y = [(i, (i + 1) % count_y) for i in range(count_y)]
+    down_y = [((i + 1) % count_y, i) for i in range(count_y)]
+    column = jnp.stack(
+        [lax.ppermute(own, "gx", up_x), own, lax.ppermute(own, "gx", down_x)], axis=0
+    )
+    return jnp.stack(
+        [lax.ppermute(column, "gy", up_y), column, lax.ppermute(column, "gy", down_y)], axis=1
+    )
+
+
 def halo(grid):
     count_x = lax.axis_size("gx")
     count_y = lax.axis_size("gy")
@@ -103,12 +118,24 @@
     kinds = embedding.shape[0]
     sends = send_lists.shape[3]
     own_pos = positions.reshape(3, blocks, atoms).transpose(1, 0, 2)
-    own_kind = species.reshape(blocks, 1, atoms).astype(jnp.float32)
-    payload = jnp.concatenate([own_pos, own_kind], axis=1)
     chosen = send_lists.reshape(8, sends)
     pick = (chosen[:, :, None] == jnp.arange(blocks)).astype(jnp.float32)
-    outgoing = jnp.einsum("dgb,bra->dgra", pick, payload, precision=HIGHEST)
-    incoming = collect(halo(place(outgoing))).reshape(8 * sends, 4, atoms)
+    raw = jnp.concatenate([positions, species.astype(jnp.float32)[None]], axis=0)
+    raw = raw.reshape(4 * blocks, atoms)
+    listing = jnp.zeros((atoms,), jnp.float32).at[: 8 * sends].set(
+        chosen.astype(jnp.float32).reshape(-1)
+    )
+    payload = jnp.concatenate([raw, listing[None]], axis=0)
+    near = neighbourhood(payload)
+    incoming = []
+    for d, pair in enumerate(OFFSETS):
+        cell = near[1 + pair[0], 1 + pair[1]]
+        rows = cell[: 4 * blocks].reshape(4, blocks, atoms)
+        sent = cell[4 * blocks, : 8 * sends].reshape(8, sends)[7 - d]
+        for g in range(sends):
+            hit = sent[g] == jnp.arange(blocks).astype(jnp.float32)
+            incoming.append(jnp.sum(jnp.where(hit[None, :, None], rows, 0.0), axis=1))
+    incoming = jnp.stack(incoming)
     ghost_pos = incoming[:, :3]
     ghost_kind = incoming[:, 3]
 

time: 61 us -> 77.3 us (1.27)
  other arithmetic: 11.8 us -> 24.3 us
  local copies, waits for them, and re-layouts: 2.34 us -> 8.09 us
  starting transfers between devices: 34.1 us -> 32.1 us
  matrix products: 8.15 us -> 7.27 us
  waiting for transfers between devices: 2.26 us -> 3.09 us
    ppermute x0 -> x4, starting transfers between devices: none -> 21.8 us  [the longest x1 10.5 us: neighbourhood(): lax.ppermute(own, 'gx', down_x)]
    ppermute x2 -> x1, starting transfers between devices: 13.9 us -> 1.38 us  [halo(): from_right_x = lax.ppermute(grid[0], 'gx', down_x)]
    eq x0 -> x16, other arithmetic: none -> 10.4 us  [local(): hit = sent[g] == jnp.arange(blocks).astype(jnp.float32)]
    ppermute x2 -> x1, starting transfers between devices: 16.4 us -> 6.68 us  [halo(): from_right_y = lax.ppermute(rows[:, 0], 'gy', down_y)]
    slice x0 -> x12, local copies, waits for them, and re-layouts: none -> 4.7 us  [the longest x8 4.69 us: local(): hit = sent[g] == jnp.arange(blocks).astype(jnp.float32)]
    ppermute x2 -> x1, starting transfers between devices: 3.84 us -> 1.92 us  [halo(): from_left_y = lax.ppermute(rows[:, 2], 'gy', up_y)]
    ppermute x2 -> x1, waiting for transfers between devices: 0.69 us -> 2.29 us  [halo(): from_left_x = lax.ppermute(grid[2], 'gx', up_x)]
    dot_general x1 -> x0, matrix products: 0.88 us -> none  [local(): outgoing = jnp.einsum('dgb,bra->dgra', pick, payload, precision=HIGHEST)]
  transfers between devices with their start and end apart: 8 -> 8, of which waited for: 3 -> 2; matrix products, arithmetic and copies ran while one was open for 6% -> 14% of each run, Pallas kernels for 0% -> 0%
where the time goes in v11:
time: 77.3 us; the launch traced here: 76.7 us
  starting transfers between devices  32.1 us (42%)
  other arithmetic  24.3 us (31%)
  local copies, waits for them, and re-layouts  8.09 us (10%)
  matrix products  7.27 us (9%)
  waiting for transfers between devices  3.09 us (4%)
  between operations  1.84 us (2%)
    ppermute x1, starting transfers between devices, neighbourhood(): lax.ppermute(own, 'gx', down_x)  10.5 us
    eq x16, other arithmetic, local(): hit = sent[g] == jnp.arange(blocks).astype(jnp.float32)  10.4 us
    ppermute x1, starting transfers between devices, neighbourhood(): lax.ppermute(column, 'gy', down_y)  9.31 us
    ppermute x1, starting transfers between devices, halo(): from_right_y = lax.ppermute(rows[:, 0], 'gy', down_y)  6.68 us
    slice x8, local copies, waits for them, and re-layouts, local(): hit = sent[g] == jnp.arange(blocks).astype(jnp.float32)  4.69 us
    dot_general x8, matrix products, tile_terms(): jnp.einsum('qij,cj->qci', tiles.astype(jnp.bfloat16), other_feat, preferr...  4.19 us
    ppermute x1, waiting for transfers between devices, halo(): from_left_x = lax.ppermute(grid[2], 'gx', up_x)  2.29 us
    ppermute x1, starting transfers between devices, halo(): from_left_y = lax.ppermute(rows[:, 2], 'gy', up_y)  1.92 us
  transfers between devices with their start and end apart: 8, of which 2 were waited for; matrix products, arithmetic and copies ran while one was open for 14% of the time, Pallas kernels for 0%

profile of v11, /device:TPU:1, one launch (start us, length us, event | category | flops | bytes accessed | tf_op | source)
XLA Modules:
  0.0 76.7 jit_solution(8102369752242290121)
XLA Ops:
  0.6 0.7 convert_element_type.224
  1.5 0.7 convert_element_type.223
  2.2 0.7 pad_maximum_fusion.7
  2.9 10.5 %collective-permute-start.1 = (f32[9,128]{1,0:T(8,128)S(1)}, f32[9,128]{1,0:T(8,128)S(1)}, u32[]{:S(2)}, u32[]{:S(2)}) collective-permute-start(f32[9,128]{1,0:T(8,128)S(1)} %get-tuple-element.125), channel_id=1, source_target_pairs={{96,0},{192,96},{288,192},{384,288},{480,384},{576,480},{672,576},... | collective-permute-start | bytes 13832 | tf_op jit(solution)/shard_map/ppermute | solution.py:81
  13.5 0.7 reshape.727
  14.2 1.0 %multiply_bitcast_fusion = (f32[128,128]{1,0:T(8,128)S(1)}, f32[128,128]{1,0:T(8,128)S(1)}, f32[128,128]{1,0:T(8,128)S(1)}, f32[128,128]{1,0:T(8,128)S(1)}) fusion(s32[2,2,128,128]{3,2,1,0:T(8,128)} %param.14), kind=kLoop, calls=%fused_computation.426 | loop fusion | flops 131072 | bytes 524288 | tf_op jit(solution)/shard_map/jvp()/mul | solution.py:41
  15.2 0.7 iota_compare_fusion
  15.9 0.9 %convolution_bitcast_fusion.3 = f32[64,256]{1,0:T(8,128)S(1)} fusion(f32[4,64]{1,0:T(4,128)} %param.16, s32[256]{0:T(256)} %param.12), kind=kOutput, calls=%fused_computation.42 | convolution fusion | flops 787456 | bytes 67584 | tf_op jit(solution)/shard_map/dot_general | solution.py:144
  17.0 0.7 mul.1306
  17.8 1.9 %collective-permute-start.2 = (f32[3,9,128]{2,1,0:T(8,128)S(1)}, f32[3,9,128]{2,1,0:T(8,128)S(1)}, u32[]{:S(2)}, u32[]{:S(2)}) collective-permute-start(f32[3,9,128]{2,1,0:T(8,128)S(1)} %pad_maximum_fusion.2), channel_id=1, source_target_pairs={{0,1},{1,2},{2,3},{3,4},{4,5},{5,6},{6,7},{7,8},{8,9},{9,10},{10,1... | collective-permute-start | bytes 41480 | tf_op jit(solution)/shard_map/ppermute | solution.py:84
  19.8 9.3 %collective-permute-start.3 = (f32[3,9,128]{2,1,0:T(8,128)S(1)}, f32[3,9,128]{2,1,0:T(8,128)S(1)}, u32[]{:S(2)}, u32[]{:S(2)}) collective-permute-start(f32[3,9,128]{2,1,0:T(8,128)S(1)} %pad_maximum_fusion.2), channel_id=1, source_target_pairs={{1,0},{2,1},{3,2},{4,3},{5,4},{6,5},{7,6},{8,7},{9,8},{10,9},{11,1... | collective-permute-start | bytes 41480 | tf_op jit(solution)/shard_map/ppermute | solution.py:84
  30.3 0.7 convert_compare_fusion.13
  32.2 0.7 convert_compare_fusion.3
  34.4 0.7 convert_compare_fusion.15
  36.4 0.7 convert_compare_fusion.11
  38.3 0.7 convert_compare_fusion.9
  40.2 0.7 convert_compare_fusion.7
  57.0 0.9 %fusion.2 = (f32[9,128,128]{2,1,0:T(8,128)S(1)}, f32[4,128,128]{2,1,0:T(8,128)S(1)}, f32[4,128,128]{2,1,0:T(8,128)S(1)}, f32[9,128,128]{2,1,0:T(8,128)S(1)}) fusion(bf16[4,9,128,128]{3,2,1,0:T(8,128)(2,1)S(1)} %bitcast.829, f32[128,128]{1,0:T(8,128)S(1)} %get-tuple-element.70, f32[4,128,128]{2,1,0:T(8,128)S(1)} %get-tuple-element.133, ...), kind=kLoop, calls=%fused_computation.3 | loop fusion | flops 6651904 | bytes 5898240 | tf_op jit(solution)/shard_map/transpose(jvp())/reduce_sum | solution.py:41
  58.1 0.9 %fusion.10 = (f32[9,128,128]{2,1,0:T(8,128)S(1)}, f32[4,128,128]{2,1,0:T(8,128)S(1)}, f32[4,128,128]{2,1,0:T(8,128)S(1)}, f32[9,128,128]{2,1,0:T(8,128)S(1)}) fusion(bf16[4,9,128,128]{3,2,1,0:T(8,128)(2,1)S(1)} %bitcast.827, f32[128,128]{1,0:T(8,128)S(1)} %get-tuple-element.71, f32[4,128,128]{2,1,0:T(8,128)S(1)} %get-tuple-element.135, ...), kind=kLoop, calls=%fused_computation.13 | loop fusion | flops 6651904 | bytes 5898240 | tf_op jit(solution)/shard_map/transpose(jvp())/reduce_sum | solution.py:41
  61.6 1.4 %collective-permute-start.5 = (f32[3,2,3,128]{3,1,2,0:T(2,128)S(1)}, f32[3,2,3,128]{3,1,2,0:T(2,128)S(1)}, u32[]{:S(2)}, u32[]{:S(2)}) collective-permute-start(f32[3,2,3,128]{3,1,2,0:T(2,128)S(1)} %copy.37), channel_id=1, source_target_pairs={{96,0},{192,96},{288,192},{384,288},{480,384},{576,480},{672,576},... | collective-permute-start | bytes 27656 | tf_op jit(solution)/shard_map/ppermute | solution.py:96
  64.1 2.3 %collective-permute-done.4 = f32[3,2,3,128]{3,1,2,0:T(2,128)S(1)} collective-permute-done((f32[3,2,3,128]{3,1,2,0:T(2,128)S(1)}, f32[3,2,3,128]{3,1,2,0:T(2,128)S(1)}, u32[]{:S(2)}, u32[]{:S(2)}) %collective-permute-start.4) | collective-permute-done | bytes 9248 | tf_op jit(solution)/shard_map/ppermute | solution.py:95
  66.4 1.9 %collective-permute-start.6 = (f32[3,2,3,128]{3,0,1,2:T(4,128)S(1)}, f32[3,2,3,128]{3,0,1,2:T(4,128)S(1)}, u32[]{:S(2)}, u32[]{:S(2)}) collective-permute-start(f32[3,2,3,128]{3,0,1,2:T(4,128)S(1)} %get-tuple-element.83), channel_id=1, source_target_pairs={{0,1},{1,2},{2,3},{3,4},{4,5},{5,6},{6,7},{7,8},{8,9},{9,10},{10,1... | collective-permute-start | bytes 27656 | tf_op jit(solution)/shard_map/ppermute | solution.py:98
  68.3 6.7 %collective-permute-start.7 = (f32[3,2,3,128]{3,0,1,2:T(4,128)S(1)}, f32[3,2,3,128]{3,0,1,2:T(4,128)S(1)}, u32[]{:S(2)}, u32[]{:S(2)}) collective-permute-start(f32[3,2,3,128]{3,0,1,2:T(4,128)S(1)} %get-tuple-element.82), channel_id=1, source_target_pairs={{1,0},{2,1},{3,2},{4,3},{5,4},{6,5},{7,6},{8,7},{9,8},{10,9},{11,1... | collective-permute-start | bytes 27656 | tf_op jit(solution)/shard_map/ppermute | solution.py:99
  75.0 0.8 %collective-permute-done.7 = f32[3,2,3,128]{3,0,1,2:T(4,128)S(1)} collective-permute-done((f32[3,2,3,128]{3,0,1,2:T(4,128)S(1)}, f32[3,2,3,128]{3,0,1,2:T(4,128)S(1)}, u32[]{:S(2)}, u32[]{:S(2)}) %collective-permute-start.7) | collective-permute-done | bytes 9248 | tf_op jit(solution)/shard_map/ppermute | solution.py:99
  (216 shorter events, 28.2 us)
Async XLA Ops:
  0.6 52.1 %copy-start = (f32[192,64]{0,1:T(8,128)S(1)}, f32[192,64]{0,1:T(8,128)}, u32[]{:S(2)}) copy-start(f32[192,64]{0,1:T(8,128)} %param.18) | copy-start | bytes 147460
  2.9 14.9 %collective-permute-start.1 = (f32[9,128]{1,0:T(8,128)S(1)}, f32[9,128]{1,0:T(8,128)S(1)}, u32[]{:S(2)}, u32[]{:S(2)}) collective-permute-start(f32[9,128]{1,0:T(8,128)S(1)} %get-tuple-element.125), channel_id=1, source_target_pairs={{96,0},{192,96},{288,192},{384,288},{480,384},{576,480},{672,576},... | collective-permute-start | bytes 13832 | tf_op jit(solution)/shard_map/ppermute | solution.py:81
  13.4 4.4 %collective-permute-start = (f32[9,128]{1,0:T(8,128)S(1)}, f32[9,128]{1,0:T(8,128)S(1)}, u32[]{:S(2)}, u32[]{:S(2)}) collective-permute-start(f32[9,128]{1,0:T(8,128)S(1)} %get-tuple-element.125), channel_id=1, source_target_pairs={{0,96},{96,192},{192,288},{288,384},{384,480},{480,576},{576,672},... | collective-permute-start | bytes 13832 | tf_op jit(solution)/shard_map/ppermute | solution.py:81
  17.8 15.3 %collective-permute-start.2 = (f32[3,9,128]{2,1,0:T(8,128)S(1)}, f32[3,9,128]{2,1,0:T(8,128)S(1)}, u32[]{:S(2)}, u32[]{:S(2)}) collective-permute-start(f32[3,9,128]{2,1,0:T(8,128)S(1)} %pad_maximum_fusion.2), channel_id=1, source_target_pairs={{0,1},{1,2},{2,3},{3,4},{4,5},{5,6},{6,7},{7,8},{8,9},{9,10},{10,1... | collective-permute-start | bytes 41480 | tf_op jit(solution)/shard_map/ppermute | solution.py:84
  19.8 15.4 %collective-permute-start.3 = (f32[3,9,128]{2,1,0:T(8,128)S(1)}, f32[3,9,128]{2,1,0:T(8,128)S(1)}, u32[]{:S(2)}, u32[]{:S(2)}) collective-permute-start(f32[3,9,128]{2,1,0:T(8,128)S(1)} %pad_maximum_fusion.2), channel_id=1, source_target_pairs={{1,0},{2,1},{3,2},{4,3},{5,4},{6,5},{7,6},{8,7},{9,8},{10,9},{11,1... | collective-permute-start | bytes 41480 | tf_op jit(solution)/shard_map/ppermute | solution.py:84
  45.7 0.7 copy-start.1
  51.6 0.7 copy-start.2
  52.3 0.7 copy-start.4
  60.8 15.0 %copy-start.3 = (s32[1,1,8,2]{2,3,1,0:T(2,128)S(1)}, s32[1,1,8,2]{2,3,1,0:T(2,128)}, u32[]{:S(2)}) copy-start(s32[1,1,8,2]{2,3,1,0:T(2,128)} %param.15) | copy-start | bytes 196
  61.6 4.8 %collective-permute-start.5 = (f32[3,2,3,128]{3,1,2,0:T(2,128)S(1)}, f32[3,2,3,128]{3,1,2,0:T(2,128)S(1)}, u32[]{:S(2)}, u32[]{:S(2)}) collective-permute-start(f32[3,2,3,128]{3,1,2,0:T(2,128)S(1)} %copy.37), channel_id=1, source_target_pairs={{96,0},{192,96},{288,192},{384,288},{480,384},{576,480},{672,576},... | collective-permute-start | bytes 27656 | tf_op jit(solution)/shard_map/ppermute | solution.py:96
  63.0 3.4 %collective-permute-start.4 = (f32[3,2,3,128]{3,1,2,0:T(2,128)S(1)}, f32[3,2,3,128]{3,1,2,0:T(2,128)S(1)}, u32[]{:S(2)}, u32[]{:S(2)}) collective-permute-start(f32[3,2,3,128]{3,1,2,0:T(2,128)S(1)} %copy.31), channel_id=1, source_target_pairs={{0,96},{96,192},{192,288},{288,384},{384,480},{480,576},{576,672},... | collective-permute-start | bytes 27656 | tf_op jit(solution)/shard_map/ppermute | solution.py:95
  66.4 8.6 %collective-permute-start.6 = (f32[3,2,3,128]{3,0,1,2:T(4,128)S(1)}, f32[3,2,3,128]{3,0,1,2:T(4,128)S(1)}, u32[]{:S(2)}, u32[]{:S(2)}) collective-permute-start(f32[3,2,3,128]{3,0,1,2:T(4,128)S(1)} %get-tuple-element.83), channel_id=1, source_target_pairs={{0,1},{1,2},{2,3},{3,4},{4,5},{5,6},{6,7},{7,8},{8,9},{9,10},{10,1... | collective-permute-start | bytes 27656 | tf_op jit(solution)/shard_map/ppermute | solution.py:98
  68.3 7.5 %collective-permute-start.7 = (f32[3,2,3,128]{3,0,1,2:T(4,128)S(1)}, f32[3,2,3,128]{3,0,1,2:T(4,128)S(1)}, u32[]{:S(2)}, u32[]{:S(2)}) collective-permute-start(f32[3,2,3,128]{3,0,1,2:T(4,128)S(1)} %get-tuple-element.82), channel_id=1, source_target_pairs={{1,0},{2,1},{3,2},{4,3},{5,4},{6,5},{7,6},{8,7},{9,8},{10,9},{11,1... | collective-permute-start | bytes 27656 | tf_op jit(solution)/shard_map/ppermute | solution.py:99

commit v12 on v3

--- a/solution.py
+++ b/solution.py
@@ -59,8 +59,8 @@
     first = jnp.sum(message[1:4] * message[1:4], axis=0)
     second = jnp.sum(message[4:9] * message[4:9], axis=0)
     invariants = jnp.concatenate([message[0], first, second], axis=0)
-    hidden = jax.nn.silu(jnp.dot(readin.T, invariants, precision=HIGHEST))
-    return jnp.dot(readout, hidden, precision=HIGHEST)
+    hidden = jax.nn.silu(jnp.dot(readin.T, invariants, precision=lax.Precision.HIGH))
+    return jnp.dot(readout, hidden, precision=lax.Precision.HIGH)
 
 
 def select_slots(table, chosen):

time: 61 us -> 60.7 us (level)
  no operation moved by 1% of the time
where the time goes in v12:
time: 60.7 us; the launch traced here: 60.1 us
  starting transfers between devices  34.1 us (56%)
  other arithmetic  11.8 us (19%)
  matrix products  7.91 us (13%)
  local copies, waits for them, and re-layouts  2.34 us (4%)
  waiting for transfers between devices  2.26 us (4%)
  between operations  1.74 us (3%)
    ppermute x2, starting transfers between devices, halo(): from_right_y = lax.ppermute(rows[:, 0], 'gy', down_y)  16.4 us
    ppermute x2, starting transfers between devices, halo(): from_right_x = lax.ppermute(grid[0], 'gx', down_x)  13.9 us
    dot_general x8, matrix products, tile_terms(): jnp.einsum('qij,cj->qci', tiles.astype(jnp.bfloat16), other_feat, preferr...  4.2 us
    ppermute x2, starting transfers between devices, halo(): from_left_y = lax.ppermute(rows[:, 2], 'gy', up_y)  3.84 us
    reduce_sum x2, other arithmetic, tile_terms(): basis[:, None] * angular[None] * weight[None, None]  1.88 us
    ppermute x2, waiting for transfers between devices, halo(): from_right_y = lax.ppermute(rows[:, 0], 'gy', down_y)  1.56 us
    convert_element_type x4, other arithmetic, tile_terms(): tiles.astype(jnp.bfloat16)  1.39 us
    dot_general x2, matrix products, features(): return jnp.dot(embedding.T, onehot, precision=HIGHEST)  1.36 us
  transfers between devices with their start and end apart: 8, of which 3 were waited for; matrix products, arithmetic and copies ran while one was open for 6% of the time, Pallas kernels for 0%

profile of v12, /device:TPU:1, one launch (start us, length us, event | category | flops | bytes accessed | tf_op | source)
XLA Modules:
  0.0 60.1 jit_solution(1753697148068362471)
XLA Ops:
  0.7 0.7 %convert_bitcast_fusion = f32[2,1,128]{2,0,1:T(2,128)S(1)} fusion(s32[256]{0:T(256)} %param.10), kind=kLoop, calls=%fused_computation.514 | loop fusion | flops 256 | bytes 2048 | tf_op jit(solution)/shard_map/convert_element_type | solution.py:106
  1.4 0.7 %reshape.507 = f32[3,2,128]{2,1,0:T(2,128)S(1)} reshape(f32[3,256]{1,0:T(4,128)} %param.9) | data formatting | bytes 6144 | tf_op jit(solution)/shard_map/reshape | solution.py:105
  2.1 0.9 %fusion.241 = f32[8,2,4,128]{3,0,2,1:T(8,128)S(1)} fusion(f32[2,1,128]{2,0,1:T(2,128)S(1)} %convert_bitcast_fusion, f32[2,3,128]{2,0,1:T(2,128)S(1)} %bitcast.786, s32[8,2]{0,1:T(2,128)} %bitcast.814), kind=kOutput, calls=%fused_computation.492 | convolution fusion | flops 197664 | bytes 36928 | tf_op jit(solution)/shard_map/dgb,bra->dgra/dot_general | solution.py:110
  3.0 10.5 %collective-permute-start.1 = (f32[3,2,4,128]{3,0,2,1:T(4,128)S(1)}, f32[3,2,4,128]{3,0,2,1:T(4,128)S(1)}, u32[]{:S(2)}, u32[]{:S(2)}) collective-permute-start(f32[3,2,4,128]{3,0,2,1:T(4,128)S(1)} %get-tuple-element.57), channel_id=1, source_target_pairs={{96,0},{192,96},{288,192},{384,288},{480,384},{576,480},{672,576},... | collective-permute-start | bytes 36872 | tf_op jit(solution)/shard_map/ppermute | solution.py:81
  13.6 1.0 %multiply_bitcast_fusion = (f32[128,128]{1,0:T(8,128)S(1)}, f32[128,128]{1,0:T(8,128)S(1)}, f32[128,128]{1,0:T(8,128)S(1)}, f32[128,128]{1,0:T(8,128)S(1)}) fusion(s32[2,2,128,128]{3,2,1,0:T(8,128)} %param.12), kind=kLoop, calls=%fused_computation.418 | loop fusion | flops 131072 | bytes 524288 | tf_op jit(solution)/shard_map/jvp()/mul | solution.py:41
  14.5 0.7 %iota_compare_fusion = pred[2,2,18]{1,2,0:T(8,128)(4,1)S(1)} fusion(s32[2,2]{1,0:T(2,128)} %param.11), kind=kLoop, calls=%fused_computation.460 | loop fusion | flops 72 | bytes 88 | tf_op jit(solution)/shard_map/jvp()/eq | solution.py:68
  15.4 0.9 %convolution_bitcast_fusion.3 = f32[64,256]{1,0:T(8,128)S(1)} fusion(f32[4,64]{1,0:T(4,128)} %param.14, s32[256]{0:T(256)} %param.10), kind=kOutput, calls=%fused_computation.42 | convolution fusion | flops 787456 | bytes 67584 | tf_op jit(solution)/shard_map/dot_general | solution.py:117
  16.5 1.9 %collective-permute-start.2 = (f32[3,2,4,128]{3,2,1,0:T(4,128)S(1)}, f32[3,2,4,128]{3,2,1,0:T(4,128)S(1)}, u32[]{:S(2)}, u32[]{:S(2)}) collective-permute-start(f32[3,2,4,128]{3,2,1,0:T(4,128)S(1)} %get-tuple-element.55), channel_id=1, source_target_pairs={{0,1},{1,2},{2,3},{3,4},{4,5},{5,6},{6,7},{7,8},{8,9},{9,10},{10,1... | collective-permute-start | bytes 36872 | tf_op jit(solution)/shard_map/ppermute | solution.py:83
  18.6 9.3 %collective-permute-start.3 = (f32[3,2,4,128]{3,2,1,0:T(4,128)S(1)}, f32[3,2,4,128]{3,2,1,0:T(4,128)S(1)}, u32[]{:S(2)}, u32[]{:S(2)}) collective-permute-start(f32[3,2,4,128]{3,2,1,0:T(4,128)S(1)} %get-tuple-element.54), channel_id=1, source_target_pairs={{1,0},{2,1},{3,2},{4,3},{5,4},{6,5},{7,6},{8,7},{9,8},{10,9},{11,1... | collective-permute-start | bytes 36872 | tf_op jit(solution)/shard_map/ppermute | solution.py:84
  28.0 0.8 %collective-permute-done.3 = f32[3,2,4,128]{3,2,1,0:T(4,128)S(1)} collective-permute-done((f32[3,2,4,128]{3,2,1,0:T(4,128)S(1)}, f32[3,2,4,128]{3,2,1,0:T(4,128)S(1)}, u32[]{:S(2)}, u32[]{:S(2)}) %collective-permute-start.3) | collective-permute-done | bytes 12320 | tf_op jit(solution)/shard_map/ppermute | solution.py:84
  32.1 0.5 fusion.236
  33.0 0.5 fusion.237
  34.2 0.5 convolution_add_fusion.1
  35.1 0.5 convolution_add_fusion
  39.6 0.5 convolution_convert_fusion.1
  40.1 0.9 %fusion.2 = (f32[9,128,128]{2,1,0:T(8,128)S(1)}, f32[4,128,128]{2,1,0:T(8,128)S(1)}, f32[4,128,128]{2,1,0:T(8,128)S(1)}, f32[9,128,128]{2,1,0:T(8,128)S(1)}) fusion(bf16[4,9,128,128]{3,2,1,0:T(8,128)(2,1)S(1)} %bitcast.778, f32[128,128]{1,0:T(8,128)S(1)} %get-tuple-element.42, f32[4,128,128]{2,1,0:T(8,128)S(1)} %get-tuple-element.81, ...), kind=kLoop, calls=%fused_computation.3 | loop fusion | flops 6651904 | bytes 5898240 | tf_op jit(solution)/shard_map/transpose(jvp())/reduce_sum | solution.py:41
  41.2 0.9 %fusion.10 = (f32[9,128,128]{2,1,0:T(8,128)S(1)}, f32[4,128,128]{2,1,0:T(8,128)S(1)}, f32[4,128,128]{2,1,0:T(8,128)S(1)}, f32[9,128,128]{2,1,0:T(8,128)S(1)}) fusion(bf16[4,9,128,128]{3,2,1,0:T(8,128)(2,1)S(1)} %bitcast.776, f32[128,128]{1,0:T(8,128)S(1)} %get-tuple-element.43, f32[4,128,128]{2,1,0:T(8,128)S(1)} %get-tuple-element.83, ...), kind=kLoop, calls=%fused_computation.13 | loop fusion | flops 6651904 | bytes 5898240 | tf_op jit(solution)/shard_map/transpose(jvp())/reduce_sum | solution.py:41
  44.7 3.3 %collective-permute-start.5 = (f32[3,2,3,128]{3,1,2,0:T(2,128)S(1)}, f32[3,2,3,128]{3,1,2,0:T(2,128)S(1)}, u32[]{:S(2)}, u32[]{:S(2)}) collective-permute-start(f32[3,2,3,128]{3,1,2,0:T(2,128)S(1)} %copy.46), channel_id=1, source_target_pairs={{96,0},{192,96},{288,192},{384,288},{480,384},{576,480},{672,576},... | collective-permute-start | bytes 27656 | tf_op jit(solution)/shard_map/ppermute | solution.py:81
  48.1 0.6 maximum_bitcast_fusion.4
  48.7 0.7 %collective-permute-done.4 = f32[3,2,3,128]{3,1,2,0:T(2,128)S(1)} collective-permute-done((f32[3,2,3,128]{3,1,2,0:T(2,128)S(1)}, f32[3,2,3,128]{3,1,2,0:T(2,128)S(1)}, u32[]{:S(2)}, u32[]{:S(2)}) %collective-permute-start.4) | collective-permute-done | bytes 9248 | tf_op jit(solution)/shard_map/ppermute | solution.py:80
  49.4 1.9 %collective-permute-start.6 = (f32[3,2,3,128]{3,0,1,2:T(4,128)S(1)}, f32[3,2,3,128]{3,0,1,2:T(4,128)S(1)}, u32[]{:S(2)}, u32[]{:S(2)}) collective-permute-start(f32[3,2,3,128]{3,0,1,2:T(4,128)S(1)} %get-tuple-element.61), channel_id=1, source_target_pairs={{0,1},{1,2},{2,3},{3,4},{4,5},{5,6},{6,7},{7,8},{8,9},{9,10},{10,1... | collective-permute-start | bytes 27656 | tf_op jit(solution)/shard_map/ppermute | solution.py:83
  51.4 7.0 %collective-permute-start.7 = (f32[3,2,3,128]{3,0,1,2:T(4,128)S(1)}, f32[3,2,3,128]{3,0,1,2:T(4,128)S(1)}, u32[]{:S(2)}, u32[]{:S(2)}) collective-permute-start(f32[3,2,3,128]{3,0,1,2:T(4,128)S(1)} %get-tuple-element.60), channel_id=1, source_target_pairs={{1,0},{2,1},{3,2},{4,3},{5,4},{6,5},{7,6},{8,7},{9,8},{10,9},{11,1... | collective-permute-start | bytes 27656 | tf_op jit(solution)/shard_map/ppermute | solution.py:84
  58.5 0.8 %collective-permute-done.7 = f32[3,2,3,128]{3,0,1,2:T(4,128)S(1)} collective-permute-done((f32[3,2,3,128]{3,0,1,2:T(4,128)S(1)}, f32[3,2,3,128]{3,0,1,2:T(4,128)S(1)}, u32[]{:S(2)}, u32[]{:S(2)}) %collective-permute-start.7) | collective-permute-done | bytes 9248 | tf_op jit(solution)/shard_map/ppermute | solution.py:84
  59.5 0.6 %copy.81 = f32[1,3,2,128]{3,1,2,0:T(4,128)} copy(f32[1,3,2,128]{3,2,1,0:T(2,128)S(1)} %fusion.22) | data formatting | bytes 6144
  (173 shorter events, 11.5 us)
Async XLA Ops:
  0.6 35.5 %copy-start = (f32[192,64]{0,1:T(8,128)S(1)}, f32[192,64]{0,1:T(8,128)}, u32[]{:S(2)}) copy-start(f32[192,64]{0,1:T(8,128)} %param.16) | copy-start | bytes 147460
  0.6 17.9 %copy-start.2 = (f32[4,64]{1,0:T(4,128)S(1)}, f32[4,64]{1,0:T(4,128)}, u32[]{:S(2)}) copy-start(f32[4,64]{1,0:T(4,128)} %param.15) | copy-start | bytes 3076
  3.0 13.4 %collective-permute-start.1 = (f32[3,2,4,128]{3,0,2,1:T(4,128)S(1)}, f32[3,2,4,128]{3,0,2,1:T(4,128)S(1)}, u32[]{:S(2)}, u32[]{:S(2)}) collective-permute-start(f32[3,2,4,128]{3,0,2,1:T(4,128)S(1)} %get-tuple-element.57), channel_id=1, source_target_pairs={{96,0},{192,96},{288,192},{384,288},{480,384},{576,480},{672,576},... | collective-permute-start | bytes 36872 | tf_op jit(solution)/shard_map/ppermute | solution.py:81
  13.5 2.9 %collective-permute-start = (f32[3,2,4,128]{3,2,1,0:T(4,128)S(1)}, f32[3,2,4,128]{3,2,1,0:T(4,128)S(1)}, u32[]{:S(2)}, u32[]{:S(2)}) collective-permute-start(f32[3,2,4,128]{3,2,1,0:T(4,128)S(1)} %copy.65), channel_id=1, source_target_pairs={{0,96},{96,192},{192,288},{288,384},{384,480},{480,576},{576,672},... | collective-permute-start | bytes 36872 | tf_op jit(solution)/shard_map/ppermute | solution.py:80
  16.5 11.5 %collective-permute-start.2 = (f32[3,2,4,128]{3,2,1,0:T(4,128)S(1)}, f32[3,2,4,128]{3,2,1,0:T(4,128)S(1)}, u32[]{:S(2)}, u32[]{:S(2)}) collective-permute-start(f32[3,2,4,128]{3,2,1,0:T(4,128)S(1)} %get-tuple-element.55), channel_id=1, source_target_pairs={{0,1},{1,2},{2,3},{3,4},{4,5},{5,6},{6,7},{7,8},{8,9},{9,10},{10,1... | collective-permute-start | bytes 36872 | tf_op jit(solution)/shard_map/ppermute | solution.py:83
  18.6 10.1 %collective-permute-start.3 = (f32[3,2,4,128]{3,2,1,0:T(4,128)S(1)}, f32[3,2,4,128]{3,2,1,0:T(4,128)S(1)}, u32[]{:S(2)}, u32[]{:S(2)}) collective-permute-start(f32[3,2,4,128]{3,2,1,0:T(4,128)S(1)} %get-tuple-element.54), channel_id=1, source_target_pairs={{1,0},{2,1},{3,2},{4,3},{5,4},{6,5},{7,6},{8,7},{9,8},{10,9},{11,1... | collective-permute-start | bytes 36872 | tf_op jit(solution)/shard_map/ppermute | solution.py:84
  29.2 0.7 %copy-start.1 = (f32[4,64]{1,0:T(4,128)S(1)}, f32[4,64]{1,0:T(4,128)}, u32[]{:S(2)}) copy-start(f32[4,64]{1,0:T(4,128)} %param.14) | copy-start | bytes 3076
  35.6 0.7 %copy-start.4 = (f32[64]{0:T(128)S(1)}, f32[64]{0:T(128)}, u32[]{:S(2)}) copy-start(f32[64]{0:T(128)} %param.17) | copy-start | bytes 772
  43.9 15.4 %copy-start.3 = (s32[1,1,8,2]{2,3,1,0:T(2,128)S(1)}, s32[1,1,8,2]{2,3,1,0:T(2,128)}, u32[]{:S(2)}) copy-start(s32[1,1,8,2]{2,3,1,0:T(2,128)} %param.13) | copy-start | bytes 196
  44.7 4.8 %collective-permute-start.5 = (f32[3,2,3,128]{3,1,2,0:T(2,128)S(1)}, f32[3,2,3,128]{3,1,2,0:T(2,128)S(1)}, u32[]{:S(2)}, u32[]{:S(2)}) collective-permute-start(f32[3,2,3,128]{3,1,2,0:T(2,128)S(1)} %copy.46), channel_id=1, source_target_pairs={{96,0},{192,96},{288,192},{384,288},{480,384},{576,480},{672,576},... | collective-permute-start | bytes 27656 | tf_op jit(solution)/shard_map/ppermute | solution.py:81
  48.0 1.4 %collective-permute-start.4 = (f32[3,2,3,128]{3,1,2,0:T(2,128)S(1)}, f32[3,2,3,128]{3,1,2,0:T(2,128)S(1)}, u32[]{:S(2)}, u32[]{:S(2)}) collective-permute-start(f32[3,2,3,128]{3,1,2,0:T(2,128)S(1)} %copy.40), channel_id=1, source_target_pairs={{0,96},{96,192},{192,288},{288,384},{384,480},{480,576},{576,672},... | collective-permute-start | bytes 27656 | tf_op jit(solution)/shard_map/ppermute | solution.py:80
  49.4 9.0 %collective-permute-start.6 = (f32[3,2,3,128]{3,0,1,2:T(4,128)S(1)}, f32[3,2,3,128]{3,0,1,2:T(4,128)S(1)}, u32[]{:S(2)}, u32[]{:S(2)}) collective-permute-start(f32[3,2,3,128]{3,0,1,2:T(4,128)S(1)} %get-tuple-element.61), channel_id=1, source_target_pairs={{0,1},{1,2},{2,3},{3,4},{4,5},{5,6},{6,7},{7,8},{8,9},{9,10},{10,1... | collective-permute-start | bytes 27656 | tf_op jit(solution)/shard_map/ppermute | solution.py:83
  51.4 7.9 %collective-permute-start.7 = (f32[3,2,3,128]{3,0,1,2:T(4,128)S(1)}, f32[3,2,3,128]{3,0,1,2:T(4,128)S(1)}, u32[]{:S(2)}, u32[]{:S(2)}) collective-permute-start(f32[3,2,3,128]{3,0,1,2:T(4,128)S(1)} %get-tuple-element.60), channel_id=1, source_target_pairs={{1,0},{2,1},{3,2},{4,3},{5,4},{6,5},{7,6},{8,7},{9,8},{10,9},{11,1... | collective-permute-start | bytes 27656 | tf_op jit(solution)/shard_map/ppermute | solution.py:84

commit v13 on v12

--- a/solution.py
+++ b/solution.py
@@ -113,8 +113,8 @@
     ghost_kind = incoming[:, 3]
 
     def features(kind):
-        onehot = (kind[None, :] == jnp.arange(kinds).astype(kind.dtype)[:, None]).astype(jnp.float32)
-        return jnp.dot(embedding.T, onehot, precision=HIGHEST)
+        hit = kind[None, None, :] == jnp.arange(kinds).astype(kind.dtype)[:, None, None]
+        return jnp.sum(jnp.where(hit, embedding[:, :, None], 0.0), axis=0)
 
     own_feats32 = features(species).reshape(-1, blocks, atoms).transpose(1, 0, 2)
     ghost_feats32 = (

time: 60.7 us -> 60.8 us (level)
  other arithmetic: 11.8 us -> 13.6 us
  matrix products: 7.91 us -> 6.55 us
  starting transfers between devices: 34.1 us -> 33.4 us
    dot_general x2 -> x0, matrix products: 1.36 us -> none  [features(): return jnp.dot(embedding.T, onehot, precision=HIGHEST)]
    reduce_sum x0 -> x2, other arithmetic: none -> 1.06 us  [features(): return jnp.sum(jnp.where(hit, embedding[:, :, None], 0.0), axis=0)]
    eq x0 -> x2, other arithmetic: none -> 0.77 us  [features(): kind[None, None, :] == jnp.arange(kinds).astype(kind.dtype)[:, None, None]]
  transfers between devices with their start and end apart: 8 -> 8, of which waited for: 3 -> 3; matrix products, arithmetic and copies ran while one was open for 6% -> 7% of each run, Pallas kernels for 0% -> 0%
where the time goes in v13:
time: 60.8 us; the launch traced here: 60.4 us
  starting transfers between devices  33.4 us (55%)
  other arithmetic  13.6 us (22%)
  matrix products  6.55 us (11%)
  waiting for transfers between devices  2.79 us (5%)
  local copies, waits for them, and re-layouts  2.26 us (4%)
  between operations  1.74 us (3%)
    ppermute x2, starting transfers between devices, halo(): from_right_y = lax.ppermute(rows[:, 0], 'gy', down_y)  16.3 us
    ppermute x2, starting transfers between devices, halo(): from_right_x = lax.ppermute(grid[0], 'gx', down_x)  13.3 us
    dot_general x8, matrix products, tile_terms(): jnp.einsum('qij,cj->qci', tiles.astype(jnp.bfloat16), other_feat, preferr...  4.19 us
    ppermute x2, starting transfers between devices, halo(): from_left_y = lax.ppermute(rows[:, 2], 'gy', up_y)  3.84 us
    reduce_sum x2, other arithmetic, tile_terms(): basis[:, None] * angular[None] * weight[None, None]  1.88 us
    ppermute x2, waiting for transfers between devices, halo(): from_right_y = lax.ppermute(rows[:, 0], 'gy', down_y)  1.56 us
    convert_element_type x4, other arithmetic, tile_terms(): tiles.astype(jnp.bfloat16)  1.39 us
    ppermute x2, waiting for transfers between devices, halo(): from_left_x = lax.ppermute(grid[2], 'gx', up_x)  1.22 us
  transfers between devices with their start and end apart: 8, of which 3 were waited for; matrix products, arithmetic and copies ran while one was open for 7% of the time, Pallas kernels for 0%

profile of v13, /device:TPU:1, one launch (start us, length us, event | category | flops | bytes accessed | tf_op | source)
XLA Modules:
  0.0 60.4 jit_solution(10218121994473406526)
XLA Ops:
  0.7 0.7 %convert_bitcast_fusion = f32[2,1,128]{2,0,1:T(2,128)S(1)} fusion(s32[256]{0:T(256)} %param.10), kind=kLoop, calls=%fused_computation.511 | loop fusion | flops 256 | bytes 2048 | tf_op jit(solution)/shard_map/convert_element_type | solution.py:106
  1.4 0.7 %reshape.557 = f32[3,2,128]{2,1,0:T(2,128)S(1)} reshape(f32[3,256]{1,0:T(4,128)} %param.9) | data formatting | bytes 6144 | tf_op jit(solution)/shard_map/reshape | solution.py:105
  2.1 0.9 %fusion.238 = f32[8,2,4,128]{3,0,2,1:T(8,128)S(1)} fusion(f32[2,1,128]{2,0,1:T(2,128)S(1)} %convert_bitcast_fusion, f32[2,3,128]{2,0,1:T(2,128)S(1)} %bitcast.781, s32[8,2]{0,1:T(2,128)} %bitcast.809), kind=kOutput, calls=%fused_computation.490 | convolution fusion | flops 197664 | bytes 36928 | tf_op jit(solution)/shard_map/dgb,bra->dgra/dot_general | solution.py:110
  3.0 10.5 %collective-permute-start.1 = (f32[3,2,4,128]{3,0,2,1:T(4,128)S(1)}, f32[3,2,4,128]{3,0,2,1:T(4,128)S(1)}, u32[]{:S(2)}, u32[]{:S(2)}) collective-permute-start(f32[3,2,4,128]{3,0,2,1:T(4,128)S(1)} %get-tuple-element.57), channel_id=1, source_target_pairs={{96,0},{192,96},{288,192},{384,288},{480,384},{576,480},{672,576},... | collective-permute-start | bytes 36872 | tf_op jit(solution)/shard_map/ppermute | solution.py:81
  13.5 0.7 %iota_compare_fusion.1 = pred[4,256]{1,0:T(4,128)(4,1)S(1)} fusion(s32[256]{0:T(256)} %param.10), kind=kLoop, calls=%fused_computation.493 | loop fusion | flops 1024 | bytes 2048 | tf_op jit(solution)/shard_map/eq | solution.py:116
  14.3 1.0 %multiply_bitcast_fusion = (f32[128,128]{1,0:T(8,128)S(1)}, f32[128,128]{1,0:T(8,128)S(1)}, f32[128,128]{1,0:T(8,128)S(1)}, f32[128,128]{1,0:T(8,128)S(1)}) fusion(s32[2,2,128,128]{3,2,1,0:T(8,128)} %param.12), kind=kLoop, calls=%fused_computation.418 | loop fusion | flops 131072 | bytes 524288 | tf_op jit(solution)/shard_map/jvp()/mul | solution.py:41
  15.2 0.7 %iota_compare_fusion = pred[2,2,18]{1,2,0:T(8,128)(4,1)S(1)} fusion(s32[2,2]{1,0:T(2,128)} %param.11), kind=kLoop, calls=%fused_computation.459 | loop fusion | flops 72 | bytes 88 | tf_op jit(solution)/shard_map/jvp()/eq | solution.py:68
  16.1 0.8 %select_reduce_fusion.2 = f32[64,256]{1,0:T(8,128)S(1)} fusion(f32[4,64]{1,0:T(4,128)} %param.14, pred[4,256]{1,0:T(4,128)(4,1)S(1)} %iota_compare_fusion.1), kind=kLoop, calls=%fused_computation.89 | loop fusion | flops 114688 | bytes 67584 | tf_op jit(solution)/shard_map/reduce_sum | solution.py:117
  17.0 1.9 %collective-permute-start.2 = (f32[3,2,4,128]{3,2,1,0:T(4,128)S(1)}, f32[3,2,4,128]{3,2,1,0:T(4,128)S(1)}, u32[]{:S(2)}, u32[]{:S(2)}) collective-permute-start(f32[3,2,4,128]{3,2,1,0:T(4,128)S(1)} %get-tuple-element.55), channel_id=1, source_target_pairs={{0,1},{1,2},{2,3},{3,4},{4,5},{5,6},{6,7},{7,8},{8,9},{9,10},{10,1... | collective-permute-start | bytes 36872 | tf_op jit(solution)/shard_map/ppermute | solution.py:83
  19.2 9.3 %collective-permute-start.3 = (f32[3,2,4,128]{3,2,1,0:T(4,128)S(1)}, f32[3,2,4,128]{3,2,1,0:T(4,128)S(1)}, u32[]{:S(2)}, u32[]{:S(2)}) collective-permute-start(f32[3,2,4,128]{3,2,1,0:T(4,128)S(1)} %get-tuple-element.54), channel_id=1, source_target_pairs={{1,0},{2,1},{3,2},{4,3},{5,4},{6,5},{7,6},{8,7},{9,8},{10,9},{11,1... | collective-permute-start | bytes 36872 | tf_op jit(solution)/shard_map/ppermute | solution.py:84
  28.5 0.8 %collective-permute-done.3 = f32[3,2,4,128]{3,2,1,0:T(4,128)S(1)} collective-permute-done((f32[3,2,4,128]{3,2,1,0:T(4,128)S(1)}, f32[3,2,4,128]{3,2,1,0:T(4,128)S(1)}, u32[]{:S(2)}, u32[]{:S(2)}) %collective-permute-start.3) | collective-permute-done | bytes 12320 | tf_op jit(solution)/shard_map/ppermute | solution.py:84
  32.5 0.5 fusion.233
  33.4 0.5 fusion.234
  34.6 0.5 convolution_add_fusion.1
  35.5 0.5 convolution_add_fusion
  40.5 0.9 %fusion.2 = (f32[9,128,128]{2,1,0:T(8,128)S(1)}, f32[4,128,128]{2,1,0:T(8,128)S(1)}, f32[4,128,128]{2,1,0:T(8,128)S(1)}, f32[9,128,128]{2,1,0:T(8,128)S(1)}) fusion(bf16[4,9,128,128]{3,2,1,0:T(8,128)(2,1)S(1)} %bitcast.772, f32[128,128]{1,0:T(8,128)S(1)} %get-tuple-element.42, f32[4,128,128]{2,1,0:T(8,128)S(1)} %get-tuple-element.81, ...), kind=kLoop, calls=%fused_computation.3 | loop fusion | flops 6651904 | bytes 5898240 | tf_op jit(solution)/shard_map/transpose(jvp())/reduce_sum | solution.py:41
  41.6 0.9 %fusion.10 = (f32[9,128,128]{2,1,0:T(8,128)S(1)}, f32[4,128,128]{2,1,0:T(8,128)S(1)}, f32[4,128,128]{2,1,0:T(8,128)S(1)}, f32[9,128,128]{2,1,0:T(8,128)S(1)}) fusion(bf16[4,9,128,128]{3,2,1,0:T(8,128)(2,1)S(1)} %bitcast.770, f32[128,128]{1,0:T(8,128)S(1)} %get-tuple-element.43, f32[4,128,128]{2,1,0:T(8,128)S(1)} %get-tuple-element.83, ...), kind=kLoop, calls=%fused_computation.13 | loop fusion | flops 6651904 | bytes 5898240 | tf_op jit(solution)/shard_map/transpose(jvp())/reduce_sum | solution.py:41
  45.0 2.8 %collective-permute-start.5 = (f32[3,2,3,128]{3,1,2,0:T(2,128)S(1)}, f32[3,2,3,128]{3,1,2,0:T(2,128)S(1)}, u32[]{:S(2)}, u32[]{:S(2)}) collective-permute-start(f32[3,2,3,128]{3,1,2,0:T(2,128)S(1)} %copy.45), channel_id=1, source_target_pairs={{96,0},{192,96},{288,192},{384,288},{480,384},{576,480},{672,576},... | collective-permute-start | bytes 27656 | tf_op jit(solution)/shard_map/ppermute | solution.py:81
  47.9 0.6 maximum_bitcast_fusion.4
  48.6 1.2 %collective-permute-done.4 = f32[3,2,3,128]{3,1,2,0:T(2,128)S(1)} collective-permute-done((f32[3,2,3,128]{3,1,2,0:T(2,128)S(1)}, f32[3,2,3,128]{3,1,2,0:T(2,128)S(1)}, u32[]{:S(2)}, u32[]{:S(2)}) %collective-permute-start.4) | collective-permute-done | bytes 9248 | tf_op jit(solution)/shard_map/ppermute | solution.py:80
  49.8 1.9 %collective-permute-start.6 = (f32[3,2,3,128]{3,0,1,2:T(4,128)S(1)}, f32[3,2,3,128]{3,0,1,2:T(4,128)S(1)}, u32[]{:S(2)}, u32[]{:S(2)}) collective-permute-start(f32[3,2,3,128]{3,0,1,2:T(4,128)S(1)} %get-tuple-element.61), channel_id=1, source_target_pairs={{0,1},{1,2},{2,3},{3,4},{4,5},{5,6},{6,7},{7,8},{8,9},{9,10},{10,1... | collective-permute-start | bytes 27656 | tf_op jit(solution)/shard_map/ppermute | solution.py:83
  51.8 7.0 %collective-permute-start.7 = (f32[3,2,3,128]{3,0,1,2:T(4,128)S(1)}, f32[3,2,3,128]{3,0,1,2:T(4,128)S(1)}, u32[]{:S(2)}, u32[]{:S(2)}) collective-permute-start(f32[3,2,3,128]{3,0,1,2:T(4,128)S(1)} %get-tuple-element.60), channel_id=1, source_target_pairs={{1,0},{2,1},{3,2},{4,3},{5,4},{6,5},{7,6},{8,7},{9,8},{10,9},{11,1... | collective-permute-start | bytes 27656 | tf_op jit(solution)/shard_map/ppermute | solution.py:84
  58.7 0.8 %collective-permute-done.7 = f32[3,2,3,128]{3,0,1,2:T(4,128)S(1)} collective-permute-done((f32[3,2,3,128]{3,0,1,2:T(4,128)S(1)}, f32[3,2,3,128]{3,0,1,2:T(4,128)S(1)}, u32[]{:S(2)}, u32[]{:S(2)}) %collective-permute-start.7) | collective-permute-done | bytes 9248 | tf_op jit(solution)/shard_map/ppermute | solution.py:84
  59.8 0.6 copy.80
  (175 shorter events, 11.9 us)
Async XLA Ops:
  0.6 35.8 %copy-start = (f32[192,64]{0,1:T(8,128)S(1)}, f32[192,64]{0,1:T(8,128)}, u32[]{:S(2)}) copy-start(f32[192,64]{0,1:T(8,128)} %param.16) | copy-start | bytes 147460
  0.6 18.5 %copy-start.2 = (f32[4,64]{1,0:T(4,128)S(1)}, f32[4,64]{1,0:T(4,128)}, u32[]{:S(2)}) copy-start(f32[4,64]{1,0:T(4,128)} %param.15) | copy-start | bytes 3076
  3.0 14.0 %collective-permute-start.1 = (f32[3,2,4,128]{3,0,2,1:T(4,128)S(1)}, f32[3,2,4,128]{3,0,2,1:T(4,128)S(1)}, u32[]{:S(2)}, u32[]{:S(2)}) collective-permute-start(f32[3,2,4,128]{3,0,2,1:T(4,128)S(1)} %get-tuple-element.57), channel_id=1, source_target_pairs={{96,0},{192,96},{288,192},{384,288},{480,384},{576,480},{672,576},... | collective-permute-start | bytes 36872 | tf_op jit(solution)/shard_map/ppermute | solution.py:81
  13.5 3.5 %collective-permute-start = (f32[3,2,4,128]{3,2,1,0:T(4,128)S(1)}, f32[3,2,4,128]{3,2,1,0:T(4,128)S(1)}, u32[]{:S(2)}, u32[]{:S(2)}) collective-permute-start(f32[3,2,4,128]{3,2,1,0:T(4,128)S(1)} %copy.64), channel_id=1, source_target_pairs={{0,96},{96,192},{192,288},{288,384},{384,480},{480,576},{576,672},... | collective-permute-start | bytes 36872 | tf_op jit(solution)/shard_map/ppermute | solution.py:80
  17.0 11.5 %collective-permute-start.2 = (f32[3,2,4,128]{3,2,1,0:T(4,128)S(1)}, f32[3,2,4,128]{3,2,1,0:T(4,128)S(1)}, u32[]{:S(2)}, u32[]{:S(2)}) collective-permute-start(f32[3,2,4,128]{3,2,1,0:T(4,128)S(1)} %get-tuple-element.55), channel_id=1, source_target_pairs={{0,1},{1,2},{2,3},{3,4},{4,5},{5,6},{6,7},{7,8},{8,9},{9,10},{10,1... | collective-permute-start | bytes 36872 | tf_op jit(solution)/shard_map/ppermute | solution.py:83
  19.2 10.1 %collective-permute-start.3 = (f32[3,2,4,128]{3,2,1,0:T(4,128)S(1)}, f32[3,2,4,128]{3,2,1,0:T(4,128)S(1)}, u32[]{:S(2)}, u32[]{:S(2)}) collective-permute-start(f32[3,2,4,128]{3,2,1,0:T(4,128)S(1)} %get-tuple-element.54), channel_id=1, source_target_pairs={{1,0},{2,1},{3,2},{4,3},{5,4},{6,5},{7,6},{8,7},{9,8},{10,9},{11,1... | collective-permute-start | bytes 36872 | tf_op jit(solution)/shard_map/ppermute | solution.py:84
  29.8 0.7 %copy-start.1 = (f32[4,64]{1,0:T(4,128)S(1)}, f32[4,64]{1,0:T(4,128)}, u32[]{:S(2)}) copy-start(f32[4,64]{1,0:T(4,128)} %param.14) | copy-start | bytes 3076
  36.0 0.7 %copy-start.4 = (f32[64]{0:T(128)S(1)}, f32[64]{0:T(128)}, u32[]{:S(2)}) copy-start(f32[64]{0:T(128)} %param.17) | copy-start | bytes 772
  44.3 15.3 %copy-start.3 = (s32[1,1,8,2]{2,3,1,0:T(2,128)S(1)}, s32[1,1,8,2]{2,3,1,0:T(2,128)}, u32[]{:S(2)}) copy-start(s32[1,1,8,2]{2,3,1,0:T(2,128)} %param.13) | copy-start | bytes 196
  45.0 4.7 %collective-permute-start.5 = (f32[3,2,3,128]{3,1,2,0:T(2,128)S(1)}, f32[3,2,3,128]{3,1,2,0:T(2,128)S(1)}, u32[]{:S(2)}, u32[]{:S(2)}) collective-permute-start(f32[3,2,3,128]{3,1,2,0:T(2,128)S(1)} %copy.45), channel_id=1, source_target_pairs={{96,0},{192,96},{288,192},{384,288},{480,384},{576,480},{672,576},... | collective-permute-start | bytes 27656 | tf_op jit(solution)/shard_map/ppermute | solution.py:81
  47.9 1.9 %collective-permute-start.4 = (f32[3,2,3,128]{3,1,2,0:T(2,128)S(1)}, f32[3,2,3,128]{3,1,2,0:T(2,128)S(1)}, u32[]{:S(2)}, u32[]{:S(2)}) collective-permute-start(f32[3,2,3,128]{3,1,2,0:T(2,128)S(1)} %copy.39), channel_id=1, source_target_pairs={{0,96},{96,192},{192,288},{288,384},{384,480},{480,576},{576,672},... | collective-permute-start | bytes 27656 | tf_op jit(solution)/shard_map/ppermute | solution.py:80
  49.8 8.9 %collective-permute-start.6 = (f32[3,2,3,128]{3,0,1,2:T(4,128)S(1)}, f32[3,2,3,128]{3,0,1,2:T(4,128)S(1)}, u32[]{:S(2)}, u32[]{:S(2)}) collective-permute-start(f32[3,2,3,128]{3,0,1,2:T(4,128)S(1)} %get-tuple-element.61), channel_id=1, source_target_pairs={{0,1},{1,2},{2,3},{3,4},{4,5},{5,6},{6,7},{7,8},{8,9},{9,10},{10,1... | collective-permute-start | bytes 27656 | tf_op jit(solution)/shard_map/ppermute | solution.py:83
  51.8 7.8 %collective-permute-start.7 = (f32[3,2,3,128]{3,0,1,2:T(4,128)S(1)}, f32[3,2,3,128]{3,0,1,2:T(4,128)S(1)}, u32[]{:S(2)}, u32[]{:S(2)}) collective-permute-start(f32[3,2,3,128]{3,0,1,2:T(4,128)S(1)} %get-tuple-element.60), channel_id=1, source_target_pairs={{1,0},{2,1},{3,2},{4,3},{5,4},{6,5},{7,6},{8,7},{9,8},{10,9},{11,1... | collective-permute-start | bytes 27656 | tf_op jit(solution)/shard_map/ppermute | solution.py:84

commit v14 on v12

--- a/solution.py
+++ b/solution.py
@@ -107,7 +107,7 @@
     payload = jnp.concatenate([own_pos, own_kind], axis=1)
     chosen = send_lists.reshape(8, sends)
     pick = (chosen[:, :, None] == jnp.arange(blocks)).astype(jnp.float32)
-    outgoing = jnp.einsum("dgb,bra->dgra", pick, payload, precision=HIGHEST)
+    outgoing = jnp.sum(jnp.where(pick[:, :, :, None, None] > 0, payload[None, None], 0.0), axis=2)
     incoming = collect(halo(place(outgoing))).reshape(8 * sends, 4, atoms)
     ghost_pos = incoming[:, :3]
     ghost_kind = incoming[:, 3]

time: 60.7 us -> 61 us (level)
  other arithmetic: 11.8 us -> 13.3 us
  matrix products: 7.91 us -> 7.03 us
  starting transfers between devices: 34.1 us -> 33.3 us
  waiting for transfers between devices: 2.26 us -> 2.94 us
    dot_general x1 -> x0, matrix products: 0.88 us -> none  [local(): outgoing = jnp.einsum('dgb,bra->dgra', pick, payload, precision=HIGHEST)]
    sub x0 -> x1, local copies, waits for them, and re-layouts: none -> 0.7 us  [tile_terms(): rel = other_pos[:, None, :] - own_pos[:, :, None]]
    reshape x1 -> x0, local copies, waits for them, and re-layouts: 0.7 us -> none  [local(): own_pos = positions.reshape(3, blocks, atoms).transpose(1, 0, 2)]
    concatenate x0 -> x1, other arithmetic: none -> 0.69 us  [local(): payload = jnp.concatenate([own_pos, own_kind], axis=1)]
    gt x0 -> x1, other arithmetic: none -> 0.69 us  [local(): pick[:, :, :, None, None] > 0]
    ppermute x2, starting transfers between devices: 13.9 us -> 13.2 us  [halo(): from_right_x = lax.ppermute(grid[0], 'gx', down_x)]
    ppermute x2, waiting for transfers between devices: 0.69 us -> 1.38 us  [halo(): from_left_x = lax.ppermute(grid[2], 'gx', up_x)]
  transfers between devices with their start and end apart: 8 -> 8, of which waited for: 3 -> 3; matrix products, arithmetic and copies ran while one was open for 6% -> 7% of each run, Pallas kernels for 0% -> 0%
where the time goes in v14:
time: 61 us; the launch traced here: 60.6 us
  starting transfers between devices  33.3 us (55%)
  other arithmetic  13.3 us (22%)
  matrix products  7.03 us (12%)
  waiting for transfers between devices  2.94 us (5%)
  local copies, waits for them, and re-layouts  2.34 us (4%)
  between operations  1.71 us (3%)
    ppermute x2, starting transfers between devices, halo(): from_right_y = lax.ppermute(rows[:, 0], 'gy', down_y)  16.3 us
    ppermute x2, starting transfers between devices, halo(): from_right_x = lax.ppermute(grid[0], 'gx', down_x)  13.2 us
    dot_general x8, matrix products, tile_terms(): jnp.einsum('qij,cj->qci', tiles.astype(jnp.bfloat16), other_feat, preferr...  4.2 us
    ppermute x2, starting transfers between devices, halo(): from_left_y = lax.ppermute(rows[:, 2], 'gy', up_y)  3.84 us
    reduce_sum x2, other arithmetic, tile_terms(): basis[:, None] * angular[None] * weight[None, None]  1.88 us
    ppermute x2, waiting for transfers between devices, halo(): from_right_y = lax.ppermute(rows[:, 0], 'gy', down_y)  1.56 us
    convert_element_type x4, other arithmetic, tile_terms(): tiles.astype(jnp.bfloat16)  1.39 us
    ppermute x2, waiting for transfers between devices, halo(): from_left_x = lax.ppermute(grid[2], 'gx', up_x)  1.38 us
  transfers between devices with their start and end apart: 8, of which 3 were waited for; matrix products, arithmetic and copies ran while one was open for 7% of the time, Pallas kernels for 0%

profile of v14, /device:TPU:1, one launch (start us, length us, event | category | flops | bytes accessed | tf_op | source)
XLA Modules:
  0.0 60.6 jit_solution(16045685356010289264)
XLA Ops:
  0.7 0.7 %convert_element_type.130 = f32[256]{0:T(256)S(1)} convert(s32[256]{0:T(256)} %param.10) | non-fusion elementwise | flops 256 | bytes 2048 | tf_op jit(solution)/shard_map/convert_element_type | solution.py:106
  1.4 0.7 %convert_compare_fusion = pred[8,2,2]{0,2,1:T(4,128)(4,1)S(1)} fusion(s32[8,2]{0,1:T(2,128)} %bitcast.803), kind=kLoop, calls=%fused_computation.508 | loop fusion | flops 96 | bytes 96 | tf_op jit(solution)/shard_map/gt | solution.py:110
  2.1 0.7 %pad_maximum_fusion.10 = f32[2,4,128]{2,1,0:T(4,128)S(1)} fusion(f32[2,1,128]{2,1,0:T(1,128)S(1)} %bitcast.805, f32[2,3,128]{2,1,0:T(4,128)} %bitcast.780), kind=kLoop, calls=%fused_computation.492 | loop fusion | flops 1024 | bytes 8192 | tf_op jit(solution)/shard_map/concatenate | solution.py:107
  2.9 10.5 %collective-permute-start.1 = (f32[3,2,4,128]{3,0,2,1:T(4,128)S(1)}, f32[3,2,4,128]{3,0,2,1:T(4,128)S(1)}, u32[]{:S(2)}, u32[]{:S(2)}) collective-permute-start(f32[3,2,4,128]{3,0,2,1:T(4,128)S(1)} %get-tuple-element.57), channel_id=1, source_target_pairs={{96,0},{192,96},{288,192},{384,288},{480,384},{576,480},{672,576},... | collective-permute-start | bytes 36872 | tf_op jit(solution)/shard_map/ppermute | solution.py:81
  13.4 0.7 %slice_bitcast_fusion.19 = (f32[3,128]{1,0:T(4,128)S(1)}, f32[3,128]{1,0:T(4,128)S(1)}) fusion(f32[2,3,128]{2,1,0:T(4,128)} %bitcast.781), kind=kLoop, calls=%fused_computation.500 | loop fusion | bytes 6144 | tf_op jit(solution)/shard_map/jvp()/sub | solution.py:35
  14.1 1.0 %multiply_bitcast_fusion = (f32[128,128]{1,0:T(8,128)S(1)}, f32[128,128]{1,0:T(8,128)S(1)}, f32[128,128]{1,0:T(8,128)S(1)}, f32[128,128]{1,0:T(8,128)S(1)}) fusion(s32[2,2,128,128]{3,2,1,0:T(8,128)} %param.12), kind=kLoop, calls=%fused_computation.418 | loop fusion | flops 131072 | bytes 524288 | tf_op jit(solution)/shard_map/jvp()/mul | solution.py:41
  15.1 0.7 %iota_compare_fusion = pred[2,2,18]{1,2,0:T(8,128)(4,1)S(1)} fusion(s32[2,2]{1,0:T(2,128)} %param.11), kind=kLoop, calls=%fused_computation.461 | loop fusion | flops 72 | bytes 88 | tf_op jit(solution)/shard_map/jvp()/eq | solution.py:68
  16.0 0.9 %convolution_bitcast_fusion.3 = f32[64,256]{1,0:T(8,128)S(1)} fusion(f32[4,64]{1,0:T(4,128)} %param.14, s32[256]{0:T(256)} %param.10), kind=kOutput, calls=%fused_computation.42 | convolution fusion | flops 787456 | bytes 67584 | tf_op jit(solution)/shard_map/dot_general | solution.py:117
  17.0 1.9 %collective-permute-start.2 = (f32[3,2,4,128]{3,2,1,0:T(4,128)S(1)}, f32[3,2,4,128]{3,2,1,0:T(4,128)S(1)}, u32[]{:S(2)}, u32[]{:S(2)}) collective-permute-start(f32[3,2,4,128]{3,2,1,0:T(4,128)S(1)} %get-tuple-element.55), channel_id=1, source_target_pairs={{0,1},{1,2},{2,3},{3,4},{4,5},{5,6},{6,7},{7,8},{8,9},{9,10},{10,1... | collective-permute-start | bytes 36872 | tf_op jit(solution)/shard_map/ppermute | solution.py:83
  19.1 9.3 %collective-permute-start.3 = (f32[3,2,4,128]{3,2,1,0:T(4,128)S(1)}, f32[3,2,4,128]{3,2,1,0:T(4,128)S(1)}, u32[]{:S(2)}, u32[]{:S(2)}) collective-permute-start(f32[3,2,4,128]{3,2,1,0:T(4,128)S(1)} %get-tuple-element.54), channel_id=1, source_target_pairs={{1,0},{2,1},{3,2},{4,3},{5,4},{6,5},{7,6},{8,7},{9,8},{10,9},{11,1... | collective-permute-start | bytes 36872 | tf_op jit(solution)/shard_map/ppermute | solution.py:84
  28.5 0.8 %collective-permute-done.3 = f32[3,2,4,128]{3,2,1,0:T(4,128)S(1)} collective-permute-done((f32[3,2,4,128]{3,2,1,0:T(4,128)S(1)}, f32[3,2,4,128]{3,2,1,0:T(4,128)S(1)}, u32[]{:S(2)}, u32[]{:S(2)}) %collective-permute-start.3) | collective-permute-done | bytes 12320 | tf_op jit(solution)/shard_map/ppermute | solution.py:84
  32.7 0.5 fusion.236
  33.6 0.5 fusion.237
  34.7 0.5 convolution_add_fusion.1
  35.6 0.5 convolution_add_fusion
  40.6 0.9 %fusion.2 = (f32[9,128,128]{2,1,0:T(8,128)S(1)}, f32[4,128,128]{2,1,0:T(8,128)S(1)}, f32[4,128,128]{2,1,0:T(8,128)S(1)}, f32[9,128,128]{2,1,0:T(8,128)S(1)}) fusion(bf16[4,9,128,128]{3,2,1,0:T(8,128)(2,1)S(1)} %bitcast.770, f32[128,128]{1,0:T(8,128)S(1)} %get-tuple-element.42, f32[4,128,128]{2,1,0:T(8,128)S(1)} %get-tuple-element.81, ...), kind=kLoop, calls=%fused_computation.3 | loop fusion | flops 6651904 | bytes 5898240 | tf_op jit(solution)/shard_map/transpose(jvp())/reduce_sum | solution.py:41
  41.8 0.9 %fusion.10 = (f32[9,128,128]{2,1,0:T(8,128)S(1)}, f32[4,128,128]{2,1,0:T(8,128)S(1)}, f32[4,128,128]{2,1,0:T(8,128)S(1)}, f32[9,128,128]{2,1,0:T(8,128)S(1)}) fusion(bf16[4,9,128,128]{3,2,1,0:T(8,128)(2,1)S(1)} %bitcast.768, f32[128,128]{1,0:T(8,128)S(1)} %get-tuple-element.43, f32[4,128,128]{2,1,0:T(8,128)S(1)} %get-tuple-element.83, ...), kind=kLoop, calls=%fused_computation.13 | loop fusion | flops 6651904 | bytes 5898240 | tf_op jit(solution)/shard_map/transpose(jvp())/reduce_sum | solution.py:41
  45.2 2.6 %collective-permute-start.5 = (f32[3,2,3,128]{3,1,2,0:T(2,128)S(1)}, f32[3,2,3,128]{3,1,2,0:T(2,128)S(1)}, u32[]{:S(2)}, u32[]{:S(2)}) collective-permute-start(f32[3,2,3,128]{3,1,2,0:T(2,128)S(1)} %copy.44), channel_id=1, source_target_pairs={{96,0},{192,96},{288,192},{384,288},{480,384},{576,480},{672,576},... | collective-permute-start | bytes 27656 | tf_op jit(solution)/shard_map/ppermute | solution.py:81
  47.9 0.6 maximum_bitcast_fusion.2
  48.6 1.4 %collective-permute-done.4 = f32[3,2,3,128]{3,1,2,0:T(2,128)S(1)} collective-permute-done((f32[3,2,3,128]{3,1,2,0:T(2,128)S(1)}, f32[3,2,3,128]{3,1,2,0:T(2,128)S(1)}, u32[]{:S(2)}, u32[]{:S(2)}) %collective-permute-start.4) | collective-permute-done | bytes 9248 | tf_op jit(solution)/shard_map/ppermute | solution.py:80
  50.0 1.9 %collective-permute-start.6 = (f32[3,2,3,128]{3,0,1,2:T(4,128)S(1)}, f32[3,2,3,128]{3,0,1,2:T(4,128)S(1)}, u32[]{:S(2)}, u32[]{:S(2)}) collective-permute-start(f32[3,2,3,128]{3,0,1,2:T(4,128)S(1)} %get-tuple-element.61), channel_id=1, source_target_pairs={{0,1},{1,2},{2,3},{3,4},{4,5},{5,6},{6,7},{7,8},{8,9},{9,10},{10,1... | collective-permute-start | bytes 27656 | tf_op jit(solution)/shard_map/ppermute | solution.py:83
  51.9 6.9 %collective-permute-start.7 = (f32[3,2,3,128]{3,0,1,2:T(4,128)S(1)}, f32[3,2,3,128]{3,0,1,2:T(4,128)S(1)}, u32[]{:S(2)}, u32[]{:S(2)}) collective-permute-start(f32[3,2,3,128]{3,0,1,2:T(4,128)S(1)} %get-tuple-element.60), channel_id=1, source_target_pairs={{1,0},{2,1},{3,2},{4,3},{5,4},{6,5},{7,6},{8,7},{9,8},{10,9},{11,1... | collective-permute-start | bytes 27656 | tf_op jit(solution)/shard_map/ppermute | solution.py:84
  58.9 0.8 %collective-permute-done.7 = f32[3,2,3,128]{3,0,1,2:T(4,128)S(1)} collective-permute-done((f32[3,2,3,128]{3,0,1,2:T(4,128)S(1)}, f32[3,2,3,128]{3,0,1,2:T(4,128)S(1)}, u32[]{:S(2)}, u32[]{:S(2)}) %collective-permute-start.7) | collective-permute-done | bytes 9248 | tf_op jit(solution)/shard_map/ppermute | solution.py:84
  60.0 0.6 copy.74
  (173 shorter events, 12.1 us)
Async XLA Ops:
  0.6 36.0 %copy-start = (f32[192,64]{0,1:T(8,128)S(1)}, f32[192,64]{0,1:T(8,128)}, u32[]{:S(2)}) copy-start(f32[192,64]{0,1:T(8,128)} %param.16) | copy-start | bytes 147460
  0.6 28.7 %copy-start.1 = (f32[3,256]{1,0:T(4,128)S(1)}, f32[3,256]{1,0:T(4,128)}, u32[]{:S(2)}) copy-start(f32[3,256]{1,0:T(4,128)} %param.9) | copy-start | bytes 9220
  0.7 18.5 %copy-start.3 = (f32[4,64]{1,0:T(4,128)S(1)}, f32[4,64]{1,0:T(4,128)}, u32[]{:S(2)}) copy-start(f32[4,64]{1,0:T(4,128)} %param.15) | copy-start | bytes 3076
  2.9 14.1 %collective-permute-start.1 = (f32[3,2,4,128]{3,0,2,1:T(4,128)S(1)}, f32[3,2,4,128]{3,0,2,1:T(4,128)S(1)}, u32[]{:S(2)}, u32[]{:S(2)}) collective-permute-start(f32[3,2,4,128]{3,0,2,1:T(4,128)S(1)} %get-tuple-element.57), channel_id=1, source_target_pairs={{96,0},{192,96},{288,192},{384,288},{480,384},{576,480},{672,576},... | collective-permute-start | bytes 36872 | tf_op jit(solution)/shard_map/ppermute | solution.py:81
  13.4 3.6 %collective-permute-start = (f32[3,2,4,128]{3,2,1,0:T(4,128)S(1)}, f32[3,2,4,128]{3,2,1,0:T(4,128)S(1)}, u32[]{:S(2)}, u32[]{:S(2)}) collective-permute-start(f32[3,2,4,128]{3,2,1,0:T(4,128)S(1)} %copy.60), channel_id=1, source_target_pairs={{0,96},{96,192},{192,288},{288,384},{384,480},{480,576},{576,672},... | collective-permute-start | bytes 36872 | tf_op jit(solution)/shard_map/ppermute | solution.py:80
  17.0 11.4 %collective-permute-start.2 = (f32[3,2,4,128]{3,2,1,0:T(4,128)S(1)}, f32[3,2,4,128]{3,2,1,0:T(4,128)S(1)}, u32[]{:S(2)}, u32[]{:S(2)}) collective-permute-start(f32[3,2,4,128]{3,2,1,0:T(4,128)S(1)} %get-tuple-element.55), channel_id=1, source_target_pairs={{0,1},{1,2},{2,3},{3,4},{4,5},{5,6},{6,7},{7,8},{8,9},{9,10},{10,1... | collective-permute-start | bytes 36872 | tf_op jit(solution)/shard_map/ppermute | solution.py:83
  19.1 10.1 %collective-permute-start.3 = (f32[3,2,4,128]{3,2,1,0:T(4,128)S(1)}, f32[3,2,4,128]{3,2,1,0:T(4,128)S(1)}, u32[]{:S(2)}, u32[]{:S(2)}) collective-permute-start(f32[3,2,4,128]{3,2,1,0:T(4,128)S(1)} %get-tuple-element.54), channel_id=1, source_target_pairs={{1,0},{2,1},{3,2},{4,3},{5,4},{6,5},{7,6},{8,7},{9,8},{10,9},{11,1... | collective-permute-start | bytes 36872 | tf_op jit(solution)/shard_map/ppermute | solution.py:84
  29.7 0.7 %copy-start.2 = (f32[4,64]{1,0:T(4,128)S(1)}, f32[4,64]{1,0:T(4,128)}, u32[]{:S(2)}) copy-start(f32[4,64]{1,0:T(4,128)} %param.14) | copy-start | bytes 3076
  36.2 0.7 %copy-start.5 = (f32[64]{0:T(128)S(1)}, f32[64]{0:T(128)}, u32[]{:S(2)}) copy-start(f32[64]{0:T(128)} %param.17) | copy-start | bytes 772
  44.5 15.3 %copy-start.4 = (s32[1,1,8,2]{2,3,1,0:T(2,128)S(1)}, s32[1,1,8,2]{2,3,1,0:T(2,128)}, u32[]{:S(2)}) copy-start(s32[1,1,8,2]{2,3,1,0:T(2,128)} %param.13) | copy-start | bytes 196
  45.2 4.8 %collective-permute-start.5 = (f32[3,2,3,128]{3,1,2,0:T(2,128)S(1)}, f32[3,2,3,128]{3,1,2,0:T(2,128)S(1)}, u32[]{:S(2)}, u32[]{:S(2)}) collective-permute-start(f32[3,2,3,128]{3,1,2,0:T(2,128)S(1)} %copy.44), channel_id=1, source_target_pairs={{96,0},{192,96},{288,192},{384,288},{480,384},{576,480},{672,576},... | collective-permute-start | bytes 27656 | tf_op jit(solution)/shard_map/ppermute | solution.py:81
  47.9 2.1 %collective-permute-start.4 = (f32[3,2,3,128]{3,1,2,0:T(2,128)S(1)}, f32[3,2,3,128]{3,1,2,0:T(2,128)S(1)}, u32[]{:S(2)}, u32[]{:S(2)}) collective-permute-start(f32[3,2,3,128]{3,1,2,0:T(2,128)S(1)} %copy.38), channel_id=1, source_target_pairs={{0,96},{96,192},{192,288},{288,384},{384,480},{480,576},{576,672},... | collective-permute-start | bytes 27656 | tf_op jit(solution)/shard_map/ppermute | solution.py:80
  50.0 8.9 %collective-permute-start.6 = (f32[3,2,3,128]{3,0,1,2:T(4,128)S(1)}, f32[3,2,3,128]{3,0,1,2:T(4,128)S(1)}, u32[]{:S(2)}, u32[]{:S(2)}) collective-permute-start(f32[3,2,3,128]{3,0,1,2:T(4,128)S(1)} %get-tuple-element.61), channel_id=1, source_target_pairs={{0,1},{1,2},{2,3},{3,4},{4,5},{5,6},{6,7},{7,8},{8,9},{9,10},{10,1... | collective-permute-start | bytes 27656 | tf_op jit(solution)/shard_map/ppermute | solution.py:83
  51.9 7.8 %collective-permute-start.7 = (f32[3,2,3,128]{3,0,1,2:T(4,128)S(1)}, f32[3,2,3,128]{3,0,1,2:T(4,128)S(1)}, u32[]{:S(2)}, u32[]{:S(2)}) collective-permute-start(f32[3,2,3,128]{3,0,1,2:T(4,128)S(1)} %get-tuple-element.60), channel_id=1, source_target_pairs={{1,0},{2,1},{3,2},{4,3},{5,4},{6,5},{7,6},{8,7},{9,8},{10,9},{11,1... | collective-permute-start | bytes 27656 | tf_op jit(solution)/shard_map/ppermute | solution.py:84

commit v15 on v12

--- a/solution.py
+++ b/solution.py
@@ -144,7 +144,7 @@
     energy, pullback = jax.vjp(energies_of, own_pos, ghost_pos)
     grad_own, grad_ghost = pullback(jnp.ones_like(energy))
     returned = collect(halo(place(grad_ghost.reshape(8, sends, 3, atoms))))
-    back = jnp.einsum("dgb,dgca->bca", pick, returned, precision=HIGHEST)
+    back = jnp.sum(jnp.where(pick[:, :, :, None, None] > 0, returned[:, :, None], 0.0), axis=(0, 1))
     forces = -(grad_own + back)
     return (energy.reshape(blocks * atoms), forces.transpose(1, 0, 2).reshape(3, blocks * atoms))
 

time: 60.7 us -> 61.5 us (1.013)
  other arithmetic: 11.8 us -> 13.2 us
  waiting for transfers between devices: 2.26 us -> 3.55 us
  starting transfers between devices: 34.1 us -> 33.3 us
  local copies, waits for them, and re-layouts: 2.34 us -> 1.69 us
    ppermute x2, waiting for transfers between devices: 0.01 us -> 0.75 us  [halo(): from_right_x = lax.ppermute(grid[0], 'gx', down_x)]
    gt x0 -> x1, other arithmetic: none -> 0.69 us  [local(): pick[:, :, :, None, None] > 0]
    ppermute x2, starting transfers between devices: 13.9 us -> 13.2 us  [halo(): from_right_x = lax.ppermute(grid[0], 'gx', down_x)]
  transfers between devices with their start and end apart: 8 -> 8, of which waited for: 3 -> 4; matrix products, arithmetic and copies ran while one was open for 6% -> 7% of each run, Pallas kernels for 0% -> 0%
where the time goes in v15:
time: 61.5 us; the launch traced here: 61 us
  starting transfers between devices  33.3 us (54%)
  other arithmetic  13.2 us (21%)
  matrix products  7.7 us (13%)
  waiting for transfers between devices  3.55 us (6%)
  local copies, waits for them, and re-layouts  1.69 us (3%)
  between operations  1.68 us (3%)
    ppermute x2, starting transfers between devices, halo(): from_right_y = lax.ppermute(rows[:, 0], 'gy', down_y)  16.2 us
    ppermute x2, starting transfers between devices, halo(): from_right_x = lax.ppermute(grid[0], 'gx', down_x)  13.2 us
    dot_general x8, matrix products, tile_terms(): jnp.einsum('qij,cj->qci', tiles.astype(jnp.bfloat16), other_feat, preferr...  4.19 us
    ppermute x2, starting transfers between devices, halo(): from_left_y = lax.ppermute(rows[:, 2], 'gy', up_y)  3.84 us
    reduce_sum x2, other arithmetic, tile_terms(): basis[:, None] * angular[None] * weight[None, None]  1.88 us
    ppermute x2, waiting for transfers between devices, halo(): from_right_y = lax.ppermute(rows[:, 0], 'gy', down_y)  1.55 us
    convert_element_type x4, other arithmetic, tile_terms(): tiles.astype(jnp.bfloat16)  1.39 us
    dot_general x2, matrix products, features(): return jnp.dot(embedding.T, onehot, precision=HIGHEST)  1.36 us
  transfers between devices with their start and end apart: 8, of which 4 were waited for; matrix products, arithmetic and copies ran while one was open for 7% of the time, Pallas kernels for 0%

profile of v15, /device:TPU:1, one launch (start us, length us, event | category | flops | bytes accessed | tf_op | source)
XLA Modules:
  0.0 61.0 jit_solution(13644791363654542008)
XLA Ops:
  0.7 0.7 %convert_bitcast_fusion = f32[2,1,128]{2,0,1:T(2,128)S(1)} fusion(s32[256]{0:T(256)} %param.10), kind=kLoop, calls=%fused_computation.522 | loop fusion | flops 256 | bytes 2048 | tf_op jit(solution)/shard_map/convert_element_type | solution.py:106
  1.4 0.7 %reshape.514 = f32[3,2,128]{2,1,0:T(2,128)S(1)} reshape(f32[3,256]{1,0:T(4,128)} %param.9) | data formatting | bytes 6144 | tf_op jit(solution)/shard_map/reshape | solution.py:105
  2.1 0.9 %fusion.242 = f32[8,2,4,128]{3,0,2,1:T(8,128)S(1)} fusion(f32[2,1,128]{2,0,1:T(2,128)S(1)} %convert_bitcast_fusion, f32[2,3,128]{2,0,1:T(2,128)S(1)} %bitcast.779, s32[8,2]{0,1:T(2,128)} %bitcast.806), kind=kOutput, calls=%fused_computation.503 | convolution fusion | flops 197664 | bytes 36928 | tf_op jit(solution)/shard_map/dgb,bra->dgra/dot_general | solution.py:110
  3.0 10.5 %collective-permute-start.1 = (f32[3,2,4,128]{3,0,2,1:T(4,128)S(1)}, f32[3,2,4,128]{3,0,2,1:T(4,128)S(1)}, u32[]{:S(2)}, u32[]{:S(2)}) collective-permute-start(f32[3,2,4,128]{3,0,2,1:T(4,128)S(1)} %get-tuple-element.59), channel_id=1, source_target_pairs={{96,0},{192,96},{288,192},{384,288},{480,384},{576,480},{672,576},... | collective-permute-start | bytes 36872 | tf_op jit(solution)/shard_map/ppermute | solution.py:81
  13.6 0.7 %convert_compare_fusion = pred[8,2,2]{0,2,1:T(4,128)(4,1)S(1)} fusion(s32[8,2]{0,1:T(2,128)} %bitcast.807), kind=kLoop, calls=%fused_computation.516 | loop fusion | flops 96 | bytes 96 | tf_op jit(solution)/shard_map/gt | solution.py:147
  14.3 1.0 %multiply_bitcast_fusion = (f32[128,128]{1,0:T(8,128)S(1)}, f32[128,128]{1,0:T(8,128)S(1)}, f32[128,128]{1,0:T(8,128)S(1)}, f32[128,128]{1,0:T(8,128)S(1)}) fusion(s32[2,2,128,128]{3,2,1,0:T(8,128)} %param.12), kind=kLoop, calls=%fused_computation.422 | loop fusion | flops 131072 | bytes 524288 | tf_op jit(solution)/shard_map/jvp()/mul | solution.py:41
  15.2 0.7 %iota_compare_fusion = pred[2,2,18]{1,2,0:T(8,128)(4,1)S(1)} fusion(s32[2,2]{1,0:T(2,128)} %param.11), kind=kLoop, calls=%fused_computation.465 | loop fusion | flops 72 | bytes 88 | tf_op jit(solution)/shard_map/jvp()/eq | solution.py:68
  16.1 0.9 %convolution_bitcast_fusion.3 = f32[64,256]{1,0:T(8,128)S(1)} fusion(f32[4,64]{1,0:T(4,128)} %param.14, s32[256]{0:T(256)} %param.10), kind=kOutput, calls=%fused_computation.42 | convolution fusion | flops 787456 | bytes 67584 | tf_op jit(solution)/shard_map/dot_general | solution.py:117
  17.1 1.9 %collective-permute-start.2 = (f32[3,2,4,128]{3,2,1,0:T(4,128)S(1)}, f32[3,2,4,128]{3,2,1,0:T(4,128)S(1)}, u32[]{:S(2)}, u32[]{:S(2)}) collective-permute-start(f32[3,2,4,128]{3,2,1,0:T(4,128)S(1)} %get-tuple-element.57), channel_id=1, source_target_pairs={{0,1},{1,2},{2,3},{3,4},{4,5},{5,6},{6,7},{7,8},{8,9},{9,10},{10,1... | collective-permute-start | bytes 36872 | tf_op jit(solution)/shard_map/ppermute | solution.py:83
  19.3 9.3 %collective-permute-start.3 = (f32[3,2,4,128]{3,2,1,0:T(4,128)S(1)}, f32[3,2,4,128]{3,2,1,0:T(4,128)S(1)}, u32[]{:S(2)}, u32[]{:S(2)}) collective-permute-start(f32[3,2,4,128]{3,2,1,0:T(4,128)S(1)} %get-tuple-element.56), channel_id=1, source_target_pairs={{1,0},{2,1},{3,2},{4,3},{5,4},{6,5},{7,6},{8,7},{9,8},{10,9},{11,1... | collective-permute-start | bytes 36872 | tf_op jit(solution)/shard_map/ppermute | solution.py:84
  28.6 0.8 %collective-permute-done.3 = f32[3,2,4,128]{3,2,1,0:T(4,128)S(1)} collective-permute-done((f32[3,2,4,128]{3,2,1,0:T(4,128)S(1)}, f32[3,2,4,128]{3,2,1,0:T(4,128)S(1)}, u32[]{:S(2)}, u32[]{:S(2)}) %collective-permute-start.3) | collective-permute-done | bytes 12320 | tf_op jit(solution)/shard_map/ppermute | solution.py:84
  33.7 0.5 fusion.234
  34.9 0.5 convolution_add_fusion.1
  35.8 0.5 convolution_add_fusion
  40.8 0.9 %fusion.2 = (f32[9,128,128]{2,1,0:T(8,128)S(1)}, f32[4,128,128]{2,1,0:T(8,128)S(1)}, f32[4,128,128]{2,1,0:T(8,128)S(1)}, f32[9,128,128]{2,1,0:T(8,128)S(1)}) fusion(bf16[4,9,128,128]{3,2,1,0:T(8,128)(2,1)S(1)} %bitcast.771, f32[128,128]{1,0:T(8,128)S(1)} %get-tuple-element.42, f32[4,128,128]{2,1,0:T(8,128)S(1)} %get-tuple-element.75, ...), kind=kLoop, calls=%fused_computation.3 | loop fusion | flops 6651904 | bytes 5898240 | tf_op jit(solution)/shard_map/transpose(jvp())/reduce_sum | solution.py:41
  41.9 0.9 %fusion.10 = (f32[9,128,128]{2,1,0:T(8,128)S(1)}, f32[4,128,128]{2,1,0:T(8,128)S(1)}, f32[4,128,128]{2,1,0:T(8,128)S(1)}, f32[9,128,128]{2,1,0:T(8,128)S(1)}) fusion(bf16[4,9,128,128]{3,2,1,0:T(8,128)(2,1)S(1)} %bitcast.769, f32[128,128]{1,0:T(8,128)S(1)} %get-tuple-element.43, f32[4,128,128]{2,1,0:T(8,128)S(1)} %get-tuple-element.77, ...), kind=kLoop, calls=%fused_computation.13 | loop fusion | flops 6651904 | bytes 5898240 | tf_op jit(solution)/shard_map/transpose(jvp())/reduce_sum | solution.py:41
  45.3 2.7 %collective-permute-start.5 = (f32[3,2,3,128]{3,2,1,0:T(4,128)S(1)}, f32[3,2,3,128]{3,2,1,0:T(4,128)S(1)}, u32[]{:S(2)}, u32[]{:S(2)}) collective-permute-start(f32[3,2,3,128]{3,2,1,0:T(4,128)S(1)} %bitcast.805), channel_id=1, source_target_pairs={{96,0},{192,96},{288,192},{384,288},{480,384},{576,480},{672,576},... | collective-permute-start | bytes 27656 | tf_op jit(solution)/shard_map/ppermute | solution.py:81
  48.0 0.7 %collective-permute-done.5 = f32[3,2,3,128]{3,2,1,0:T(4,128)S(1)} collective-permute-done((f32[3,2,3,128]{3,2,1,0:T(4,128)S(1)}, f32[3,2,3,128]{3,2,1,0:T(4,128)S(1)}, u32[]{:S(2)}, u32[]{:S(2)}) %collective-permute-start.5) | collective-permute-done | bytes 9248 | tf_op jit(solution)/shard_map/ppermute | solution.py:81
  48.8 1.2 %collective-permute-done.4 = f32[3,2,3,128]{3,2,1,0:T(4,128)S(1)} collective-permute-done((f32[3,2,3,128]{3,2,1,0:T(4,128)S(1)}, f32[3,2,3,128]{3,2,1,0:T(4,128)S(1)}, u32[]{:S(2)}, u32[]{:S(2)}) %collective-permute-start.4) | collective-permute-done | bytes 9248 | tf_op jit(solution)/shard_map/ppermute | solution.py:80
  50.0 1.9 %collective-permute-start.6 = (f32[3,2,3,128]{3,2,1,0:T(4,128)S(1)}, f32[3,2,3,128]{3,2,1,0:T(4,128)S(1)}, u32[]{:S(2)}, u32[]{:S(2)}) collective-permute-start(f32[3,2,3,128]{3,2,1,0:T(4,128)S(1)} %get-tuple-element.51), channel_id=1, source_target_pairs={{0,1},{1,2},{2,3},{3,4},{4,5},{5,6},{6,7},{7,8},{8,9},{9,10},{10,1... | collective-permute-start | bytes 27656 | tf_op jit(solution)/shard_map/ppermute | solution.py:83
  52.0 0.6 maximum_bitcast_fusion.4
  52.5 6.9 %collective-permute-start.7 = (f32[3,2,3,128]{3,2,1,0:T(4,128)S(1)}, f32[3,2,3,128]{3,2,1,0:T(4,128)S(1)}, u32[]{:S(2)}, u32[]{:S(2)}) collective-permute-start(f32[3,2,3,128]{3,2,1,0:T(4,128)S(1)} %get-tuple-element.50), channel_id=1, source_target_pairs={{1,0},{2,1},{3,2},{4,3},{5,4},{6,5},{7,6},{8,7},{9,8},{10,9},{11,1... | collective-permute-start | bytes 27656 | tf_op jit(solution)/shard_map/ppermute | solution.py:84
  59.5 0.8 %collective-permute-done.7 = f32[3,2,3,128]{3,2,1,0:T(4,128)S(1)} collective-permute-done((f32[3,2,3,128]{3,2,1,0:T(4,128)S(1)}, f32[3,2,3,128]{3,2,1,0:T(4,128)S(1)}, u32[]{:S(2)}, u32[]{:S(2)}) %collective-permute-start.7) | collective-permute-done | bytes 9248 | tf_op jit(solution)/shard_map/ppermute | solution.py:84
  60.4 0.6 fusion.241
  (169 shorter events, 12.4 us)
Async XLA Ops:
  0.6 36.1 %copy-start = (f32[192,64]{0,1:T(8,128)S(1)}, f32[192,64]{0,1:T(8,128)}, u32[]{:S(2)}) copy-start(f32[192,64]{0,1:T(8,128)} %param.16) | copy-start | bytes 147460
  0.6 18.6 %copy-start.2 = (f32[4,64]{1,0:T(4,128)S(1)}, f32[4,64]{1,0:T(4,128)}, u32[]{:S(2)}) copy-start(f32[4,64]{1,0:T(4,128)} %param.15) | copy-start | bytes 3076
  3.0 14.1 %collective-permute-start.1 = (f32[3,2,4,128]{3,0,2,1:T(4,128)S(1)}, f32[3,2,4,128]{3,0,2,1:T(4,128)S(1)}, u32[]{:S(2)}, u32[]{:S(2)}) collective-permute-start(f32[3,2,4,128]{3,0,2,1:T(4,128)S(1)} %get-tuple-element.59), channel_id=1, source_target_pairs={{96,0},{192,96},{288,192},{384,288},{480,384},{576,480},{672,576},... | collective-permute-start | bytes 36872 | tf_op jit(solution)/shard_map/ppermute | solution.py:81
  13.5 3.6 %collective-permute-start = (f32[3,2,4,128]{3,2,1,0:T(4,128)S(1)}, f32[3,2,4,128]{3,2,1,0:T(4,128)S(1)}, u32[]{:S(2)}, u32[]{:S(2)}) collective-permute-start(f32[3,2,4,128]{3,2,1,0:T(4,128)S(1)} %copy.51), channel_id=1, source_target_pairs={{0,96},{96,192},{192,288},{288,384},{384,480},{480,576},{576,672},... | collective-permute-start | bytes 36872 | tf_op jit(solution)/shard_map/ppermute | solution.py:80
  17.1 11.5 %collective-permute-start.2 = (f32[3,2,4,128]{3,2,1,0:T(4,128)S(1)}, f32[3,2,4,128]{3,2,1,0:T(4,128)S(1)}, u32[]{:S(2)}, u32[]{:S(2)}) collective-permute-start(f32[3,2,4,128]{3,2,1,0:T(4,128)S(1)} %get-tuple-element.57), channel_id=1, source_target_pairs={{0,1},{1,2},{2,3},{3,4},{4,5},{5,6},{6,7},{7,8},{8,9},{9,10},{10,1... | collective-permute-start | bytes 36872 | tf_op jit(solution)/shard_map/ppermute | solution.py:83
  19.3 10.1 %collective-permute-start.3 = (f32[3,2,4,128]{3,2,1,0:T(4,128)S(1)}, f32[3,2,4,128]{3,2,1,0:T(4,128)S(1)}, u32[]{:S(2)}, u32[]{:S(2)}) collective-permute-start(f32[3,2,4,128]{3,2,1,0:T(4,128)S(1)} %get-tuple-element.56), channel_id=1, source_target_pairs={{1,0},{2,1},{3,2},{4,3},{5,4},{6,5},{7,6},{8,7},{9,8},{10,9},{11,1... | collective-permute-start | bytes 36872 | tf_op jit(solution)/shard_map/ppermute | solution.py:84
  29.9 0.7 %copy-start.1 = (f32[4,64]{1,0:T(4,128)S(1)}, f32[4,64]{1,0:T(4,128)}, u32[]{:S(2)}) copy-start(f32[4,64]{1,0:T(4,128)} %param.14) | copy-start | bytes 3076
  36.3 0.7 %copy-start.3 = (f32[64]{0:T(128)S(1)}, f32[64]{0:T(128)}, u32[]{:S(2)}) copy-start(f32[64]{0:T(128)} %param.17) | copy-start | bytes 772
  45.3 3.5 %collective-permute-start.5 = (f32[3,2,3,128]{3,2,1,0:T(4,128)S(1)}, f32[3,2,3,128]{3,2,1,0:T(4,128)S(1)}, u32[]{:S(2)}, u32[]{:S(2)}) collective-permute-start(f32[3,2,3,128]{3,2,1,0:T(4,128)S(1)} %bitcast.805), channel_id=1, source_target_pairs={{96,0},{192,96},{288,192},{384,288},{480,384},{576,480},{672,576},... | collective-permute-start | bytes 27656 | tf_op jit(solution)/shard_map/ppermute | solution.py:81
  48.0 2.1 %collective-permute-start.4 = (f32[3,2,3,128]{3,2,1,0:T(4,128)S(1)}, f32[3,2,3,128]{3,2,1,0:T(4,128)S(1)}, u32[]{:S(2)}, u32[]{:S(2)}) collective-permute-start(f32[3,2,3,128]{3,2,1,0:T(4,128)S(1)} %bitcast.804), channel_id=1, source_target_pairs={{0,96},{96,192},{192,288},{288,384},{384,480},{480,576},{576,672},... | collective-permute-start | bytes 27656 | tf_op jit(solution)/shard_map/ppermute | solution.py:80
  50.0 9.4 %collective-permute-start.6 = (f32[3,2,3,128]{3,2,1,0:T(4,128)S(1)}, f32[3,2,3,128]{3,2,1,0:T(4,128)S(1)}, u32[]{:S(2)}, u32[]{:S(2)}) collective-permute-start(f32[3,2,3,128]{3,2,1,0:T(4,128)S(1)} %get-tuple-element.51), channel_id=1, source_target_pairs={{0,1},{1,2},{2,3},{3,4},{4,5},{5,6},{6,7},{7,8},{8,9},{9,10},{10,1... | collective-permute-start | bytes 27656 | tf_op jit(solution)/shard_map/ppermute | solution.py:83
  52.5 7.7 %collective-permute-start.7 = (f32[3,2,3,128]{3,2,1,0:T(4,128)S(1)}, f32[3,2,3,128]{3,2,1,0:T(4,128)S(1)}, u32[]{:S(2)}, u32[]{:S(2)}) collective-permute-start(f32[3,2,3,128]{3,2,1,0:T(4,128)S(1)} %get-tuple-element.50), channel_id=1, source_target_pairs={{1,0},{2,1},{3,2},{4,3},{5,4},{6,5},{7,6},{8,7},{9,8},{10,9},{11,1... | collective-permute-start | bytes 27656 | tf_op jit(solution)/shard_map/ppermute | solution.py:84
